TPU v7x, 1024 devices: a whole 8x8x8 slice. The times are simulated.
1024 devices in a mesh: lat: 16 (over x, core), lon: 64 (over y, z).
Axes of the slice: x: 8, y: 8, z: 8, core: 2. Of those that a mesh axis runs over, the one named last changes fastest.
Arguments:
- grid_field: bfloat16 [8, 2, 1024, 4160], P(None, None, 'lat', 'lon'), may hold values from -6 to 6
- row_shift: int32 [2, 1024, 4160], P(None, 'lat', 'lon'), may hold values from -1 to 1
- col_shift: int32 [2, 1024, 4160], P(None, 'lat', 'lon'), may hold values from -4 to 4
- lon_weight: bfloat16 [2, 1024, 4160], P(None, 'lat', 'lon'), may hold values from 0 to 1
- pair_of_slot: int32 [640], replicated, may hold values from 0 to 639, each once
- legendre: bfloat16 [1024, 640, 1281], P('lat', 'lon'), may hold values from -0.125 to 0.125
- helm_coeff: float32 [8], replicated, may hold values from 1e-07 to 1e-05
Outputs:
- spectral_solution: float32 [640, 2, 8, 1281], P('lon')
- fourier_rows: bfloat16 [640, 2, 2, 2, 8, 1024], P('lon', None, None, None, None, 'lat')
Inputs may be any that keep to these rules, and one draw needn't show every extreme that they name: `pair_of_slot`: each of the 640 pair numbers stands in exactly one slot.
All inputs are finite; a program needn't handle non-finite values.
Results may differ from a plain program's by a relative error of at most 0.0066.
Values may be sent and summed in bfloat16 or wider, within the bound.
No kernel may reach another device: no remote copies, remote signals or barrier semaphores. Data moves between devices by JAX's collectives and lax.ppermute only.
A program may use at most 64 MiB of HBM per device.

v0:
```python
import math

import jax
import jax.numpy as jnp
from jax import lax
from jax.sharding import PartitionSpec as P

TRUNC = 1279
H = 1
PAIRS = 640
NPAIR = 1281
WL = 10


def extended_2(value, sides, width):
    for axis, dim in sides:
        peers, length = (lax.axis_size(axis), value.shape[dim])
        up = [(i, (i + 1) % peers) for i in range(peers - 1)]
        down = [(j, i) for i, j in up]
        last = lax.slice_in_dim(value, length - width, length, axis=dim)
        initial = lax.slice_in_dim(value, 0, width, axis=dim)
        before = lax.ppermute(last, axis, up)
        after = lax.ppermute(initial, axis, down)
        value = jnp.concatenate([before, value, after], axis=dim)
    return value


def shortened(value):

    def short(part):
        return part.astype(jnp.bfloat16) if part.dtype == jnp.float32 else part

    return jax.tree.map(short, value)


def depart_values(
    extended, half_rows, low_rows, first_row, col_core, col_ext, row_shift, col_shift, lon_weight
):
    row_count = row_shift.shape[1]
    col_count = row_shift.shape[2]
    height = extended.shape[2]
    ext_width = extended.shape[3]
    lat_index = first_row + jnp.arange(row_count, dtype=jnp.int32)[:, None]
    lon_index = col_core + jnp.arange(col_count, dtype=jnp.int32)[None, :]
    length = 20 + 4 * lat_index
    target = jnp.maximum(lat_index + row_shift, 0)
    mirror = jnp.where(target > half_rows - 1, 2 * half_rows - 1 - target, target)
    length_dep = 20 + 4 * mirror
    shifted = jnp.clip(lon_index + col_shift, 0, length - 1)
    column = jnp.minimum(shifted * length_dep // length, length_dep - 2)
    hemisphere = jnp.arange(2, dtype=jnp.int32)[:, None, None]
    flat_index = (hemisphere * height + (target - first_row + low_rows)) * ext_width + (
        column - col_ext
    )
    flat_field = extended.reshape(extended.shape[0], -1)
    left_value = flat_field[:, flat_index].astype(jnp.float32)
    right_value = flat_field[:, flat_index + 1].astype(jnp.float32)
    blend = lon_weight.astype(jnp.float32)
    blended = (1.0 - blend) * left_value + blend * right_value
    return jnp.where(lon_index < length, blended, 0.0).astype(jnp.bfloat16)


def row_spectrum(row_data, lat_index, pair_of_slot):
    length = 20 + 4 * lat_index
    quarter_len = length // 4
    quarters = row_data.reshape(row_data.shape[0], 2, -1, 4)
    slots = jnp.arange(quarters.shape[2], dtype=jnp.int32)[:, None, None]
    offsets = jnp.arange(4, dtype=jnp.int32)[None, None, :]
    norm_scale = 1.0 / jnp.sqrt(length.astype(jnp.float32))
    block_size = math.gcd(PAIRS, 128)
    pieces = []
    for block_start in range(0, PAIRS, block_size):
        pair_ids = pair_of_slot[block_start : block_start + block_size]
        pair_orders = jnp.stack([pair_ids, TRUNC - pair_ids], axis=1)
        orders = pair_orders[None]
        phase_idx = orders * slots % quarter_len
        angles = phase_idx.astype(jnp.float32) * (2.0 * math.pi) / quarter_len.astype(jnp.float32)
        usable = (2 * orders < length) & (slots < quarter_len)
        cosine = jnp.where(usable, jnp.cos(angles), 0.0)
        minus_sine = jnp.where(usable, -jnp.sin(angles), 0.0)
        factors = jnp.stack([cosine, minus_sine], axis=-1).astype(jnp.bfloat16)
        inner = jnp.einsum(
            "aser,fhab->serfhb", factors, quarters, preferred_element_type=jnp.float32
        )
        twist_idx = pair_orders[:, :, None] * offsets % length
        twist = twist_idx.astype(jnp.float32) * (2.0 * math.pi) / length.astype(jnp.float32)
        twist_cos = jnp.cos(twist)[:, :, None, None, :]
        twist_sin = jnp.sin(twist)[:, :, None, None, :]
        real_part = jnp.sum(inner[:, :, 0] * twist_cos + inner[:, :, 1] * twist_sin, axis=-1)
        imag_part = jnp.sum(inner[:, :, 1] * twist_cos - inner[:, :, 0] * twist_sin, axis=-1)
        spectrum = jnp.stack([real_part, imag_part], axis=2)
        pieces.append((spectrum * norm_scale).astype(jnp.bfloat16).reshape(block_size, -1))
    return jnp.concatenate(pieces, axis=0)


def column_terms(pair_ids):
    columns = jnp.arange(NPAIR, dtype=jnp.int32)[None, :]
    partner = (TRUNC - pair_ids)[:, None]
    second_half = columns > partner
    degree = jnp.where(second_half, columns - 1, pair_ids[:, None] + columns)
    offset = jnp.where(second_half, columns - 1 - partner, columns)
    parity = (1 - 2 * (offset % 2)).astype(jnp.float32)
    return (second_half, degree, parity)


def analyse(legend, spectra, pair_ids):
    products = jnp.einsum("ksc,ksq->sqc", legend, spectra, preferred_element_type=jnp.float32)
    second_half, degree, parity = column_terms(pair_ids)
    products = products.reshape(products.shape[0], 2, 2, -1, 2, NPAIR)
    chosen = jnp.where(second_half[:, None, None, None, :], products[:, 1], products[:, 0])
    return chosen[:, :, :, 0] + parity[:, None, None, :] * chosen[:, :, :, 1]


def helmholtz_solve(spectral_total, pair_ids, helm_coeff):
    second_half, degree, parity = column_terms(pair_ids)
    growth = (degree * (degree + 1)).astype(jnp.float32)
    return spectral_total / (1.0 + helm_coeff[None, None, :, None] * growth[:, None, None, :])


def synthesise(legend, solved, pair_ids):
    second_half, degree, parity = column_terms(pair_ids)
    rounded = solved.astype(jnp.bfloat16)
    lower_mask = jnp.where(second_half, 0.0, 1.0)
    upper_mask = jnp.where(second_half, 1.0, 0.0)
    selector = jnp.stack([lower_mask, upper_mask], axis=1)
    sign_rows = jnp.stack([jnp.ones_like(parity), parity], axis=1)
    weights = (selector[:, :, None, :] * sign_rows[:, None, :, :]).astype(jnp.bfloat16)
    spread = weights[:, :, :, None, None, :] * rounded[:, None, None, :, :, :]
    out_shape = spread.shape[:5]
    spread = spread.reshape(spread.shape[0], -1, NPAIR)
    rows_out = jnp.einsum("ksc,sqc->sqk", legend, spread, preferred_element_type=jnp.float32)
    rows_out = (4.0 * rows_out).astype(jnp.bfloat16)
    return rows_out.reshape(out_shape + (legend.shape[0],))


def on_device(grid_field, row_shift, col_shift, lon_weight, pair_of_slot, legendre, helm_coeff):
    lat_pos = lax.axis_index("lat")
    lon_pos = lax.axis_index("lon")
    lat_count = lax.axis_size("lat")
    lon_count = lax.axis_size("lon")
    band_rows = grid_field.shape[2]
    sector_cols = grid_field.shape[3]
    half_rows = band_rows * lat_count
    row_count = band_rows // lon_count
    first_row = lat_pos * band_rows + lon_pos * row_count
    widened = extended_2(grid_field, (("lon", 3),), WL)
    extended = extended_2(widened, (("lat", 2),), H)
    mirrored = widened[:, ::-1, band_rows - H :, :][:, :, ::-1, :]
    at_equator = lat_pos == lat_count - 1
    upper_rows = jnp.where(at_equator, mirrored, extended[:, :, band_rows + H :, :])
    extended = jnp.concatenate([extended[:, :, : band_rows + H, :], upper_rows], axis=2)
    advected = depart_values(
        extended,
        half_rows,
        H,
        lat_pos * band_rows,
        lon_pos * sector_cols,
        lon_pos * sector_cols - WL,
        row_shift,
        col_shift,
        lon_weight,
    )
    row_data = lax.all_to_all(advected, "lon", split_axis=2, concat_axis=3, tiled=True)
    lat_rows = first_row + jnp.arange(row_count, dtype=jnp.int32)
    per_row = jnp.moveaxis(row_data, 2, 0)

    def spectrum_of_row(row_item):
        return row_spectrum(row_item[0], row_item[1], pair_of_slot)

    spectra = lax.map(spectrum_of_row, (per_row, lat_rows))
    gathered = jax.tree.map(
        lambda part, own: part.astype(own.dtype),
        lax.all_to_all(shortened(spectra), "lon", split_axis=1, concat_axis=0, tiled=True),
        spectra,
    )
    slot_count = legendre.shape[1]
    pair_ids = lax.dynamic_slice_in_dim(pair_of_slot, lon_pos * slot_count, slot_count)
    partial_sum = analyse(legendre, gathered, pair_ids)
    spectral_total = lax.psum(partial_sum, "lat")
    spectral_solution = helmholtz_solve(spectral_total, pair_ids, helm_coeff)
    fourier_rows = synthesise(legendre, spectral_solution, pair_ids)
    return (spectral_solution, fourier_rows)


def solution(mesh):
    return jax.shard_map(
        on_device,
        mesh=mesh,
        in_specs=(
            P(None, None, "lat", "lon"),
            P(None, "lat", "lon"),
            P(None, "lat", "lon"),
            P(None, "lat", "lon"),
            P(),
            P("lat", "lon", None),
            P(),
        ),
        out_specs=(P("lon", None, None, None), P("lon", None, None, None, None, "lat")),
        check_vma=False,
    )
```

profile of v0, /device:TPU:1, one launch (start us, length us, event | category | flops | bytes accessed | tf_op | source)
XLA Modules:
  0.0 365.4 jit_solution(12377830376043378094)
XLA Ops:
  7.2 2.1 fusion.132
  9.3 1.3 collective-permute-start.1
  10.6 6.4 %collective-permute-start = (bf16[8,2,64,10]{3,2,1,0:T(8,128)(2,1)}, bf16[8,2,64,10]{3,2,1,0:T(8,128)(2,1)S(1)}, u32[]{:S(2)}, u32[]{:S(2)}) collective-permute-start(bf16[8,2,64,10]{3,2,1,0:T(8,128)(2,1)} %get-tuple-element.37), channel_id=1, source_target_pairs={{0,1},{1,2},{2,3},{3,4},{4,5},{5,6},{6,7},{7,8},{8,9},{9,10},{10,1... | collective-permute-start | bytes 61448 | tf_op jit(solution)/shard_map/ppermute | solution.py:22
  17.4 0.8 fusion.72
  18.1 0.7 broadcast_compare_fusion
  18.8 0.8 compare_select_fusion.3
  20.1 0.6 broadcast_subtract_fusion
  20.7 0.9 fusion.69
  22.0 0.8 fusion.122
  22.7 73.0 %fusion.10 = (bf16[1040,128,2,1]{1,0,3,2:T(8,128)(2,1)}, bf16[1040,128,2,1]{1,0,3,2:T(8,128)(2,1)}, bf16[1040,128,2,1]{1,0,3,2:T(8,128)(2,1)}, bf16[1040,128,2,1...) fusion(pred[128,2]{0,1:T(4,128)(4,1)S(1)} %get-tuple-element.85, ...), kind=kLoop, calls=%fused_computation.30 | loop fusion | flops 22630400 | bytes 5332249 | tf_op jit(solution)/shard_map/convert
  95.7 0.8 fusion.120
  96.6 14.2 %collective-permute-start.3 = (bf16[8,2,1,85]{3,2,1,0:T(2,128)(2,1)S(1)}, bf16[8,2,1,85]{3,2,1,0:T(2,128)(2,1)S(1)}, u32[]{:S(2)}, u32[]{:S(2)}) collective-permute-start(bf16[8,2,1,85]{3,2,1,0:T(2,128)(2,1)S(1)} %get-tuple-element.36), channel_id=1, source_target_pairs={{64,0},{128,64},{192,128},{256,192},{320,256},{384,320},{448,384},... | collective-permute-start | bytes 8168 | tf_op jit(solution)/shard_map/ppermute | solution.py:23
  110.9 0.8 fusion.118
  111.6 0.6 convert_element_type.248
  112.3 2.1 collective-permute-start.2
  114.4 0.9 collective-permute-done.2
  115.3 1.4 pad_maximum_fusion
  117.0 2.1 copy.61
  119.0 18.4 %gather_fusion.1 = bf16[8320,8]{1,0:T(8,128)(2,1)} fusion(bf16[8,11220]{0,1:T(8,128)(2,1)} %copy.61, s32[9216]{0:T(1024)S(1)} %pad_clamp_fusion), kind=kCustom, calls=%fused_computation.1 | custom fusion | bytes 299520 | tf_op jit(solution)/shard_map/gather | solution.py:57
  137.4 2.1 copy.64
  139.5 0.5 reshape.889
  140.1 18.4 %gather_fusion = bf16[8320,8]{1,0:T(8,128)(2,1)} fusion(bf16[8,11220]{0,1:T(8,128)(2,1)} %copy.61, s32[9216]{0:T(1024)S(1)} %pad_clamp_fusion.1), kind=kCustom, calls=%fused_computation | custom fusion | bytes 299520 | tf_op jit(solution)/shard_map/gather | solution.py:56
  158.5 2.1 copy.62
  160.6 0.5 reshape.888
  161.1 1.0 fusion.54
  162.1 1.0 copy.65
  163.1 13.3 %all-to-all-start = ((bf16[8,2,64,65]{3,1,0,2:T(2,128)(2,1)}), bf16[8,2,64,65]{3,1,0,2:T(2,128)(2,1)S(1)}, u32[]{:S(2)}, u32[]{:S(2)}) async-start(bf16[8,2,64,65]{3,1,0,2:T(2,128)(2,1)} %copy.65), calls=%async_computation | async-start | bytes 524288 | tf_op jit(solution)/shard_map/all_to_all | solution.py:163
  177.0 13.5 %all-to-all-done = bf16[8,2,64,65]{3,1,0,2:T(2,128)(2,1)S(1)} async-done(((bf16[8,2,64,65]{3,1,0,2:T(2,128)(2,1)}), bf16[8,2,64,65]{3,1,0,2:T(2,128)(2,1)S(1)}, u32[]{:S(2)}, u32[]{:S(2)}) %all-to-all-start) | async-done | bytes 133152 | tf_op jit(solution)/shard_map/all_to_all | solution.py:163
  190.4 4.0 %copy.66 = bf16[8,2,64,65]{0,1,3,2:T(2,128)(2,1)} copy(bf16[8,2,64,65]{3,1,0,2:T(2,128)(2,1)S(1)} %all-to-all-done) | data formatting | bytes 266240 | tf_op jit(solution)/shard_map/all_to_all | solution.py:163
  194.4 4.8 %copy.87 = bf16[8,2,1040,4,1,1]{2,0,3,1,5,4:T(8,128)(2,1)S(1)} copy(bf16[8,2,1040,4,1,1]{0,1,3,2,5,4:T(2,128)(2,1)} %bitcast.175) | data formatting | bytes 266240 | tf_op jit(solution)/shard_map/while/body/eval_jaxpr/reshape | solution.py:66
  199.3 1.5 fusion.41
  200.9 0.3 fusion.40
  201.6 0.3 copy-done.7
  202.5 0.6 copy-done.5
  203.7 0.6 copy-done.3
  205.2 0.5 broadcast.1540
  205.7 1.7 reduce.2
  207.4 0.8 reshape.901
  208.2 5.1 %all-to-all-start.1 = ((bf16[64,2,320]{2,1,0:T(2,128)(2,1)}), bf16[64,2,320]{2,1,0:T(2,128)(2,1)S(1)}, u32[]{:S(2)}, u32[]{:S(2)}) async-start(bf16[64,2,320]{2,1,0:T(2,128)(2,1)} %reshape.901), calls=%async_computation.1 | async-start | bytes 196608 | tf_op jit(solution)/shard_map/all_to_all | solution.py:173
  213.6 10.9 %all-to-all-done.1 = bf16[64,2,320]{2,1,0:T(2,128)(2,1)S(1)} async-done(((bf16[64,2,320]{2,1,0:T(2,128)(2,1)}), bf16[64,2,320]{2,1,0:T(2,128)(2,1)S(1)}, u32[]{:S(2)}, u32[]{:S(2)}) %all-to-all-start.1) | async-done | bytes 81952 | tf_op jit(solution)/shard_map/all_to_all | solution.py:173
  224.7 1.0 bitcast_reduce_fusion
  225.7 2.4 fusion.55
  228.2 5.4 %reshape.866 = f32[10,2,2,8,2,1281]{5,4,3,2,1,0:T(2,128)} reshape(f32[10,64,1281]{2,1,0:T(8,128)} %fusion.55) | data formatting | bytes 6558720 | tf_op jit(solution)/shard_map/reshape | solution.py:109
  233.5 3.3 fusion.131
  237.1 1.0 fusion.53
  238.2 116.4 %all-reduce.3.cloned.1.call-done = f32[10,2,8,1281]{3,2,1,0:T(8,128)} async-done(((f32[10,2,8,1281]{3,2,1,0:T(8,128)}), f32[10,2,8,1281]{3,2,1,0:T(8,128)}) %all-reduce.3.cloned.1.call-update) | async-done | bytes 819856 | tf_op jit(solution)/shard_map/psum | solution.py:179
  354.7 2.2 fusion.129
  357.1 1.4 fusion.1
  (118 shorter events, 5.4 us)
Async XLA Ops:
  7.2 218.5 %copy-start = (bf16[64,10,1281]{2,0,1:T(8,128)(2,1)S(1)}, bf16[64,10,1281]{2,0,1:T(8,128)(2,1)}, u32[]{:S(2)}) copy-start(bf16[64,10,1281]{2,0,1:T(8,128)(2,1)} %param.12) | copy-start | bytes 4919044
  7.2 9.8 %copy-start.27 = (s32[640]{0:T(1024)S(1)}, s32[640]{0:T(1024)}, u32[]{:S(2)}) copy-start(s32[640]{0:T(1024)} %param.11) | copy-start | bytes 7684
  7.2 11.6 %copy-start.16 = (s32[2,64,65]{2,1,0:T(8,128)S(1)}, s32[2,64,65]{2,1,0:T(8,128)}, u32[]{:S(2)}) copy-start(s32[2,64,65]{2,1,0:T(8,128)} %param.9) | copy-start | bytes 99844
  7.2 11.6 %copy-start.17 = (s32[2,64,65]{2,1,0:T(8,128)S(1)}, s32[2,64,65]{2,1,0:T(8,128)}, u32[]{:S(2)}) copy-start(s32[2,64,65]{2,1,0:T(8,128)} %param.8) | copy-start | bytes 99844
  7.2 12.9 %copy-start.15 = (bf16[2,64,65]{2,1,0:T(8,128)(2,1)S(1)}, bf16[2,64,65]{2,1,0:T(8,128)(2,1)}, u32[]{:S(2)}) copy-start(bf16[2,64,65]{2,1,0:T(8,128)(2,1)} %param.10) | copy-start | bytes 49924
  7.2 14.6 %copy-start.28 = (f32[8]{0:T(128)S(1)}, f32[8]{0:T(128)}, u32[]{:S(2)}) copy-start(f32[8]{0:T(128)} %param.13) | copy-start | bytes 100
  9.3 87.2 %collective-permute-start.1 = (bf16[8,2,64,10]{3,2,1,0:T(8,128)(2,1)}, bf16[8,2,64,10]{3,2,1,0:T(8,128)(2,1)S(1)}, u32[]{:S(2)}, u32[]{:S(2)}) collective-permute-start(bf16[8,2,64,10]{3,2,1,0:T(8,128)(2,1)} %get-tuple-element.38), channel_id=1, source_target_pairs={{1,0},{2,1},{3,2},{4,3},{5,4},{6,5},{7,6},{8,7},{9,8},{10,9},{11,1... | collective-permute-start | bytes 61448 | tf_op jit(solution)/shard_map/ppermute | solution.py:23
  10.6 85.9 %collective-permute-start = (bf16[8,2,64,10]{3,2,1,0:T(8,128)(2,1)}, bf16[8,2,64,10]{3,2,1,0:T(8,128)(2,1)S(1)}, u32[]{:S(2)}, u32[]{:S(2)}) collective-permute-start(bf16[8,2,64,10]{3,2,1,0:T(8,128)(2,1)} %get-tuple-element.37), channel_id=1, source_target_pairs={{0,1},{1,2},{2,3},{3,4},{4,5},{5,6},{6,7},{7,8},{8,9},{9,10},{10,1... | collective-permute-start | bytes 61448 | tf_op jit(solution)/shard_map/ppermute | solution.py:22
  17.1 78.6 %copy-start.23 = (s32[128,2]{0,1:T(2,128)}, s32[128,2]{0,1:T(2,128)S(1)}, u32[]{:S(2)}) copy-start(s32[128,2]{0,1:T(2,128)S(1)} %pad_add_fusion.4) | copy-start | bytes 3076
  17.1 78.6 %copy-start.25 = (s32[128,2]{0,1:T(2,128)}, s32[128,2]{0,1:T(2,128)S(1)}, u32[]{:S(2)}) copy-start(s32[128,2]{0,1:T(2,128)S(1)} %get-tuple-element.92) | copy-start | bytes 3076
  22.7 73.8 %copy-start.1 = (bf16[8,2,64,65]{3,2,1,0:T(8,128)(2,1)S(1)}, bf16[8,2,64,65]{3,2,1,0:T(8,128)(2,1)}, u32[]{:S(2)}) copy-start(bf16[8,2,64,65]{3,2,1,0:T(8,128)(2,1)} %param.7) | copy-start | bytes 399364
  96.5 17.9 %copy-start.2 = (bf16[8,2,64,10]{3,2,1,0:T(8,128)(2,1)}, bf16[8,2,64,10]{3,2,1,0:T(8,128)(2,1)S(1)}, u32[]{:S(2)}) copy-start(bf16[8,2,64,10]{3,2,1,0:T(8,128)(2,1)S(1)} %collective-permute-done) | copy-start | bytes 61444
  96.6 17.7 %collective-permute-start.3 = (bf16[8,2,1,85]{3,2,1,0:T(2,128)(2,1)S(1)}, bf16[8,2,1,85]{3,2,1,0:T(2,128)(2,1)S(1)}, u32[]{:S(2)}, u32[]{:S(2)}) collective-permute-start(bf16[8,2,1,85]{3,2,1,0:T(2,128)(2,1)S(1)} %get-tuple-element.36), channel_id=1, source_target_pairs={{64,0},{128,64},{192,128},{256,192},{320,256},{384,320},{448,384},... | collective-permute-start | bytes 8168 | tf_op jit(solution)/shard_map/ppermute | solution.py:23
  112.3 3.1 collective-permute-start.2
  161.1 15.3 %copy-start.26 = (s32[128,2]{0,1:T(2,128)S(1)}, s32[128,2]{0,1:T(2,128)}, u32[]{:S(2)}) copy-start(s32[128,2]{0,1:T(2,128)} %copy-done.25) | copy-start | bytes 3076
  161.1 15.6 %copy-start.14 = (f32[10,1,1281]{2,1,0:T(1,128)S(1)}, f32[10,1,1281]{2,1,0:T(1,128)}, u32[]{:S(2)}) copy-start(f32[10,1,1281]{2,1,0:T(1,128)} %fusion.69) | copy-start | bytes 153724
  161.1 15.6 %copy-start.24 = (s32[128,2]{0,1:T(2,128)S(1)}, s32[128,2]{0,1:T(2,128)}, u32[]{:S(2)}) copy-start(s32[128,2]{0,1:T(2,128)} %copy-done.23) | copy-start | bytes 3076
  163.1 27.3 %all-to-all-start = ((bf16[8,2,64,65]{3,1,0,2:T(2,128)(2,1)}), bf16[8,2,64,65]{3,1,0,2:T(2,128)(2,1)S(1)}, u32[]{:S(2)}, u32[]{:S(2)}) async-start(bf16[8,2,64,65]{3,1,0,2:T(2,128)(2,1)} %copy.65), calls=%async_computation | async-start | bytes 524288 | tf_op jit(solution)/shard_map/all_to_all | solution.py:163
  194.4 4.8 %copy-start.11 = (bf16[1040,128,2,1]{1,0,3,2:T(8,128)(2,1)S(1)}, bf16[1040,128,2,1]{1,0,3,2:T(8,128)(2,1)}, u32[]{:S(2)}) copy-start(bf16[1040,128,2,1]{1,0,3,2:T(8,128)(2,1)} %get-tuple-element.67) | copy-start | bytes 1597444
  199.2 1.5 copy-start.18
  199.3 1.6 copy-start.9
  199.3 1.6 copy-start.10
  200.8 0.7 copy-start.19
  200.8 0.7 copy-start.20
  200.9 1.0 copy-start.7
  200.9 1.2 copy-start.8
  201.5 0.9 copy-start.21
  201.6 0.9 copy-start.22
  202.1 1.0 copy-start.5
  202.1 1.2 copy-start.6
  203.3 1.0 copy-start.3
  203.3 1.2 copy-start.4
  204.8 8.7 %copy-start.12 = (f32[10,1,1281]{2,1,0:T(1,128)S(1)}, f32[10,1,1281]{2,1,0:T(1,128)}, u32[]{:S(2)}) copy-start(f32[10,1,1281]{2,1,0:T(1,128)} %get-tuple-element.79) | copy-start | bytes 153724
  204.8 8.7 %copy-start.13 = (f32[10,1,1281]{2,1,0:T(1,128)S(1)}, f32[10,1,1281]{2,1,0:T(1,128)}, u32[]{:S(2)}) copy-start(f32[10,1,1281]{2,1,0:T(1,128)} %get-tuple-element.80) | copy-start | bytes 153724
  208.2 16.3 %all-to-all-start.1 = ((bf16[64,2,320]{2,1,0:T(2,128)(2,1)}), bf16[64,2,320]{2,1,0:T(2,128)(2,1)S(1)}, u32[]{:S(2)}, u32[]{:S(2)}) async-start(bf16[64,2,320]{2,1,0:T(2,128)(2,1)} %reshape.901), calls=%async_computation.1 | async-start | bytes 196608 | tf_op jit(solution)/shard_map/all_to_all | solution.py:173
  213.2 141.4 %all-reduce.3.cloned.1.call-start = ((), (), s32[]{:S(2)}) async-start(), calls=%async_computation.2 | async-start | bytes 1802240 | tf_op jit(solution)/shard_map/psum | solution.py:179
Sparse Core Ops, SparseCore 0:
  238.3 116.3 all-reduce.2
where the time goes:
time: 366 us; the launch traced here: 365 us
  waiting for transfers between devices  142 us (39%)
  other arithmetic  88.9 us (24%)
  local copies, waits for them, and re-layouts  70.7 us (19%)
  starting transfers between devices  42.6 us (12%)
  between operations  14.9 us (4%)
  matrix products  6.56 us (2%)
    psum x1, waiting for transfers between devices, on_device(): spectral_total = lax.psum(partial_sum, 'lat')  116 us
    another operation x1, other arithmetic  73 us
    gather x2, local copies, waits for them, and re-layouts, depart_values(): left_value = flat_field[:, flat_index].astype(jnp.float32)  20.5 us
    gather x2, local copies, waits for them, and re-layouts, depart_values(): right_value = flat_field[:, flat_index + 1].astype(jnp.float32)  20.5 us
    ppermute x2, starting transfers between devices, extended_2(): after = lax.ppermute(initial, axis, down)  15.5 us
    all_to_all x1, waiting for transfers between devices, on_device(): lax.all_to_all(advected, 'lon', split_axis=2, concat_axis=3, tiled=True)  13.5 us
    all_to_all x1, starting transfers between devices, on_device(): lax.all_to_all(advected, 'lon', split_axis=2, concat_axis=3, tiled=True)  13.3 us
    all_to_all x1, waiting for transfers between devices, on_device(): lax.all_to_all(shortened(spectra), 'lon', split_axis=1, concat_axis=0, ti...  10.9 us
  transfers between devices with their start and end apart: 7, of which 4 were waited for; matrix products, arithmetic and copies ran while one was open for 22% of the time, Pallas kernels for 0%

commit v1 on v0

--- a/solution.py
+++ b/solution.py
@@ -60,37 +60,55 @@
     return jnp.where(lon_index < length, blended, 0.0).astype(jnp.bfloat16)
 
 
+def phase_table(orders, steps, quarter_len):
+    phase_idx = orders[None] * steps[:, None, None] % quarter_len
+    angles = phase_idx.astype(jnp.float32) * (2.0 * math.pi) / quarter_len.astype(jnp.float32)
+    return jnp.cos(angles), jnp.sin(angles)
+
+
 def row_spectrum(row_data, lat_index, pair_of_slot):
     length = 20 + 4 * lat_index
     quarter_len = length // 4
     quarters = row_data.reshape(row_data.shape[0], 2, -1, 4)
-    slots = jnp.arange(quarters.shape[2], dtype=jnp.int32)[:, None, None]
+    slot_count = quarters.shape[2]
+    inner_n = 32
+    outer_n = -(-slot_count // inner_n)
     offsets = jnp.arange(4, dtype=jnp.int32)[None, None, :]
     norm_scale = 1.0 / jnp.sqrt(length.astype(jnp.float32))
-    block_size = math.gcd(PAIRS, 128)
-    pieces = []
-    for block_start in range(0, PAIRS, block_size):
-        pair_ids = pair_of_slot[block_start : block_start + block_size]
-        pair_orders = jnp.stack([pair_ids, TRUNC - pair_ids], axis=1)
-        orders = pair_orders[None]
-        phase_idx = orders * slots % quarter_len
-        angles = phase_idx.astype(jnp.float32) * (2.0 * math.pi) / quarter_len.astype(jnp.float32)
-        usable = (2 * orders < length) & (slots < quarter_len)
-        cosine = jnp.where(usable, jnp.cos(angles), 0.0)
-        minus_sine = jnp.where(usable, -jnp.sin(angles), 0.0)
-        factors = jnp.stack([cosine, minus_sine], axis=-1).astype(jnp.bfloat16)
-        inner = jnp.einsum(
-            "aser,fhab->serfhb", factors, quarters, preferred_element_type=jnp.float32
-        )
-        twist_idx = pair_orders[:, :, None] * offsets % length
-        twist = twist_idx.astype(jnp.float32) * (2.0 * math.pi) / length.astype(jnp.float32)
-        twist_cos = jnp.cos(twist)[:, :, None, None, :]
-        twist_sin = jnp.sin(twist)[:, :, None, None, :]
-        real_part = jnp.sum(inner[:, :, 0] * twist_cos + inner[:, :, 1] * twist_sin, axis=-1)
-        imag_part = jnp.sum(inner[:, :, 1] * twist_cos - inner[:, :, 0] * twist_sin, axis=-1)
-        spectrum = jnp.stack([real_part, imag_part], axis=2)
-        pieces.append((spectrum * norm_scale).astype(jnp.bfloat16).reshape(block_size, -1))
-    return jnp.concatenate(pieces, axis=0)
+    pair_orders = jnp.stack([pair_of_slot, TRUNC - pair_of_slot], axis=1)
+    outer_cos, outer_sin = phase_table(
+        pair_orders, jnp.arange(outer_n, dtype=jnp.int32) * inner_n, quarter_len
+    )
+    inner_cos, inner_sin = phase_table(pair_orders, jnp.arange(inner_n, dtype=jnp.int32), quarter_len)
+    cosine = outer_cos[:, None] * inner_cos[None] - outer_sin[:, None] * inner_sin[None]
+    minus_sine = -(outer_sin[:, None] * inner_cos[None] + outer_cos[:, None] * inner_sin[None])
+    cosine = cosine.reshape((outer_n * inner_n,) + cosine.shape[2:])[:slot_count]
+    minus_sine = minus_sine.reshape((outer_n * inner_n,) + minus_sine.shape[2:])[:slot_count]
+    slots = jnp.arange(slot_count, dtype=jnp.int32)[:, None, None]
+    usable = (2 * pair_orders[None] < length) & (slots < quarter_len)
+    factors = jnp.stack(
+        [jnp.where(usable, cosine, 0.0), jnp.where(usable, minus_sine, 0.0)], axis=-1
+    ).astype(jnp.bfloat16)
+    inner = jnp.einsum("aser,fhab->serfhb", factors, quarters, preferred_element_type=jnp.float32)
+    twist_idx = pair_orders[:, :, None] * offsets % length
+    twist = twist_idx.astype(jnp.float32) * (2.0 * math.pi) / length.astype(jnp.float32)
+    twist_cos = jnp.cos(twist)[:, :, None, None, :]
+    twist_sin = jnp.sin(twist)[:, :, None, None, :]
+    real_part = jnp.sum(inner[:, :, 0] * twist_cos + inner[:, :, 1] * twist_sin, axis=-1)
+    imag_part = jnp.sum(inner[:, :, 1] * twist_cos - inner[:, :, 0] * twist_sin, axis=-1)
+    spectrum = jnp.stack([real_part, imag_part], axis=2)
+    return (spectrum * norm_scale).astype(jnp.bfloat16).reshape(PAIRS, -1)
+
+
+def lat_sum(value):
+    peers = lax.axis_size("lat")
+    count = value.size
+    pad = (-count) % (peers * 1024)
+    flat = jnp.pad(value.reshape(-1), (0, pad)).reshape(peers, -1, 1024)
+    pieces = lax.all_to_all(flat, "lat", 0, 0, tiled=True)
+    reduced = jnp.sum(pieces, axis=0, keepdims=True)
+    whole = lax.all_gather(reduced, "lat", axis=0, tiled=True)
+    return whole.reshape(-1)[:count].reshape(value.shape)
 
 
 def column_terms(pair_ids):
@@ -176,7 +194,7 @@
     slot_count = legendre.shape[1]
     pair_ids = lax.dynamic_slice_in_dim(pair_of_slot, lon_pos * slot_count, slot_count)
     partial_sum = analyse(legendre, gathered, pair_ids)
-    spectral_total = lax.psum(partial_sum, "lat")
+    spectral_total = lat_sum(partial_sum)
     spectral_solution = helmholtz_solve(spectral_total, pair_ids, helm_coeff)
     fourier_rows = synthesise(legendre, spectral_solution, pair_ids)
     return (spectral_solution, fourier_rows)

time: 366 us -> 233 us (0.64)
  waiting for transfers between devices: 142 us -> 48.1 us
  other arithmetic: 88.9 us -> 28 us
  blocking collectives: 0 us -> 17.4 us
  between operations: 14.9 us -> 1.18 us
  starting transfers between devices: 42.6 us -> 50.9 us
  local copies, waits for them, and re-layouts: 70.7 us -> 78.3 us
    psum x1 -> x0, waiting for transfers between devices: 116 us -> none  [on_device(): spectral_total = lax.psum(partial_sum, 'lat')]
    another operation x5 -> x2, other arithmetic: 73 us -> 3.27 us  [the longest x1 3.26 us: row_spectrum(): jnp.stack([jnp.where(usable, cosine, 0.0), jnp.where(usable, minus_sine,...]
    all_to_all x0 -> x1, waiting for transfers between devices: none -> 26.1 us  [lat_sum(): pieces = lax.all_to_all(flat, 'lat', 0, 0, tiled=True)]
    all_gather x0 -> x1, blocking collectives: none -> 17.4 us  [lat_sum(): whole = lax.all_gather(reduced, 'lat', axis=0, tiled=True)]
    all_to_all x0 -> x1, starting transfers between devices: none -> 10.1 us  [lat_sum(): pieces = lax.all_to_all(flat, 'lat', 0, 0, tiled=True)]
    cos x0 -> x2, other arithmetic: none -> 5.02 us  [phase_table(): return (jnp.cos(angles), jnp.sin(angles))]
    squeeze x0 -> x2, local copies, waits for them, and re-layouts: none -> 4.09 us  [analyse(): return chosen[:, :, :, 0] + parity[:, None, None, :] * chosen[:, :, :, 1]]
  transfers between devices with their start and end apart: 7 -> 7, of which waited for: 4 -> 4; matrix products, arithmetic and copies ran while one was open for 22% -> 9% of each run, Pallas kernels for 0% -> 0%
where the time goes in v1:
time: 233 us; the launch traced here: 232 us
  local copies, waits for them, and re-layouts  78.3 us (34%)
  starting transfers between devices  50.9 us (22%)
  waiting for transfers between devices  48.1 us (21%)
  other arithmetic  28 us (12%)
  blocking collectives  17.4 us (7%)
  matrix products  8.28 us (4%)
    all_to_all x1, waiting for transfers between devices, lat_sum(): pieces = lax.all_to_all(flat, 'lat', 0, 0, tiled=True)  26.1 us
    gather x2, local copies, waits for them, and re-layouts, depart_values(): left_value = flat_field[:, flat_index].astype(jnp.float32)  20.6 us
    gather x2, local copies, waits for them, and re-layouts, depart_values(): right_value = flat_field[:, flat_index + 1].astype(jnp.float32)  20.6 us
    all_gather x1, blocking collectives, lat_sum(): whole = lax.all_gather(reduced, 'lat', axis=0, tiled=True)  17.4 us
    all_to_all x1, starting transfers between devices, on_device(): lax.all_to_all(advected, 'lon', split_axis=2, concat_axis=3, tiled=True)  14.5 us
    ppermute x2, starting transfers between devices, extended_2(): after = lax.ppermute(initial, axis, down)  12.9 us
    all_to_all x1, waiting for transfers between devices, on_device(): lax.all_to_all(advected, 'lon', split_axis=2, concat_axis=3, tiled=True)  12.4 us
    all_to_all x1, starting transfers between devices, lat_sum(): pieces = lax.all_to_all(flat, 'lat', 0, 0, tiled=True)  10.1 us
  transfers between devices with their start and end apart: 7, of which 4 were waited for; matrix products, arithmetic and copies ran while one was open for 9% of the time, Pallas kernels for 0%

profile of v1, /device:TPU:1, one launch (start us, length us, event | category | flops | bytes accessed | tf_op | source)
XLA Modules:
  0.0 232.2 jit_solution(15703510390597631062)
XLA Ops:
  0.6 2.0 fusion.61
  2.7 5.7 %collective-permute-start = (bf16[8,2,64,10]{3,2,1,0:T(8,128)(2,1)}, bf16[8,2,64,10]{3,2,1,0:T(8,128)(2,1)S(1)}, u32[]{:S(2)}, u32[]{:S(2)}) collective-permute-start(bf16[8,2,64,10]{3,2,1,0:T(8,128)(2,1)} %get-tuple-element.31), channel_id=1, source_target_pairs={{0,1},{1,2},{2,3},{3,4},{4,5},{5,6},{6,7},{7,8},{8,9},{9,10},{10,1... | collective-permute-start | bytes 61448 | tf_op jit(solution)/shard_map/ppermute | solution.py:22
  8.4 1.3 collective-permute-start.1
  11.2 2.2 fusion.36
  13.4 2.8 %fusion.29 = (f32[33,640,2]{1,0,2:T(8,128)S(1)}, f32[33,640,2]{1,0,2:T(8,128)S(1)}) fusion(f32[]{:T(128)S(6)} %convert_element_type.115, pred[]{:T(512)S(6)} %lt.113, s32[]{:T(128)S(6)} %select_n.166, s32[33]{0:T(128)S(1)} %iota_multiply_fusion.1, s32[640,2]{0,1:T(2,128)S(1)} %pad_add_fusion), kind=kLoop, calls=%fused_computation.68 | loop fusion | flops 464640 | bytes 343181 | tf_op jit(solution)/shard_map/while/body/eval_jaxpr/cos | solution.py:66
  16.3 1.7 compare_select_fusion.3
  18.4 0.8 broadcast_subtract_fusion
  19.2 0.8 broadcast_subtract_fusion.2
  19.9 0.8 fusion.34
  20.7 2.0 multiply_subtract_fusion
  22.8 3.3 %fusion.6 = (bf16[1040,640,2,1]{1,0,3,2:T(8,128)(2,1)}, bf16[1040,640,2,1]{1,0,3,2:T(8,128)(2,1)}) fusion(bf16[1056,640,2]{1,0,2:T(8,128)(2,1)S(1)} %bitcast.65, pred[640,2]{0,1:T(4,128)(4,1)S(1)} %multiply_compare_fusion, pred[1040]{0:T(1024)(128)(4,1)S(1)} %iota_compare_fusion.2, bf16[1056,640,2]{1,0,2:T(8,128)(2,1)S(1)} %bitcast.66), kind=kLoop, calls=%fused_computation.13 | loop fusion | flops 3993600 | bytes 10651920 | tf_op jit(solution)/shard_map/while/body/eval_jaxpr/stack | solution.py:89
  26.2 11.6 %collective-permute-start.3 = (bf16[8,2,1,85]{3,2,1,0:T(2,128)(2,1)S(1)}, bf16[8,2,1,85]{3,2,1,0:T(2,128)(2,1)S(1)}, u32[]{:S(2)}, u32[]{:S(2)}) collective-permute-start(bf16[8,2,1,85]{3,2,1,0:T(2,128)(2,1)S(1)} %get-tuple-element.28), channel_id=1, source_target_pairs={{64,0},{128,64},{192,128},{256,192},{320,256},{384,320},{448,384},... | collective-permute-start | bytes 8168 | tf_op jit(solution)/shard_map/ppermute | solution.py:23
  37.9 2.1 collective-permute-start.2
  40.0 0.9 collective-permute-done.2
  41.7 2.1 copy.38
  43.7 18.6 %gather_fusion.1 = bf16[8320,8]{1,0:T(8,128)(2,1)} fusion(bf16[8,11220]{0,1:T(8,128)(2,1)} %copy.38, s32[9216]{0:T(1024)S(1)} %pad_clamp_fusion), kind=kCustom, calls=%fused_computation.1 | custom fusion | bytes 299520 | tf_op jit(solution)/shard_map/gather | solution.py:57
  62.3 2.1 copy.41
  64.9 18.6 %gather_fusion = bf16[8320,8]{1,0:T(8,128)(2,1)} fusion(bf16[8,11220]{0,1:T(8,128)(2,1)} %copy.38, s32[9216]{0:T(1024)S(1)} %pad_clamp_fusion.1), kind=kCustom, calls=%fused_computation | custom fusion | bytes 299520 | tf_op jit(solution)/shard_map/gather | solution.py:56
  83.5 2.1 copy.39
  86.2 1.0 copy.42
  87.2 14.5 %all-to-all-start = ((bf16[8,2,64,65]{3,1,0,2:T(2,128)(2,1)}), bf16[8,2,64,65]{3,1,0,2:T(2,128)(2,1)S(1)}, u32[]{:S(2)}, u32[]{:S(2)}) async-start(bf16[8,2,64,65]{3,1,0,2:T(2,128)(2,1)} %copy.42), calls=%async_computation | async-start | bytes 524288 | tf_op jit(solution)/shard_map/all_to_all | solution.py:181
  101.7 0.9 fusion.44
  103.3 12.4 %all-to-all-done = bf16[8,2,64,65]{3,1,0,2:T(2,128)(2,1)S(1)} async-done(((bf16[8,2,64,65]{3,1,0,2:T(2,128)(2,1)}), bf16[8,2,64,65]{3,1,0,2:T(2,128)(2,1)S(1)}, u32[]{:S(2)}, u32[]{:S(2)}) %all-to-all-start) | async-done | bytes 133152 | tf_op jit(solution)/shard_map/all_to_all | solution.py:181
  115.6 4.0 %copy.43 = bf16[8,2,64,65]{0,1,3,2:T(2,128)(2,1)} copy(bf16[8,2,64,65]{3,1,0,2:T(2,128)(2,1)S(1)} %all-to-all-done) | data formatting | bytes 266240 | tf_op jit(solution)/shard_map/all_to_all | solution.py:181
  119.6 4.5 %fusion.2 = f32[640,2,2,8,2,4]{0,3,5,4,2,1:T(8,128)S(1)} fusion(bf16[1040,640,2,1]{1,0,3,2:T(8,128)(2,1)} %get-tuple-element.42, bf16[1040,640,2,1]{1,0,3,2:T(8,128)(2,1)} %get-tuple-element.41, bf16[8,2,1040,4,1,1]{0,1,3,2,5,4:T(2,128)(2,1)} %bitcast.68), kind=kOutput, calls=%fused_computation.9 | convolution fusion | flops 351436800 | bytes 6113280 | tf_op jit(solution)/shard_map/while/body/eval_jaxpr/aser,fhab->serfhb/dot_general | solution.py:92
  125.0 1.7 reduce.6
  126.7 0.8 reshape.540
  127.5 5.6 %all-to-all-start.1 = ((bf16[64,2,320]{2,1,0:T(2,128)(2,1)}), bf16[64,2,320]{2,1,0:T(2,128)(2,1)}, u32[]{:S(2)}, u32[]{:S(2)}) async-start(bf16[64,2,320]{2,1,0:T(2,128)(2,1)} %reshape.540), calls=%async_computation.1 | async-start | bytes 196608 | tf_op jit(solution)/shard_map/all_to_all | solution.py:191
  133.9 1.5 stack.58
  135.4 8.7 %all-to-all-done.1 = bf16[64,2,320]{2,1,0:T(2,128)(2,1)} async-done(((bf16[64,2,320]{2,1,0:T(2,128)(2,1)}), bf16[64,2,320]{2,1,0:T(2,128)(2,1)}, u32[]{:S(2)}, u32[]{:S(2)}) %all-to-all-start.1) | async-done | bytes 81952 | tf_op jit(solution)/shard_map/all_to_all | solution.py:191
  144.1 1.4 reshape.541
  145.5 1.0 bitcast_reduce_fusion
  146.6 2.4 %fusion.22 = f32[10,64,1281]{2,1,0:T(8,128)} fusion(bf16[64,10,1281]{2,0,1:T(8,128)(2,1)S(1)} %copy-done, bf16[64,10,64]{2,1,0:T(8,128)(2,1)S(1)} %all_to_all.10), kind=kOutput, calls=%fused_computation.55 | convolution fusion | flops 104939520 | bytes 5000960 | tf_op jit(solution)/shard_map/ksc,ksq->sqc/dot_general | solution.py:125
  149.0 5.4 %reshape.503 = f32[10,2,2,8,2,1281]{5,4,3,2,1,0:T(2,128)} reshape(f32[10,64,1281]{2,1,0:T(8,128)} %fusion.22) | data formatting | bytes 6558720 | tf_op jit(solution)/shard_map/reshape | solution.py:127
  154.5 3.0 %fusion.8 = f32[10,2,8,2,1281]{4,3,2,1,0:T(2,128)S(1)} fusion(f32[10,2,2,8,2,1281]{5,4,3,2,1,0:T(2,128)} %reshape.503, pred[10,1281]{1,0:T(8,128)(4,1)S(1)} %iota_compare_fusion), kind=kLoop, calls=%fused_computation.16 | loop fusion | flops 409920 | bytes 4931850 | tf_op jit(solution)/shard_map/jit(_where)/select_n | solution.py:128
  157.5 5.7 %slice_reduce_fusion = (f32[10,2,8,1281]{3,2,1,0:T(8,128)S(1)}, f32[10,2,8,1281]{3,2,1,0:T(8,128)}) fusion(f32[10,2,8,2,1281]{4,3,2,1,0:T(2,128)S(1)} %fusion.8), kind=kLoop, calls=%fused_computation.20 | loop fusion | bytes 3279360 | tf_op jit(solution)/shard_map/slice | solution.py:129
  163.1 2.6 %squeeze.32 = f32[204960]{0:T(1024)} reshape(f32[10,2,8,1281]{3,2,1,0:T(8,128)} %get-tuple-element.13) | data formatting | bytes 1639680 | tf_op jit(solution)/shard_map/squeeze | solution.py:129
  165.8 1.4 squeeze.33
  167.2 1.5 multiply_add_fusion
  168.8 1.1 reshape.504
  169.9 10.1 %all-to-all-start.2 = ((f32[16,13,1024]{2,1,0:T(8,128)}), f32[16,13,1024]{2,1,0:T(8,128)S(1)}, u32[]{:S(2)}, u32[]{:S(2)}) async-start(f32[16,13,1024]{2,1,0:T(8,128)} %reshape.504), calls=%async_computation.2 | async-start | bytes 2097152 | tf_op jit(solution)/shard_map/all_to_all | solution.py:108
  181.1 0.9 multiply_add_fusion.1
  181.9 26.1 %all-to-all-done.2 = f32[16,13,1024]{2,1,0:T(8,128)S(1)} async-done(((f32[16,13,1024]{2,1,0:T(8,128)}), f32[16,13,1024]{2,1,0:T(8,128)S(1)}, u32[]{:S(2)}, u32[]{:S(2)}) %all-to-all-start.2) | async-done | bytes 852000 | tf_op jit(solution)/shard_map/all_to_all | solution.py:108
  208.1 17.4 %all-gather.1 = f32[16,13,1024]{2,1,0:T(8,128)S(1)} all-gather(f32[1,13,1024]{2,1,0:T(8,128)S(1)} %bitcast.72), channel_id=2, replica_groups=mesh['lat'=16,'lon'=64] {'lat'}, dimensions={0}, use_global_device_ids=true | all-gather | bytes 905216 | tf_op jit(solution)/shard_map/all_gather | solution.py:110
  225.5 1.1 reshape.505
  226.6 1.2 slice.71
  228.5 2.1 fusion.59
  230.8 1.4 fusion.9
  (61 shorter events, 8.4 us)
Async XLA Ops:
  0.6 146.0 %copy-start = (bf16[64,10,1281]{2,0,1:T(8,128)(2,1)S(1)}, bf16[64,10,1281]{2,0,1:T(8,128)(2,1)}, u32[]{:S(2)}) copy-start(bf16[64,10,1281]{2,0,1:T(8,128)(2,1)} %param.12) | copy-start | bytes 4919044
  2.7 23.4 %collective-permute-start = (bf16[8,2,64,10]{3,2,1,0:T(8,128)(2,1)}, bf16[8,2,64,10]{3,2,1,0:T(8,128)(2,1)S(1)}, u32[]{:S(2)}, u32[]{:S(2)}) collective-permute-start(bf16[8,2,64,10]{3,2,1,0:T(8,128)(2,1)} %get-tuple-element.31), channel_id=1, source_target_pairs={{0,1},{1,2},{2,3},{3,4},{4,5},{5,6},{6,7},{7,8},{8,9},{9,10},{10,1... | collective-permute-start | bytes 61448 | tf_op jit(solution)/shard_map/ppermute | solution.py:22
  8.4 17.6 %collective-permute-start.1 = (bf16[8,2,64,10]{3,2,1,0:T(8,128)(2,1)}, bf16[8,2,64,10]{3,2,1,0:T(8,128)(2,1)S(1)}, u32[]{:S(2)}, u32[]{:S(2)}) collective-permute-start(bf16[8,2,64,10]{3,2,1,0:T(8,128)(2,1)} %get-tuple-element.32), channel_id=1, source_target_pairs={{1,0},{2,1},{3,2},{4,3},{5,4},{6,5},{7,6},{8,7},{9,8},{10,9},{11,1... | collective-permute-start | bytes 61448 | tf_op jit(solution)/shard_map/ppermute | solution.py:23
  22.7 3.3 %copy-start.1 = (bf16[8,2,64,65]{3,2,1,0:T(8,128)(2,1)S(1)}, bf16[8,2,64,65]{3,2,1,0:T(8,128)(2,1)}, u32[]{:S(2)}) copy-start(bf16[8,2,64,65]{3,2,1,0:T(8,128)(2,1)} %param.7) | copy-start | bytes 399364
  22.8 15.1 %copy-start.5 = (bf16[2,64,65]{2,1,0:T(8,128)(2,1)S(1)}, bf16[2,64,65]{2,1,0:T(8,128)(2,1)}, u32[]{:S(2)}) copy-start(bf16[2,64,65]{2,1,0:T(8,128)(2,1)} %param.10) | copy-start | bytes 49924
  26.2 13.8 %collective-permute-start.3 = (bf16[8,2,1,85]{3,2,1,0:T(2,128)(2,1)S(1)}, bf16[8,2,1,85]{3,2,1,0:T(2,128)(2,1)S(1)}, u32[]{:S(2)}, u32[]{:S(2)}) collective-permute-start(bf16[8,2,1,85]{3,2,1,0:T(2,128)(2,1)S(1)} %get-tuple-element.28), channel_id=1, source_target_pairs={{64,0},{128,64},{192,128},{256,192},{320,256},{384,320},{448,384},... | collective-permute-start | bytes 8168 | tf_op jit(solution)/shard_map/ppermute | solution.py:23
  37.9 3.1 %collective-permute-start.2 = (bf16[8,2,1,85]{3,2,1,0:T(2,128)(2,1)S(1)}, bf16[8,2,1,85]{3,2,1,0:T(2,128)(2,1)S(1)}, u32[]{:S(2)}, u32[]{:S(2)}) collective-permute-start(bf16[8,2,1,85]{3,2,1,0:T(2,128)(2,1)S(1)} %get-tuple-element.27), channel_id=1, source_target_pairs={{0,64},{64,128},{128,192},{192,256},{256,320},{320,384},{384,448},... | collective-permute-start | bytes 8168 | tf_op jit(solution)/shard_map/ppermute | solution.py:22
  87.2 28.4 %all-to-all-start = ((bf16[8,2,64,65]{3,1,0,2:T(2,128)(2,1)}), bf16[8,2,64,65]{3,1,0,2:T(2,128)(2,1)S(1)}, u32[]{:S(2)}, u32[]{:S(2)}) async-start(bf16[8,2,64,65]{3,1,0,2:T(2,128)(2,1)} %copy.42), calls=%async_computation | async-start | bytes 524288 | tf_op jit(solution)/shard_map/all_to_all | solution.py:181
  127.5 16.6 %all-to-all-start.1 = ((bf16[64,2,320]{2,1,0:T(2,128)(2,1)}), bf16[64,2,320]{2,1,0:T(2,128)(2,1)}, u32[]{:S(2)}, u32[]{:S(2)}) async-start(bf16[64,2,320]{2,1,0:T(2,128)(2,1)} %reshape.540), calls=%async_computation.1 | async-start | bytes 196608 | tf_op jit(solution)/shard_map/all_to_all | solution.py:191
  168.7 11.6 %copy-start.2 = (f32[10,2,1281]{2,1,0:T(2,128)S(1)}, f32[10,2,1281]{2,1,0:T(2,128)}, u32[]{:S(2)}) copy-start(f32[10,2,1281]{2,1,0:T(2,128)} %stack.58) | copy-start | bytes 307444
  168.8 12.2 %copy-start.4 = (f32[10,1281]{1,0:T(8,128)S(1)}, f32[10,1281]{1,0:T(8,128)}, u32[]{:S(2)}) copy-start(f32[10,1281]{1,0:T(8,128)} %get-tuple-element.33) | copy-start | bytes 153724
  168.8 12.2 %copy-start.6 = (f32[8]{0:T(128)S(1)}, f32[8]{0:T(128)}, u32[]{:S(2)}) copy-start(f32[8]{0:T(128)} %param.13) | copy-start | bytes 100
  169.9 38.1 %all-to-all-start.2 = ((f32[16,13,1024]{2,1,0:T(8,128)}), f32[16,13,1024]{2,1,0:T(8,128)S(1)}, u32[]{:S(2)}, u32[]{:S(2)}) async-start(f32[16,13,1024]{2,1,0:T(8,128)} %reshape.504), calls=%async_computation.2 | async-start | bytes 2097152 | tf_op jit(solution)/shard_map/all_to_all | solution.py:108
  228.5 2.1 copy-start.3

commit v2 on v1

--- a/solution.py
+++ b/solution.py
@@ -3,6 +3,7 @@
 import jax
 import jax.numpy as jnp
 from jax import lax
+from jax.experimental import pallas as pl
 from jax.sharding import PartitionSpec as P
 
 TRUNC = 1279
@@ -31,6 +32,21 @@
         return part.astype(jnp.bfloat16) if part.dtype == jnp.float32 else part
 
     return jax.tree.map(short, value)
+
+
+def depart_kernel(ext_ref, code_ref, weight_ref, out_ref):
+    code = code_ref[...]
+    rows, cols = code.shape[1], code.shape[2]
+    left = jnp.zeros(code.shape, jnp.float32)
+    right = left
+    for dr in range(ext_ref.shape[2] - rows + 1):
+        for dc in range(1, ext_ref.shape[3] - cols - 1):
+            window = ext_ref[0, :, dr : dr + rows, dc : dc + cols]
+            key = dr * 64 + dc
+            left = jnp.where(code == key, window, left)
+            right = jnp.where(code == key - 1, window, right)
+    blend = weight_ref[...]
+    out_ref[0] = (1.0 - blend) * left + blend * right
 
 
 def depart_values(
@@ -48,15 +64,21 @@
     length_dep = 20 + 4 * mirror
     shifted = jnp.clip(lon_index + col_shift, 0, length - 1)
     column = jnp.minimum(shifted * length_dep // length, length_dep - 2)
-    hemisphere = jnp.arange(2, dtype=jnp.int32)[:, None, None]
-    flat_index = (hemisphere * height + (target - first_row + low_rows)) * ext_width + (
-        column - col_ext
-    )
-    flat_field = extended.reshape(extended.shape[0], -1)
-    left_value = flat_field[:, flat_index].astype(jnp.float32)
-    right_value = flat_field[:, flat_index + 1].astype(jnp.float32)
-    blend = lon_weight.astype(jnp.float32)
-    blended = (1.0 - blend) * left_value + blend * right_value
+    row_off = target - first_row + low_rows - (lat_index - first_row)
+    col_off = column - col_ext - (lon_index - col_core)
+    code = jnp.where(lon_index < length, row_off * 64 + col_off, -4096).astype(jnp.int32)
+    field_count = extended.shape[0]
+    blended = pl.pallas_call(
+        depart_kernel,
+        grid=(field_count,),
+        in_specs=[
+            pl.BlockSpec((1,) + extended.shape[1:], lambda f: (f, 0, 0, 0)),
+            pl.BlockSpec(code.shape, lambda f: (0, 0, 0)),
+            pl.BlockSpec(code.shape, lambda f: (0, 0, 0)),
+        ],
+        out_specs=pl.BlockSpec((1,) + code.shape, lambda f: (f, 0, 0, 0)),
+        out_shape=jax.ShapeDtypeStruct((field_count,) + code.shape, jnp.float32),
+    )(extended.astype(jnp.float32), code, lon_weight.astype(jnp.float32))
     return jnp.where(lon_index < length, blended, 0.0).astype(jnp.bfloat16)
 
 

time: 233 us -> 200 us (0.86)
  local copies, waits for them, and re-layouts: 78.3 us -> 33.2 us
  Pallas kernels: 0 us -> 11 us
    gather x4 -> x0, local copies, waits for them, and re-layouts: 41.2 us -> none  [the longest x2 20.6 us: depart_values(): left_value = flat_field[:, flat_index].astype(jnp.float32)]
    pallas_call x0 -> x1, Pallas kernels: none -> 11 us  [depart_values(): pl.pallas_call(depart_kernel, grid=(field_count,), in_specs=[pl.BlockSpec...]
    reshape x2 -> x0, local copies, waits for them, and re-layouts: 2.38 us -> none  [depart_values(): flat_field = extended.reshape(extended.shape[0], -1)]
  transfers between devices with their start and end apart: 7 -> 7, of which waited for: 4 -> 4; matrix products, arithmetic and copies ran while one was open for 9% -> 11% of each run, Pallas kernels for 0% -> 0%
where the time goes in v2:
time: 200 us
  starting transfers between devices  50.7 us (25%)
  waiting for transfers between devices  48.5 us (24%)
  local copies, waits for them, and re-layouts  33.2 us (17%)
  other arithmetic  29.3 us (15%)
  blocking collectives  17.4 us (9%)
  Pallas kernels  11 us (6%)
  matrix products  8.28 us (4%)
    all_to_all x1, waiting for transfers between devices, lat_sum(): pieces = lax.all_to_all(flat, 'lat', 0, 0, tiled=True)  26.1 us
    all_gather x1, blocking collectives, lat_sum(): whole = lax.all_gather(reduced, 'lat', axis=0, tiled=True)  17.4 us
    all_to_all x1, starting transfers between devices, on_device(): lax.all_to_all(advected, 'lon', split_axis=2, concat_axis=3, tiled=True)  14.7 us
    ppermute x2, starting transfers between devices, extended_2(): after = lax.ppermute(initial, axis, down)  12.9 us
    all_to_all x1, waiting for transfers between devices, on_device(): lax.all_to_all(advected, 'lon', split_axis=2, concat_axis=3, tiled=True)  12.4 us
    pallas_call x1, Pallas kernels, depart_values(): pl.pallas_call(depart_kernel, grid=(field_count,), in_specs=[pl.BlockSpec...  11 us
    all_to_all x1, starting transfers between devices, lat_sum(): pieces = lax.all_to_all(flat, 'lat', 0, 0, tiled=True)  10.1 us
    all_to_all x1, waiting for transfers between devices, on_device(): lax.all_to_all(shortened(spectra), 'lon', split_axis=1, concat_axis=0, ti...  8.96 us
  transfers between devices with their start and end apart: 7, of which 4 were waited for; matrix products, arithmetic and copies ran while one was open for 11% of the time, Pallas kernels for 0%

profile of v2, /device:TPU:1, one launch (start us, length us, event | category | flops | bytes accessed | tf_op | source)
XLA Modules:
  0.0 199.5 jit_solution(17392060707931570786)
XLA Ops:
  0.6 2.0 %fusion.61 = (bf16[8,2,64,10]{3,2,1,0:T(8,128)(2,1)}, bf16[8,2,64,10]{3,2,1,0:T(8,128)(2,1)S(1)}) fusion(bf16[8,2,64,65]{3,2,1,0:T(8,128)(2,1)} %param.7), kind=kLoop, calls=%fused_computation.121 | loop fusion | bytes 81920 | tf_op jit(solution)/shard_map/slice | solution.py:21
  2.6 5.7 %collective-permute-start = (bf16[8,2,64,10]{3,2,1,0:T(8,128)(2,1)}, bf16[8,2,64,10]{3,2,1,0:T(8,128)(2,1)S(1)}, u32[]{:S(2)}, u32[]{:S(2)}) collective-permute-start(bf16[8,2,64,10]{3,2,1,0:T(8,128)(2,1)} %get-tuple-element.29), channel_id=1, source_target_pairs={{0,1},{1,2},{2,3},{3,4},{4,5},{5,6},{6,7},{7,8},{8,9},{9,10},{10,1... | collective-permute-start | bytes 61448 | tf_op jit(solution)/shard_map/ppermute | solution.py:23
  8.4 1.3 collective-permute-start.1
  9.7 0.7 broadcast_subtract_fusion
  11.2 2.2 %fusion.35 = (f32[32,640,2]{1,0,2:T(8,128)S(1)}, f32[32,640,2]{1,0,2:T(8,128)S(1)}) fusion(f32[]{:T(128)S(6)} %convert_element_type.112, pred[]{:T(512)S(6)} %lt.114, s32[]{:T(128)S(6)} %select_n.164, s32[640,2]{0,1:T(2,128)S(1)} %pad_add_fusion), kind=kLoop, calls=%fused_computation.72 | loop fusion | flops 450560 | bytes 332809 | tf_op jit(solution)/shard_map/while/body/eval_jaxpr/cos | solution.py:88
  13.4 2.8 %fusion.28 = (f32[33,640,2]{1,0,2:T(8,128)S(1)}, f32[33,640,2]{1,0,2:T(8,128)S(1)}) fusion(f32[]{:T(128)S(6)} %convert_element_type.112, pred[]{:T(512)S(6)} %lt.114, s32[]{:T(128)S(6)} %select_n.164, s32[33]{0:T(128)S(1)} %iota_multiply_fusion, s32[640,2]{0,1:T(2,128)S(1)} %pad_add_fusion), kind=kLoop, calls=%fused_computation.63 | loop fusion | flops 464640 | bytes 343181 | tf_op jit(solution)/shard_map/while/body/eval_jaxpr/cos | solution.py:88
  16.2 0.8 broadcast_subtract_fusion.1
  17.1 0.8 fusion.33
  17.8 2.0 %multiply_subtract_fusion = (bf16[33,32,640,2]{2,1,0,3:T(8,128)(2,1)S(1)}, bf16[33,32,640,2]{2,1,0,3:T(8,128)(2,1)S(1)}) fusion(f32[32,640,2]{1,0,2:T(8,128)S(1)} %get-tuple-element.38, f32[33,640,2]{1,0,2:T(8,128)S(1)} %get-tuple-element.34, f32[32,640,2]{1,0,2:T(8,128)S(1)} %get-tuple-element.37, f32[33,640,2]{1,0,2:T(8,128)S(1)} %get-tuple-element.33), kind=kLoop, calls=%fused_computation.3 | loop fusion | flops 12165120 | bytes 6072320 | tf_op jit(solution)/shard_map/while/body/eval_jaxpr/sub | solution.py:105
  19.9 3.2 %fusion.6 = (bf16[1040,640,2,1]{1,0,3,2:T(8,128)(2,1)}, bf16[1040,640,2,1]{1,0,3,2:T(8,128)(2,1)}) fusion(bf16[1056,640,2]{1,0,2:T(8,128)(2,1)S(1)} %bitcast.59, pred[640,2]{0,1:T(4,128)(4,1)S(1)} %multiply_compare_fusion, pred[1040]{0:T(1024)(128)(4,1)S(1)} %iota_compare_fusion.2, bf16[1056,640,2]{1,0,2:T(8,128)(2,1)S(1)} %bitcast.60), kind=kLoop, calls=%fused_computation.11 | loop fusion | flops 3993600 | bytes 10651920 | tf_op jit(solution)/shard_map/while/body/eval_jaxpr/stack | solution.py:111
  23.3 11.6 %collective-permute-start.3 = (bf16[8,2,1,85]{3,2,1,0:T(2,128)(2,1)S(1)}, bf16[8,2,1,85]{3,2,1,0:T(2,128)(2,1)S(1)}, u32[]{:S(2)}, u32[]{:S(2)}) collective-permute-start(bf16[8,2,1,85]{3,2,1,0:T(2,128)(2,1)S(1)} %get-tuple-element.26), channel_id=1, source_target_pairs={{64,0},{128,64},{192,128},{256,192},{320,256},{384,320},{448,384},... | collective-permute-start | bytes 8168 | tf_op jit(solution)/shard_map/ppermute | solution.py:24
  34.9 1.5 fusion.40.code_ref
  37.0 1.9 collective-permute-start.2
  38.9 1.1 collective-permute-done.2
  40.0 1.2 maximum_convert_fusion.ext_ref
  41.2 11.0 %shard_map.86 = f32[8,2,64,65]{3,2,1,0:T(8,128)} custom-call(f32[8,2,66,85]{3,2,1,0:T(8,128)} %maximum_convert_fusion.ext_ref, s32[2,64,65]{2,1,0:T(8,128)} %fusion.40.code_ref, f32[2,64,65]{2,1,0:T(8,128)} %convert_element_type.115.weight_ref), custom_call_target="tpu_custom_call" | custom-call | tf_op jit(solution)/shard_map/pallas_call | solution.py:71
  52.2 1.1 select_convert_fusion
  53.3 1.0 copy.21
  54.3 14.7 %all-to-all-start = ((bf16[8,2,64,65]{3,1,0,2:T(2,128)(2,1)}), bf16[8,2,64,65]{3,1,0,2:T(2,128)(2,1)S(1)}, u32[]{:S(2)}, u32[]{:S(2)}) async-start(bf16[8,2,64,65]{3,1,0,2:T(2,128)(2,1)} %copy.21), calls=%async_computation | async-start | bytes 524288 | tf_op jit(solution)/shard_map/all_to_all | solution.py:203
  69.0 0.9 fusion.45
  70.6 12.4 %all-to-all-done = bf16[8,2,64,65]{3,1,0,2:T(2,128)(2,1)S(1)} async-done(((bf16[8,2,64,65]{3,1,0,2:T(2,128)(2,1)}), bf16[8,2,64,65]{3,1,0,2:T(2,128)(2,1)S(1)}, u32[]{:S(2)}, u32[]{:S(2)}) %all-to-all-start) | async-done | bytes 133152 | tf_op jit(solution)/shard_map/all_to_all | solution.py:203
  82.9 4.0 %copy.22 = bf16[8,2,64,65]{0,1,3,2:T(2,128)(2,1)} copy(bf16[8,2,64,65]{3,1,0,2:T(2,128)(2,1)S(1)} %all-to-all-done) | data formatting | bytes 266240 | tf_op jit(solution)/shard_map/all_to_all | solution.py:203
  87.0 4.4 %fusion.2 = f32[640,2,2,8,2,4]{0,3,5,4,2,1:T(8,128)S(1)} fusion(bf16[1040,640,2,1]{1,0,3,2:T(8,128)(2,1)} %get-tuple-element.40, bf16[1040,640,2,1]{1,0,3,2:T(8,128)(2,1)} %get-tuple-element.39, bf16[8,2,1040,4,1,1]{0,1,3,2,5,4:T(2,128)(2,1)} %bitcast.62), kind=kOutput, calls=%fused_computation.7 | convolution fusion | flops 351436800 | bytes 6113280 | tf_op jit(solution)/shard_map/while/body/eval_jaxpr/aser,fhab->serfhb/dot_general | solution.py:114
  92.4 1.7 reduce.6
  94.0 0.8 reshape.507
  94.8 5.4 %all-to-all-start.1 = ((bf16[64,2,320]{2,1,0:T(2,128)(2,1)}), bf16[64,2,320]{2,1,0:T(2,128)(2,1)}, u32[]{:S(2)}, u32[]{:S(2)}) async-start(bf16[64,2,320]{2,1,0:T(2,128)(2,1)} %reshape.507), calls=%async_computation.1 | async-start | bytes 196608 | tf_op jit(solution)/shard_map/all_to_all | solution.py:213
  101.0 1.5 stack.58
  102.5 9.0 %all-to-all-done.1 = bf16[64,2,320]{2,1,0:T(2,128)(2,1)} async-done(((bf16[64,2,320]{2,1,0:T(2,128)(2,1)}), bf16[64,2,320]{2,1,0:T(2,128)(2,1)}, u32[]{:S(2)}, u32[]{:S(2)}) %all-to-all-start.1) | async-done | bytes 81952 | tf_op jit(solution)/shard_map/all_to_all | solution.py:213
  111.5 1.4 reshape.508
  112.9 1.0 bitcast_reduce_fusion
  113.9 2.5 %fusion.21 = f32[10,64,1281]{2,1,0:T(8,128)} fusion(bf16[64,10,1281]{2,0,1:T(8,128)(2,1)S(1)} %copy-done, bf16[64,10,64]{2,1,0:T(8,128)(2,1)S(1)} %all_to_all.10), kind=kOutput, calls=%fused_computation.50 | convolution fusion | flops 104939520 | bytes 5000960 | tf_op jit(solution)/shard_map/ksc,ksq->sqc/dot_general | solution.py:147
  116.4 5.4 %reshape.492 = f32[10,2,2,8,2,1281]{5,4,3,2,1,0:T(2,128)} reshape(f32[10,64,1281]{2,1,0:T(8,128)} %fusion.21) | data formatting | bytes 6558720 | tf_op jit(solution)/shard_map/reshape | solution.py:149
  121.8 3.0 %fusion.8 = f32[10,2,8,2,1281]{4,3,2,1,0:T(2,128)S(1)} fusion(f32[10,2,2,8,2,1281]{5,4,3,2,1,0:T(2,128)} %reshape.492, pred[10,1281]{1,0:T(8,128)(4,1)S(1)} %iota_compare_fusion), kind=kLoop, calls=%fused_computation.14 | loop fusion | flops 409920 | bytes 4931850 | tf_op jit(solution)/shard_map/jit(_where)/select_n | solution.py:150
  124.8 5.7 %slice_reduce_fusion = (f32[10,2,8,1281]{3,2,1,0:T(8,128)S(1)}, f32[10,2,8,1281]{3,2,1,0:T(8,128)}) fusion(f32[10,2,8,2,1281]{4,3,2,1,0:T(2,128)S(1)} %fusion.8), kind=kLoop, calls=%fused_computation.18 | loop fusion | bytes 3279360 | tf_op jit(solution)/shard_map/slice | solution.py:151
  130.5 2.6 %squeeze.32 = f32[204960]{0:T(1024)} reshape(f32[10,2,8,1281]{3,2,1,0:T(8,128)} %get-tuple-element.13) | data formatting | bytes 1639680 | tf_op jit(solution)/shard_map/squeeze | solution.py:151
  133.1 1.4 squeeze.33
  134.6 1.5 multiply_add_fusion
  136.2 1.1 reshape.493
  137.3 10.1 %all-to-all-start.2 = ((f32[16,13,1024]{2,1,0:T(8,128)}), f32[16,13,1024]{2,1,0:T(8,128)S(1)}, u32[]{:S(2)}, u32[]{:S(2)}) async-start(f32[16,13,1024]{2,1,0:T(8,128)} %reshape.493), calls=%async_computation.2 | async-start | bytes 2097152 | tf_op jit(solution)/shard_map/all_to_all | solution.py:130
  147.6 0.7 multiply_convert_fusion
  148.4 0.9 multiply_add_fusion.1
  149.3 26.1 %all-to-all-done.2 = f32[16,13,1024]{2,1,0:T(8,128)S(1)} async-done(((f32[16,13,1024]{2,1,0:T(8,128)}), f32[16,13,1024]{2,1,0:T(8,128)S(1)}, u32[]{:S(2)}, u32[]{:S(2)}) %all-to-all-start.2) | async-done | bytes 852000 | tf_op jit(solution)/shard_map/all_to_all | solution.py:130
  175.4 17.4 %all-gather.1 = f32[16,13,1024]{2,1,0:T(8,128)S(1)} all-gather(f32[1,13,1024]{2,1,0:T(8,128)S(1)} %bitcast.66), channel_id=2, replica_groups=mesh['lat'=16,'lon'=64] {'lat'}, dimensions={0}, use_global_device_ids=true | all-gather | bytes 905216 | tf_op jit(solution)/shard_map/all_gather | solution.py:132
  192.9 1.1 reshape.494
  193.9 1.2 slice.67
  195.1 0.7 reshape.495
  195.8 2.1 %fusion.60 = (bf16[10,2,8,1281]{3,2,1,0:T(8,128)(2,1)S(1)}, f32[10,2,8,1281]{3,2,1,0:T(8,128)}) fusion(f32[10,2,8,1281]{3,2,1,0:T(8,128)S(1)} %reshape.495, f32[10,8,1281]{2,1,0:T(8,128)} %multiply_add_fusion.1), kind=kLoop, calls=%fused_computation.120 | loop fusion | flops 409920 | bytes 2459520 | tf_op jit(solution)/shard_map/convert_element_type | solution.py:162
  198.2 1.4 fusion.9
  (51 shorter events, 4.6 us)
Async XLA Ops:
  0.6 113.3 %copy-start = (bf16[64,10,1281]{2,0,1:T(8,128)(2,1)S(1)}, bf16[64,10,1281]{2,0,1:T(8,128)(2,1)}, u32[]{:S(2)}) copy-start(bf16[64,10,1281]{2,0,1:T(8,128)(2,1)} %param.12) | copy-start | bytes 4919044
  2.6 20.5 %collective-permute-start = (bf16[8,2,64,10]{3,2,1,0:T(8,128)(2,1)}, bf16[8,2,64,10]{3,2,1,0:T(8,128)(2,1)S(1)}, u32[]{:S(2)}, u32[]{:S(2)}) collective-permute-start(bf16[8,2,64,10]{3,2,1,0:T(8,128)(2,1)} %get-tuple-element.29), channel_id=1, source_target_pairs={{0,1},{1,2},{2,3},{3,4},{4,5},{5,6},{6,7},{7,8},{8,9},{9,10},{10,1... | collective-permute-start | bytes 61448 | tf_op jit(solution)/shard_map/ppermute | solution.py:23
  8.4 14.8 %collective-permute-start.1 = (bf16[8,2,64,10]{3,2,1,0:T(8,128)(2,1)S(1)}, bf16[8,2,64,10]{3,2,1,0:T(8,128)(2,1)S(1)}, u32[]{:S(2)}, u32[]{:S(2)}) collective-permute-start(bf16[8,2,64,10]{3,2,1,0:T(8,128)(2,1)S(1)} %get-tuple-element.30), channel_id=1, source_target_pairs={{1,0},{2,1},{3,2},{4,3},{5,4},{6,5},{7,6},{8,7},{9,8},{10,9},{11,1... | collective-permute-start | bytes 61448 | tf_op jit(solution)/shard_map/ppermute | solution.py:24
  19.8 3.3 %copy-start.1 = (bf16[8,2,64,65]{3,2,1,0:T(8,128)(2,1)S(1)}, bf16[8,2,64,65]{3,2,1,0:T(8,128)(2,1)}, u32[]{:S(2)}) copy-start(bf16[8,2,64,65]{3,2,1,0:T(8,128)(2,1)} %param.7) | copy-start | bytes 399364
  19.8 15.0 %copy-start.5 = (s32[2,64,65]{2,1,0:T(8,128)S(1)}, s32[2,64,65]{2,1,0:T(8,128)}, u32[]{:S(2)}) copy-start(s32[2,64,65]{2,1,0:T(8,128)} %param.9) | copy-start | bytes 99844
  19.9 15.0 %copy-start.6 = (s32[2,64,65]{2,1,0:T(8,128)S(1)}, s32[2,64,65]{2,1,0:T(8,128)}, u32[]{:S(2)}) copy-start(s32[2,64,65]{2,1,0:T(8,128)} %param.8) | copy-start | bytes 99844
  19.9 16.5 %copy-start.7 = (bf16[2,64,65]{2,1,0:T(8,128)(2,1)S(1)}, bf16[2,64,65]{2,1,0:T(8,128)(2,1)}, u32[]{:S(2)}) copy-start(bf16[2,64,65]{2,1,0:T(8,128)(2,1)} %param.10) | copy-start | bytes 49924
  23.3 15.6 %collective-permute-start.3 = (bf16[8,2,1,85]{3,2,1,0:T(2,128)(2,1)S(1)}, bf16[8,2,1,85]{3,2,1,0:T(2,128)(2,1)S(1)}, u32[]{:S(2)}, u32[]{:S(2)}) collective-permute-start(bf16[8,2,1,85]{3,2,1,0:T(2,128)(2,1)S(1)} %get-tuple-element.26), channel_id=1, source_target_pairs={{64,0},{128,64},{192,128},{256,192},{320,256},{384,320},{448,384},... | collective-permute-start | bytes 8168 | tf_op jit(solution)/shard_map/ppermute | solution.py:24
  37.0 3.1 %collective-permute-start.2 = (bf16[8,2,1,85]{3,2,1,0:T(2,128)(2,1)S(1)}, bf16[8,2,1,85]{3,2,1,0:T(2,128)(2,1)S(1)}, u32[]{:S(2)}, u32[]{:S(2)}) collective-permute-start(bf16[8,2,1,85]{3,2,1,0:T(2,128)(2,1)S(1)} %get-tuple-element.25), channel_id=1, source_target_pairs={{0,64},{64,128},{128,192},{192,256},{256,320},{320,384},{384,448},... | collective-permute-start | bytes 8168 | tf_op jit(solution)/shard_map/ppermute | solution.py:23
  54.3 28.6 %all-to-all-start = ((bf16[8,2,64,65]{3,1,0,2:T(2,128)(2,1)}), bf16[8,2,64,65]{3,1,0,2:T(2,128)(2,1)S(1)}, u32[]{:S(2)}, u32[]{:S(2)}) async-start(bf16[8,2,64,65]{3,1,0,2:T(2,128)(2,1)} %copy.21), calls=%async_computation | async-start | bytes 524288 | tf_op jit(solution)/shard_map/all_to_all | solution.py:203
  94.8 16.6 %all-to-all-start.1 = ((bf16[64,2,320]{2,1,0:T(2,128)(2,1)}), bf16[64,2,320]{2,1,0:T(2,128)(2,1)}, u32[]{:S(2)}, u32[]{:S(2)}) async-start(bf16[64,2,320]{2,1,0:T(2,128)(2,1)} %reshape.507), calls=%async_computation.1 | async-start | bytes 196608 | tf_op jit(solution)/shard_map/all_to_all | solution.py:213
  136.1 11.6 %copy-start.2 = (f32[10,2,1281]{2,1,0:T(2,128)S(1)}, f32[10,2,1281]{2,1,0:T(2,128)}, u32[]{:S(2)}) copy-start(f32[10,2,1281]{2,1,0:T(2,128)} %stack.58) | copy-start | bytes 307444
  136.2 12.2 %copy-start.4 = (f32[10,1281]{1,0:T(8,128)S(1)}, f32[10,1281]{1,0:T(8,128)}, u32[]{:S(2)}) copy-start(f32[10,1281]{1,0:T(8,128)} %get-tuple-element.31) | copy-start | bytes 153724
  136.2 12.2 %copy-start.8 = (f32[8]{0:T(128)S(1)}, f32[8]{0:T(128)}, u32[]{:S(2)}) copy-start(f32[8]{0:T(128)} %param.13) | copy-start | bytes 100
  137.3 38.1 %all-to-all-start.2 = ((f32[16,13,1024]{2,1,0:T(8,128)}), f32[16,13,1024]{2,1,0:T(8,128)S(1)}, u32[]{:S(2)}, u32[]{:S(2)}) async-start(f32[16,13,1024]{2,1,0:T(8,128)} %reshape.493), calls=%async_computation.2 | async-start | bytes 2097152 | tf_op jit(solution)/shard_map/all_to_all | solution.py:130
  195.8 2.1 %copy-start.3 = (bf16[10,2,2,1281]{3,2,1,0:T(2,128)(2,1)S(1)}, bf16[10,2,2,1281]{3,2,1,0:T(2,128)(2,1)}, u32[]{:S(2)}) copy-start(bf16[10,2,2,1281]{3,2,1,0:T(2,128)(2,1)} %multiply_convert_fusion) | copy-start | bytes 307444

commit v3 on v2

--- a/solution.py
+++ b/solution.py
@@ -127,8 +127,8 @@
     count = value.size
     pad = (-count) % (peers * 1024)
     flat = jnp.pad(value.reshape(-1), (0, pad)).reshape(peers, -1, 1024)
-    pieces = lax.all_to_all(flat, "lat", 0, 0, tiled=True)
-    reduced = jnp.sum(pieces, axis=0, keepdims=True)
+    pieces = lax.all_to_all(flat.astype(jnp.bfloat16), "lat", 0, 0, tiled=True)
+    reduced = jnp.sum(pieces.astype(jnp.float32), axis=0, keepdims=True)
     whole = lax.all_gather(reduced, "lat", axis=0, tiled=True)
     return whole.reshape(-1)[:count].reshape(value.shape)
 

time: 200 us -> 191 us (0.955)
  waiting for transfers between devices: 48.5 us -> 37 us
  other arithmetic: 29.3 us -> 31.3 us
    all_to_all x1, waiting for transfers between devices: 26.1 us -> 15.6 us  [lat_sum(): pieces = lax.all_to_all(flat.astype(jnp.bfloat16), 'lat', 0, 0, tiled=True)]
    all_to_all x1, waiting for transfers between devices: 12.4 us -> 10.2 us  [on_device(): lax.all_to_all(advected, 'lon', split_axis=2, concat_axis=3, tiled=True)]
  transfers between devices with their start and end apart: 7 -> 7, of which waited for: 4 -> 4; matrix products, arithmetic and copies ran while one was open for 11% -> 12% of each run, Pallas kernels for 0% -> 0%
where the time goes in v3:
time: 191 us; the launch traced here: 190 us
  starting transfers between devices  50.5 us (26%)
  waiting for transfers between devices  37 us (19%)
  local copies, waits for them, and re-layouts  33.4 us (17%)
  other arithmetic  31.3 us (16%)
  blocking collectives  17.4 us (9%)
  Pallas kernels  11 us (6%)
  matrix products  8.29 us (4%)
    all_gather x1, blocking collectives, lat_sum(): whole = lax.all_gather(reduced, 'lat', axis=0, tiled=True)  17.4 us
    all_to_all x1, waiting for transfers between devices, lat_sum(): pieces = lax.all_to_all(flat.astype(jnp.bfloat16), 'lat', 0, 0, tiled=True)  15.6 us
    all_to_all x1, starting transfers between devices, on_device(): lax.all_to_all(advected, 'lon', split_axis=2, concat_axis=3, tiled=True)  14.7 us
    ppermute x2, starting transfers between devices, extended_2(): after = lax.ppermute(initial, axis, down)  12.9 us
    pallas_call x1, Pallas kernels, depart_values(): pl.pallas_call(depart_kernel, grid=(field_count,), in_specs=[pl.BlockSpec...  11 us
    all_to_all x1, waiting for transfers between devices, on_device(): lax.all_to_all(shortened(spectra), 'lon', split_axis=1, concat_axis=0, ti...  10.3 us
    all_to_all x1, waiting for transfers between devices, on_device(): lax.all_to_all(advected, 'lon', split_axis=2, concat_axis=3, tiled=True)  10.2 us
    all_to_all x1, starting transfers between devices, lat_sum(): pieces = lax.all_to_all(flat.astype(jnp.bfloat16), 'lat', 0, 0, tiled=True)  9.68 us
  transfers between devices with their start and end apart: 7, of which 4 were waited for; matrix products, arithmetic and copies ran while one was open for 12% of the time, Pallas kernels for 0%

profile of v3, /device:TPU:1, one launch (start us, length us, event | category | flops | bytes accessed | tf_op | source)
XLA Modules:
  0.0 190.0 jit_solution(3290895470590131813)
XLA Ops:
  0.6 2.0 %fusion.61 = (bf16[8,2,64,10]{3,2,1,0:T(8,128)(2,1)}, bf16[8,2,64,10]{3,2,1,0:T(8,128)(2,1)S(1)}) fusion(bf16[8,2,64,65]{3,2,1,0:T(8,128)(2,1)} %param.7), kind=kLoop, calls=%fused_computation.122 | loop fusion | bytes 81920 | tf_op jit(solution)/shard_map/slice | solution.py:21
  2.6 5.7 %collective-permute-start = (bf16[8,2,64,10]{3,2,1,0:T(8,128)(2,1)}, bf16[8,2,64,10]{3,2,1,0:T(8,128)(2,1)S(1)}, u32[]{:S(2)}, u32[]{:S(2)}) collective-permute-start(bf16[8,2,64,10]{3,2,1,0:T(8,128)(2,1)} %get-tuple-element.29), channel_id=1, source_target_pairs={{0,1},{1,2},{2,3},{3,4},{4,5},{5,6},{6,7},{7,8},{8,9},{9,10},{10,1... | collective-permute-start | bytes 61448 | tf_op jit(solution)/shard_map/ppermute | solution.py:23
  8.4 1.3 collective-permute-start.1
  11.2 2.2 %fusion.35 = (f32[32,640,2]{1,0,2:T(8,128)S(1)}, f32[32,640,2]{1,0,2:T(8,128)S(1)}) fusion(f32[]{:T(128)S(6)} %convert_element_type.119, pred[]{:T(512)S(6)} %lt.114, s32[]{:T(128)S(6)} %select_n.164, s32[640,2]{0,1:T(2,128)S(1)} %pad_add_fusion), kind=kLoop, calls=%fused_computation.73 | loop fusion | flops 450560 | bytes 332809 | tf_op jit(solution)/shard_map/while/body/eval_jaxpr/cos | solution.py:88
  13.4 2.8 %fusion.28 = (f32[33,640,2]{1,0,2:T(8,128)S(1)}, f32[33,640,2]{1,0,2:T(8,128)S(1)}) fusion(f32[]{:T(128)S(6)} %convert_element_type.119, pred[]{:T(512)S(6)} %lt.114, s32[]{:T(128)S(6)} %select_n.164, s32[33]{0:T(128)S(1)} %iota_multiply_fusion, s32[640,2]{0,1:T(2,128)S(1)} %pad_add_fusion), kind=kLoop, calls=%fused_computation.64 | loop fusion | flops 464640 | bytes 343181 | tf_op jit(solution)/shard_map/while/body/eval_jaxpr/cos | solution.py:88
  16.2 0.8 broadcast_subtract_fusion.1
  17.0 0.8 fusion.48
  17.8 0.9 fusion.45
  18.7 0.8 fusion.33
  19.5 2.0 %multiply_subtract_fusion = (bf16[33,32,640,2]{2,1,0,3:T(8,128)(2,1)S(1)}, bf16[33,32,640,2]{2,1,0,3:T(8,128)(2,1)S(1)}) fusion(f32[32,640,2]{1,0,2:T(8,128)S(1)} %get-tuple-element.38, f32[33,640,2]{1,0,2:T(8,128)S(1)} %get-tuple-element.34, f32[32,640,2]{1,0,2:T(8,128)S(1)} %get-tuple-element.37, f32[33,640,2]{1,0,2:T(8,128)S(1)} %get-tuple-element.33), kind=kLoop, calls=%fused_computation.3 | loop fusion | flops 12165120 | bytes 6072320 | tf_op jit(solution)/shard_map/while/body/eval_jaxpr/sub | solution.py:105
  21.6 3.3 %fusion.6 = (bf16[1040,640,2,1]{1,0,3,2:T(8,128)(2,1)}, bf16[1040,640,2,1]{1,0,3,2:T(8,128)(2,1)}) fusion(bf16[1056,640,2]{1,0,2:T(8,128)(2,1)S(1)} %bitcast.59, pred[640,2]{0,1:T(4,128)(4,1)S(1)} %multiply_compare_fusion, pred[1040]{0:T(1024)(128)(4,1)S(1)} %iota_compare_fusion.2, bf16[1056,640,2]{1,0,2:T(8,128)(2,1)S(1)} %bitcast.60), kind=kLoop, calls=%fused_computation.11 | loop fusion | flops 3993600 | bytes 10651920 | tf_op jit(solution)/shard_map/while/body/eval_jaxpr/stack | solution.py:111
  25.0 11.6 %collective-permute-start.3 = (bf16[8,2,1,85]{3,2,1,0:T(2,128)(2,1)S(1)}, bf16[8,2,1,85]{3,2,1,0:T(2,128)(2,1)S(1)}, u32[]{:S(2)}, u32[]{:S(2)}) collective-permute-start(bf16[8,2,1,85]{3,2,1,0:T(2,128)(2,1)S(1)} %get-tuple-element.26), channel_id=1, source_target_pairs={{64,0},{128,64},{192,128},{256,192},{320,256},{384,320},{448,384},... | collective-permute-start | bytes 8168 | tf_op jit(solution)/shard_map/ppermute | solution.py:24
  36.6 1.5 fusion.40.code_ref
  38.7 2.1 %collective-permute-start.2 = (bf16[8,2,1,85]{3,2,1,0:T(2,128)(2,1)S(1)}, bf16[8,2,1,85]{3,2,1,0:T(2,128)(2,1)S(1)}, u32[]{:S(2)}, u32[]{:S(2)}) collective-permute-start(bf16[8,2,1,85]{3,2,1,0:T(2,128)(2,1)S(1)} %get-tuple-element.25), channel_id=1, source_target_pairs={{0,64},{64,128},{128,192},{192,256},{256,320},{320,384},{384,448},... | collective-permute-start | bytes 8168 | tf_op jit(solution)/shard_map/ppermute | solution.py:23
  40.9 0.9 collective-permute-done.2
  41.8 1.2 maximum_convert_fusion.ext_ref
  43.0 11.0 %shard_map.86 = f32[8,2,64,65]{3,2,1,0:T(8,128)} custom-call(f32[8,2,66,85]{3,2,1,0:T(8,128)} %maximum_convert_fusion.ext_ref, s32[2,64,65]{2,1,0:T(8,128)} %fusion.40.code_ref, f32[2,64,65]{2,1,0:T(8,128)} %convert_element_type.122.weight_ref), custom_call_target="tpu_custom_call" | custom-call | tf_op jit(solution)/shard_map/pallas_call | solution.py:71
  54.0 1.1 select_convert_fusion
  55.1 1.0 copy.21
  56.1 14.7 %all-to-all-start = ((bf16[8,2,64,65]{3,1,0,2:T(2,128)(2,1)}), bf16[8,2,64,65]{3,1,0,2:T(2,128)(2,1)}, u32[]{:S(2)}, u32[]{:S(2)}) async-start(bf16[8,2,64,65]{3,1,0,2:T(2,128)(2,1)} %copy.21), calls=%async_computation | async-start | bytes 524288 | tf_op jit(solution)/shard_map/all_to_all | solution.py:203
  71.6 1.5 stack.58
  73.1 1.3 fusion.57
  74.4 10.2 %all-to-all-done = bf16[8,2,64,65]{3,1,0,2:T(2,128)(2,1)} async-done(((bf16[8,2,64,65]{3,1,0,2:T(2,128)(2,1)}), bf16[8,2,64,65]{3,1,0,2:T(2,128)(2,1)}, u32[]{:S(2)}, u32[]{:S(2)}) %all-to-all-start) | async-done | bytes 133152 | tf_op jit(solution)/shard_map/all_to_all | solution.py:203
  84.6 5.5 %copy.22 = bf16[8,2,64,65]{0,1,3,2:T(2,128)(2,1)} copy(bf16[8,2,64,65]{3,1,0,2:T(2,128)(2,1)} %all-to-all-done) | data formatting | bytes 266240 | tf_op jit(solution)/shard_map/all_to_all | solution.py:203
  90.1 4.5 %fusion.2 = f32[640,2,2,8,2,4]{0,3,5,4,2,1:T(8,128)S(1)} fusion(bf16[1040,640,2,1]{1,0,3,2:T(8,128)(2,1)} %get-tuple-element.40, bf16[1040,640,2,1]{1,0,3,2:T(8,128)(2,1)} %get-tuple-element.39, bf16[8,2,1040,4,1,1]{0,1,3,2,5,4:T(2,128)(2,1)} %bitcast.62), kind=kOutput, calls=%fused_computation.7 | convolution fusion | flops 351436800 | bytes 6113280 | tf_op jit(solution)/shard_map/while/body/eval_jaxpr/aser,fhab->serfhb/dot_general | solution.py:114
  95.5 1.7 reduce.6
  97.2 0.8 reshape.505
  98.0 5.3 %all-to-all-start.1 = ((bf16[64,2,320]{2,1,0:T(2,128)(2,1)}), bf16[64,2,320]{2,1,0:T(2,128)(2,1)S(1)}, u32[]{:S(2)}, u32[]{:S(2)}) async-start(bf16[64,2,320]{2,1,0:T(2,128)(2,1)} %reshape.505), calls=%async_computation.1 | async-start | bytes 196608 | tf_op jit(solution)/shard_map/all_to_all | solution.py:213
  103.3 0.7 pad_maximum_fusion
  104.1 10.3 %all-to-all-done.1 = bf16[64,2,320]{2,1,0:T(2,128)(2,1)S(1)} async-done(((bf16[64,2,320]{2,1,0:T(2,128)(2,1)}), bf16[64,2,320]{2,1,0:T(2,128)(2,1)S(1)}, u32[]{:S(2)}, u32[]{:S(2)}) %all-to-all-start.1) | async-done | bytes 81952 | tf_op jit(solution)/shard_map/all_to_all | solution.py:213
  114.5 1.0 bitcast_reduce_fusion
  115.6 2.5 %fusion.21 = f32[10,64,1281]{2,1,0:T(8,128)} fusion(bf16[64,10,1281]{2,0,1:T(8,128)(2,1)S(1)} %copy-done, bf16[64,10,64]{2,1,0:T(8,128)(2,1)S(1)} %all_to_all.10), kind=kOutput, calls=%fused_computation.51 | convolution fusion | flops 104939520 | bytes 5000960 | tf_op jit(solution)/shard_map/ksc,ksq->sqc/dot_general | solution.py:147
  118.0 5.4 %reshape.491 = f32[10,2,2,8,2,1281]{5,4,3,2,1,0:T(2,128)} reshape(f32[10,64,1281]{2,1,0:T(8,128)} %fusion.21) | data formatting | bytes 6558720 | tf_op jit(solution)/shard_map/reshape | solution.py:149
  123.5 3.0 %fusion.8 = f32[10,2,8,2,1281]{4,3,2,1,0:T(2,128)S(1)} fusion(f32[10,2,2,8,2,1281]{5,4,3,2,1,0:T(2,128)} %reshape.491, pred[10,1281]{1,0:T(8,128)(4,1)S(1)} %iota_compare_fusion), kind=kLoop, calls=%fused_computation.14 | loop fusion | flops 409920 | bytes 4931850 | tf_op jit(solution)/shard_map/jit(_where)/select_n | solution.py:150
  126.5 5.7 %slice_reduce_fusion = (f32[10,2,8,1281]{3,2,1,0:T(8,128)S(1)}, f32[10,2,8,1281]{3,2,1,0:T(8,128)}) fusion(f32[10,2,8,2,1281]{4,3,2,1,0:T(2,128)S(1)} %fusion.8), kind=kLoop, calls=%fused_computation.19 | loop fusion | bytes 3279360 | tf_op jit(solution)/shard_map/slice | solution.py:151
  132.1 2.6 %squeeze.32 = f32[204960]{0:T(1024)} reshape(f32[10,2,8,1281]{3,2,1,0:T(8,128)} %get-tuple-element.13) | data formatting | bytes 1639680 | tf_op jit(solution)/shard_map/squeeze | solution.py:151
  134.8 1.4 squeeze.33
  136.2 1.5 add_convert_fusion
  137.8 1.1 convert_element_type.129
  138.9 9.7 %all-to-all-start.2 = ((bf16[16,13,1024]{2,1,0:T(8,128)(2,1)}), bf16[16,13,1024]{2,1,0:T(8,128)(2,1)S(1)}, u32[]{:S(2)}, u32[]{:S(2)}) async-start(bf16[16,13,1024]{2,1,0:T(8,128)(2,1)} %convert_element_type.129), calls=%async_computation.2 | async-start | bytes 1048576 | tf_op jit(solution)/shard_map/all_to_all | solution.py:130
  148.6 0.7 multiply_convert_fusion
  149.3 0.9 multiply_add_fusion
  150.2 15.6 %all-to-all-done.2 = bf16[16,13,1024]{2,1,0:T(8,128)(2,1)S(1)} async-done(((bf16[16,13,1024]{2,1,0:T(8,128)(2,1)}), bf16[16,13,1024]{2,1,0:T(8,128)(2,1)S(1)}, u32[]{:S(2)}, u32[]{:S(2)}) %all-to-all-start.2) | async-done | bytes 426016 | tf_op jit(solution)/shard_map/all_to_all | solution.py:130
  165.9 17.4 %all-gather.1 = f32[16,13,1024]{2,1,0:T(8,128)S(1)} all-gather(f32[1,13,1024]{2,1,0:T(8,128)S(1)} %bitcast.66), channel_id=2, replica_groups=mesh['lat'=16,'lon'=64] {'lat'}, dimensions={0}, use_global_device_ids=true | all-gather | bytes 905216 | tf_op jit(solution)/shard_map/all_gather | solution.py:132
  183.3 1.1 reshape.492
  184.3 1.2 slice.67
  186.3 2.1 %fusion.60 = (bf16[10,2,8,1281]{3,2,1,0:T(8,128)(2,1)S(1)}, f32[10,2,8,1281]{3,2,1,0:T(8,128)}) fusion(f32[10,2,8,1281]{3,2,1,0:T(8,128)S(1)} %reshape.493, f32[10,8,1281]{2,1,0:T(8,128)} %multiply_add_fusion), kind=kLoop, calls=%fused_computation.121 | loop fusion | flops 409920 | bytes 2459520 | tf_op jit(solution)/shard_map/convert_element_type | solution.py:162
  188.6 1.4 fusion.9
  (59 shorter events, 5.3 us)
Async XLA Ops:
  0.6 114.9 %copy-start = (bf16[64,10,1281]{2,0,1:T(8,128)(2,1)S(1)}, bf16[64,10,1281]{2,0,1:T(8,128)(2,1)}, u32[]{:S(2)}) copy-start(bf16[64,10,1281]{2,0,1:T(8,128)(2,1)} %param.12) | copy-start | bytes 4919044
  2.6 22.2 %collective-permute-start = (bf16[8,2,64,10]{3,2,1,0:T(8,128)(2,1)}, bf16[8,2,64,10]{3,2,1,0:T(8,128)(2,1)S(1)}, u32[]{:S(2)}, u32[]{:S(2)}) collective-permute-start(bf16[8,2,64,10]{3,2,1,0:T(8,128)(2,1)} %get-tuple-element.29), channel_id=1, source_target_pairs={{0,1},{1,2},{2,3},{3,4},{4,5},{5,6},{6,7},{7,8},{8,9},{9,10},{10,1... | collective-permute-start | bytes 61448 | tf_op jit(solution)/shard_map/ppermute | solution.py:23
  8.4 16.5 %collective-permute-start.1 = (bf16[8,2,64,10]{3,2,1,0:T(8,128)(2,1)S(1)}, bf16[8,2,64,10]{3,2,1,0:T(8,128)(2,1)S(1)}, u32[]{:S(2)}, u32[]{:S(2)}) collective-permute-start(bf16[8,2,64,10]{3,2,1,0:T(8,128)(2,1)S(1)} %get-tuple-element.30), channel_id=1, source_target_pairs={{1,0},{2,1},{3,2},{4,3},{5,4},{6,5},{7,6},{8,7},{9,8},{10,9},{11,1... | collective-permute-start | bytes 61448 | tf_op jit(solution)/shard_map/ppermute | solution.py:24
  11.1 10.4 %copy-start.8 = (s32[640,2]{0,1:T(2,128)}, s32[640,2]{0,1:T(2,128)S(1)}, u32[]{:S(2)}) copy-start(s32[640,2]{0,1:T(2,128)S(1)} %pad_add_fusion) | copy-start | bytes 15364
  21.6 3.3 %copy-start.1 = (bf16[8,2,64,65]{3,2,1,0:T(8,128)(2,1)S(1)}, bf16[8,2,64,65]{3,2,1,0:T(8,128)(2,1)}, u32[]{:S(2)}) copy-start(bf16[8,2,64,65]{3,2,1,0:T(8,128)(2,1)} %param.7) | copy-start | bytes 399364
  21.6 15.0 %copy-start.9 = (s32[2,64,65]{2,1,0:T(8,128)S(1)}, s32[2,64,65]{2,1,0:T(8,128)}, u32[]{:S(2)}) copy-start(s32[2,64,65]{2,1,0:T(8,128)} %param.9) | copy-start | bytes 99844
  21.6 15.0 %copy-start.10 = (s32[2,64,65]{2,1,0:T(8,128)S(1)}, s32[2,64,65]{2,1,0:T(8,128)}, u32[]{:S(2)}) copy-start(s32[2,64,65]{2,1,0:T(8,128)} %param.8) | copy-start | bytes 99844
  21.6 16.5 %copy-start.11 = (bf16[2,64,65]{2,1,0:T(8,128)(2,1)S(1)}, bf16[2,64,65]{2,1,0:T(8,128)(2,1)}, u32[]{:S(2)}) copy-start(bf16[2,64,65]{2,1,0:T(8,128)(2,1)} %param.10) | copy-start | bytes 49924
  25.0 15.8 %collective-permute-start.3 = (bf16[8,2,1,85]{3,2,1,0:T(2,128)(2,1)S(1)}, bf16[8,2,1,85]{3,2,1,0:T(2,128)(2,1)S(1)}, u32[]{:S(2)}, u32[]{:S(2)}) collective-permute-start(bf16[8,2,1,85]{3,2,1,0:T(2,128)(2,1)S(1)} %get-tuple-element.26), channel_id=1, source_target_pairs={{64,0},{128,64},{192,128},{256,192},{320,256},{384,320},{448,384},... | collective-permute-start | bytes 8168 | tf_op jit(solution)/shard_map/ppermute | solution.py:24
  38.7 3.1 %collective-permute-start.2 = (bf16[8,2,1,85]{3,2,1,0:T(2,128)(2,1)S(1)}, bf16[8,2,1,85]{3,2,1,0:T(2,128)(2,1)S(1)}, u32[]{:S(2)}, u32[]{:S(2)}) collective-permute-start(bf16[8,2,1,85]{3,2,1,0:T(2,128)(2,1)S(1)} %get-tuple-element.25), channel_id=1, source_target_pairs={{0,64},{64,128},{128,192},{192,256},{256,320},{320,384},{384,448},... | collective-permute-start | bytes 8168 | tf_op jit(solution)/shard_map/ppermute | solution.py:23
  56.1 28.6 %all-to-all-start = ((bf16[8,2,64,65]{3,1,0,2:T(2,128)(2,1)}), bf16[8,2,64,65]{3,1,0,2:T(2,128)(2,1)}, u32[]{:S(2)}, u32[]{:S(2)}) async-start(bf16[8,2,64,65]{3,1,0,2:T(2,128)(2,1)} %copy.21), calls=%async_computation | async-start | bytes 524288 | tf_op jit(solution)/shard_map/all_to_all | solution.py:203
  94.5 8.8 %copy-start.6 = (f32[10,1,1281]{2,1,0:T(1,128)S(1)}, f32[10,1,1281]{2,1,0:T(1,128)}, u32[]{:S(2)}) copy-start(f32[10,1,1281]{2,1,0:T(1,128)} %get-tuple-element.41) | copy-start | bytes 153724
  94.5 8.8 %copy-start.7 = (f32[10,1,1281]{2,1,0:T(1,128)S(1)}, f32[10,1,1281]{2,1,0:T(1,128)}, u32[]{:S(2)}) copy-start(f32[10,1,1281]{2,1,0:T(1,128)} %get-tuple-element.42) | copy-start | bytes 153724
  98.0 16.4 %all-to-all-start.1 = ((bf16[64,2,320]{2,1,0:T(2,128)(2,1)}), bf16[64,2,320]{2,1,0:T(2,128)(2,1)S(1)}, u32[]{:S(2)}, u32[]{:S(2)}) async-start(bf16[64,2,320]{2,1,0:T(2,128)(2,1)} %reshape.505), calls=%async_computation.1 | async-start | bytes 196608 | tf_op jit(solution)/shard_map/all_to_all | solution.py:213
  136.2 13.1 %copy-start.12 = (f32[8]{0:T(128)S(1)}, f32[8]{0:T(128)}, u32[]{:S(2)}) copy-start(f32[8]{0:T(128)} %param.13) | copy-start | bytes 100
  137.7 10.9 %copy-start.2 = (f32[10,2,1281]{2,1,0:T(2,128)S(1)}, f32[10,2,1281]{2,1,0:T(2,128)}, u32[]{:S(2)}) copy-start(f32[10,2,1281]{2,1,0:T(2,128)} %pad_maximum_fusion) | copy-start | bytes 307444
  137.7 10.9 %copy-start.3 = (f32[10,2,1281]{2,1,0:T(2,128)S(1)}, f32[10,2,1281]{2,1,0:T(2,128)}, u32[]{:S(2)}) copy-start(f32[10,2,1281]{2,1,0:T(2,128)} %stack.58) | copy-start | bytes 307444
  137.7 11.6 %copy-start.5 = (f32[10,1281]{1,0:T(8,128)S(1)}, f32[10,1281]{1,0:T(8,128)}, u32[]{:S(2)}) copy-start(f32[10,1281]{1,0:T(8,128)} %get-tuple-element.31) | copy-start | bytes 153724
  138.9 26.9 %all-to-all-start.2 = ((bf16[16,13,1024]{2,1,0:T(8,128)(2,1)}), bf16[16,13,1024]{2,1,0:T(8,128)(2,1)S(1)}, u32[]{:S(2)}, u32[]{:S(2)}) async-start(bf16[16,13,1024]{2,1,0:T(8,128)(2,1)} %convert_element_type.129), calls=%async_computation.2 | async-start | bytes 1048576 | tf_op jit(solution)/shard_map/all_to_all | solution.py:130
  186.2 2.1 %copy-start.4 = (bf16[10,2,2,1281]{3,2,1,0:T(2,128)(2,1)S(1)}, bf16[10,2,2,1281]{3,2,1,0:T(2,128)(2,1)}, u32[]{:S(2)}) copy-start(bf16[10,2,2,1281]{3,2,1,0:T(2,128)(2,1)} %multiply_convert_fusion) | copy-start | bytes 307444

commit v4 on v3

--- a/solution.py
+++ b/solution.py
@@ -118,7 +118,7 @@
     twist_sin = jnp.sin(twist)[:, :, None, None, :]
     real_part = jnp.sum(inner[:, :, 0] * twist_cos + inner[:, :, 1] * twist_sin, axis=-1)
     imag_part = jnp.sum(inner[:, :, 1] * twist_cos - inner[:, :, 0] * twist_sin, axis=-1)
-    spectrum = jnp.stack([real_part, imag_part], axis=2)
+    spectrum = jnp.stack([real_part, imag_part], axis=2).transpose(0, 1, 4, 2, 3)
     return (spectrum * norm_scale).astype(jnp.bfloat16).reshape(PAIRS, -1)
 
 
@@ -146,9 +146,9 @@
 def analyse(legend, spectra, pair_ids):
     products = jnp.einsum("ksc,ksq->sqc", legend, spectra, preferred_element_type=jnp.float32)
     second_half, degree, parity = column_terms(pair_ids)
-    products = products.reshape(products.shape[0], 2, 2, -1, 2, NPAIR)
+    products = products.reshape(products.shape[0], 2, 2, 2, -1, NPAIR)
     chosen = jnp.where(second_half[:, None, None, None, :], products[:, 1], products[:, 0])
-    return chosen[:, :, :, 0] + parity[:, None, None, :] * chosen[:, :, :, 1]
+    return chosen[:, 0] + parity[:, None, None, :] * chosen[:, 1]
 
 
 def helmholtz_solve(spectral_total, pair_ids, helm_coeff):

time: 191 us -> 177 us (0.927)
  local copies, waits for them, and re-layouts: 33.4 us -> 24.1 us
  other arithmetic: 31.3 us -> 28.7 us
    reshape x1 -> x0, local copies, waits for them, and re-layouts: 5.4 us -> none  [analyse(): products = products.reshape(products.shape[0], 2, 2, -1, 2, NPAIR)]
    slice x1, local copies, waits for them, and re-layouts: 5.67 us -> 1.03 us  [analyse(): return chosen[:, 0] + parity[:, None, None, :] * chosen[:, 1]]
    select_n x1, other arithmetic: 3 us -> 0.22 us  [analyse(): jnp.where(second_half[:, None, None, None, :], products[:, 1], products[:...]
  transfers between devices with their start and end apart: 7 -> 7, of which waited for: 4 -> 4; matrix products, arithmetic and copies ran while one was open for 12% -> 14% of each run, Pallas kernels for 0% -> 0%
where the time goes in v4:
time: 177 us; the launch traced here: 175 us
  starting transfers between devices  50.2 us (28%)
  waiting for transfers between devices  36.3 us (21%)
  other arithmetic  28.7 us (16%)
  local copies, waits for them, and re-layouts  24.1 us (14%)
  blocking collectives  17.4 us (10%)
  Pallas kernels  11 us (6%)
  matrix products  6.5 us (4%)
    all_gather x1, blocking collectives, lat_sum(): whole = lax.all_gather(reduced, 'lat', axis=0, tiled=True)  17.4 us
    all_to_all x1, waiting for transfers between devices, lat_sum(): pieces = lax.all_to_all(flat.astype(jnp.bfloat16), 'lat', 0, 0, tiled=True)  15.6 us
    all_to_all x1, starting transfers between devices, on_device(): lax.all_to_all(advected, 'lon', split_axis=2, concat_axis=3, tiled=True)  14.7 us
    ppermute x2, starting transfers between devices, extended_2(): after = lax.ppermute(initial, axis, down)  12.9 us
    pallas_call x1, Pallas kernels, depart_values(): pl.pallas_call(depart_kernel, grid=(field_count,), in_specs=[pl.BlockSpec...  11 us
    all_to_all x1, waiting for transfers between devices, on_device(): lax.all_to_all(shortened(spectra), 'lon', split_axis=1, concat_axis=0, ti...  10.5 us
    all_to_all x1, starting transfers between devices, lat_sum(): pieces = lax.all_to_all(flat.astype(jnp.bfloat16), 'lat', 0, 0, tiled=True)  9.68 us
    all_to_all x1, waiting for transfers between devices, on_device(): lax.all_to_all(advected, 'lon', split_axis=2, concat_axis=3, tiled=True)  9.35 us
  transfers between devices with their start and end apart: 7, of which 4 were waited for; matrix products, arithmetic and copies ran while one was open for 14% of the time, Pallas kernels for 0%

profile of v4, /device:TPU:1, one launch (start us, length us, event | category | flops | bytes accessed | tf_op | source)
XLA Modules:
  0.0 175.4 jit_solution(12384120605562128274)
XLA Ops:
  0.6 2.0 %fusion.62 = (bf16[8,2,64,10]{3,2,1,0:T(8,128)(2,1)}, bf16[8,2,64,10]{3,2,1,0:T(8,128)(2,1)S(1)}) fusion(bf16[8,2,64,65]{3,2,1,0:T(8,128)(2,1)} %param.7), kind=kLoop, calls=%fused_computation.121 | loop fusion | bytes 81920 | tf_op jit(solution)/shard_map/slice | solution.py:21
  2.7 5.7 %collective-permute-start = (bf16[8,2,64,10]{3,2,1,0:T(8,128)(2,1)}, bf16[8,2,64,10]{3,2,1,0:T(8,128)(2,1)S(1)}, u32[]{:S(2)}, u32[]{:S(2)}) collective-permute-start(bf16[8,2,64,10]{3,2,1,0:T(8,128)(2,1)} %get-tuple-element.29), channel_id=1, source_target_pairs={{0,1},{1,2},{2,3},{3,4},{4,5},{5,6},{6,7},{7,8},{8,9},{9,10},{10,1... | collective-permute-start | bytes 61448 | tf_op jit(solution)/shard_map/ppermute | solution.py:23
  8.4 1.3 collective-permute-start.1
  9.7 0.7 broadcast_subtract_fusion
  11.2 2.2 %fusion.35 = (f32[32,640,2]{1,0,2:T(8,128)S(1)}, f32[32,640,2]{1,0,2:T(8,128)S(1)}) fusion(f32[]{:T(128)S(6)} %convert_element_type.112, pred[]{:T(512)S(6)} %lt.114, s32[]{:T(128)S(6)} %select_n.164, s32[640,2]{0,1:T(2,128)S(1)} %pad_add_fusion), kind=kLoop, calls=%fused_computation.71 | loop fusion | flops 450560 | bytes 332809 | tf_op jit(solution)/shard_map/while/body/eval_jaxpr/cos | solution.py:88
  13.4 2.8 %fusion.28 = (f32[33,640,2]{1,0,2:T(8,128)S(1)}, f32[33,640,2]{1,0,2:T(8,128)S(1)}) fusion(f32[]{:T(128)S(6)} %convert_element_type.112, pred[]{:T(512)S(6)} %lt.114, s32[]{:T(128)S(6)} %select_n.164, s32[33]{0:T(128)S(1)} %iota_multiply_fusion, s32[640,2]{0,1:T(2,128)S(1)} %pad_add_fusion), kind=kLoop, calls=%fused_computation.62 | loop fusion | flops 464640 | bytes 343181 | tf_op jit(solution)/shard_map/while/body/eval_jaxpr/cos | solution.py:88
  16.2 0.8 broadcast_subtract_fusion.1
  17.0 0.8 fusion.48
  17.8 0.9 fusion.45
  18.7 0.8 fusion.33
  19.6 2.0 %multiply_subtract_fusion = (bf16[33,32,640,2]{2,1,0,3:T(8,128)(2,1)S(1)}, bf16[33,32,640,2]{2,1,0,3:T(8,128)(2,1)S(1)}) fusion(f32[32,640,2]{1,0,2:T(8,128)S(1)} %get-tuple-element.38, f32[33,640,2]{1,0,2:T(8,128)S(1)} %get-tuple-element.34, f32[32,640,2]{1,0,2:T(8,128)S(1)} %get-tuple-element.37, f32[33,640,2]{1,0,2:T(8,128)S(1)} %get-tuple-element.33), kind=kLoop, calls=%fused_computation.3 | loop fusion | flops 12165120 | bytes 6072320 | tf_op jit(solution)/shard_map/while/body/eval_jaxpr/sub | solution.py:105
  21.7 3.3 %fusion.6 = (bf16[1040,640,2,1]{1,0,3,2:T(8,128)(2,1)}, bf16[1040,640,2,1]{1,0,3,2:T(8,128)(2,1)}) fusion(bf16[1056,640,2]{1,0,2:T(8,128)(2,1)S(1)} %bitcast.62, pred[640,2]{0,1:T(4,128)(4,1)S(1)} %multiply_compare_fusion, pred[1040]{0:T(1024)(128)(4,1)S(1)} %iota_compare_fusion.2, bf16[1056,640,2]{1,0,2:T(8,128)(2,1)S(1)} %bitcast.63), kind=kLoop, calls=%fused_computation.11 | loop fusion | flops 3993600 | bytes 10651920 | tf_op jit(solution)/shard_map/while/body/eval_jaxpr/stack | solution.py:111
  25.1 11.6 %collective-permute-start.3 = (bf16[8,2,1,85]{3,2,1,0:T(2,128)(2,1)S(1)}, bf16[8,2,1,85]{3,2,1,0:T(2,128)(2,1)S(1)}, u32[]{:S(2)}, u32[]{:S(2)}) collective-permute-start(bf16[8,2,1,85]{3,2,1,0:T(2,128)(2,1)S(1)} %get-tuple-element.26), channel_id=1, source_target_pairs={{64,0},{128,64},{192,128},{256,192},{320,256},{384,320},{448,384},... | collective-permute-start | bytes 8168 | tf_op jit(solution)/shard_map/ppermute | solution.py:24
  36.7 1.4 fusion.40.code_ref
  38.8 2.1 %collective-permute-start.2 = (bf16[8,2,1,85]{3,2,1,0:T(2,128)(2,1)S(1)}, bf16[8,2,1,85]{3,2,1,0:T(2,128)(2,1)S(1)}, u32[]{:S(2)}, u32[]{:S(2)}) collective-permute-start(bf16[8,2,1,85]{3,2,1,0:T(2,128)(2,1)S(1)} %get-tuple-element.25), channel_id=1, source_target_pairs={{0,64},{64,128},{128,192},{192,256},{256,320},{320,384},{384,448},... | collective-permute-start | bytes 8168 | tf_op jit(solution)/shard_map/ppermute | solution.py:23
  40.9 0.9 collective-permute-done.2
  41.9 1.2 maximum_convert_fusion.ext_ref
  43.0 11.0 %shard_map.86 = f32[8,2,64,65]{3,2,1,0:T(8,128)} custom-call(f32[8,2,66,85]{3,2,1,0:T(8,128)} %maximum_convert_fusion.ext_ref, s32[2,64,65]{2,1,0:T(8,128)} %fusion.40.code_ref, f32[2,64,65]{2,1,0:T(8,128)} %convert_element_type.115.weight_ref), custom_call_target="tpu_custom_call" | custom-call | tf_op jit(solution)/shard_map/pallas_call | solution.py:71
  54.1 1.1 select_convert_fusion
  55.2 1.0 copy.21
  56.1 14.7 %all-to-all-start = ((bf16[8,2,64,65]{3,1,0,2:T(2,128)(2,1)}), bf16[8,2,64,65]{3,1,0,2:T(2,128)(2,1)}, u32[]{:S(2)}, u32[]{:S(2)}) async-start(bf16[8,2,64,65]{3,1,0,2:T(2,128)(2,1)} %copy.21), calls=%async_computation | async-start | bytes 524288 | tf_op jit(solution)/shard_map/all_to_all | solution.py:203
  71.0 1.0 mul.432
  72.5 1.5 stack.58
  74.1 1.3 fusion.57
  75.3 9.3 %all-to-all-done = bf16[8,2,64,65]{3,1,0,2:T(2,128)(2,1)} async-done(((bf16[8,2,64,65]{3,1,0,2:T(2,128)(2,1)}), bf16[8,2,64,65]{3,1,0,2:T(2,128)(2,1)}, u32[]{:S(2)}, u32[]{:S(2)}) %all-to-all-start) | async-done | bytes 133152 | tf_op jit(solution)/shard_map/all_to_all | solution.py:203
  84.7 5.4 %copy.22 = bf16[8,2,64,65]{0,1,3,2:T(2,128)(2,1)} copy(bf16[8,2,64,65]{3,1,0,2:T(2,128)(2,1)} %all-to-all-done) | data formatting | bytes 266240 | tf_op jit(solution)/shard_map/all_to_all | solution.py:203
  90.1 4.5 %fusion.2 = f32[640,2,2,8,2,4]{0,3,5,4,2,1:T(8,128)S(1)} fusion(bf16[1040,640,2,1]{1,0,3,2:T(8,128)(2,1)} %get-tuple-element.40, bf16[1040,640,2,1]{1,0,3,2:T(8,128)(2,1)} %get-tuple-element.39, bf16[8,2,1040,4,1,1]{0,1,3,2,5,4:T(2,128)(2,1)} %bitcast.65), kind=kOutput, calls=%fused_computation.7 | convolution fusion | flops 351436800 | bytes 6113280 | tf_op jit(solution)/shard_map/while/body/eval_jaxpr/aser,fhab->serfhb/dot_general | solution.py:114
  95.5 1.7 reduce.2
  97.2 0.8 reshape.487
  98.0 5.1 %all-to-all-start.1 = ((bf16[64,2,320]{2,1,0:T(2,128)(2,1)}), bf16[64,2,320]{2,1,0:T(2,128)(2,1)S(1)}, u32[]{:S(2)}, u32[]{:S(2)}) async-start(bf16[64,2,320]{2,1,0:T(2,128)(2,1)} %reshape.487), calls=%async_computation.1 | async-start | bytes 196608 | tf_op jit(solution)/shard_map/all_to_all | solution.py:213
  103.1 0.8 pad_maximum_fusion
  103.9 10.5 %all-to-all-done.1 = bf16[64,2,320]{2,1,0:T(2,128)(2,1)S(1)} async-done(((bf16[64,2,320]{2,1,0:T(2,128)(2,1)}), bf16[64,2,320]{2,1,0:T(2,128)(2,1)S(1)}, u32[]{:S(2)}, u32[]{:S(2)}) %all-to-all-start.1) | async-done | bytes 81952 | tf_op jit(solution)/shard_map/all_to_all | solution.py:213
  114.5 1.0 bitcast_reduce_fusion
  116.5 1.0 fusion.61
  117.5 2.6 %squeeze.32 = f32[204960]{0:T(1024)} reshape(f32[10,1,2,8,1281]{4,3,2,1,0:T(8,128)} %get-tuple-element.24) | data formatting | bytes 1639680 | tf_op jit(solution)/shard_map/squeeze | solution.py:151
  120.2 1.4 squeeze.33
  121.6 1.6 add_convert_fusion
  123.2 1.1 convert_element_type.122
  124.3 9.7 %all-to-all-start.2 = ((bf16[16,13,1024]{2,1,0:T(8,128)(2,1)}), bf16[16,13,1024]{2,1,0:T(8,128)(2,1)S(1)}, u32[]{:S(2)}, u32[]{:S(2)}) async-start(bf16[16,13,1024]{2,1,0:T(8,128)(2,1)} %convert_element_type.122), calls=%async_computation.2 | async-start | bytes 1048576 | tf_op jit(solution)/shard_map/all_to_all | solution.py:130
  134.0 0.7 multiply_convert_fusion
  134.8 0.9 multiply_add_fusion
  135.6 15.6 %all-to-all-done.2 = bf16[16,13,1024]{2,1,0:T(8,128)(2,1)S(1)} async-done(((bf16[16,13,1024]{2,1,0:T(8,128)(2,1)}), bf16[16,13,1024]{2,1,0:T(8,128)(2,1)S(1)}, u32[]{:S(2)}, u32[]{:S(2)}) %all-to-all-start.2) | async-done | bytes 426016 | tf_op jit(solution)/shard_map/all_to_all | solution.py:130
  151.3 17.4 %all-gather.1 = f32[16,13,1024]{2,1,0:T(8,128)S(1)} all-gather(f32[1,13,1024]{2,1,0:T(8,128)S(1)} %bitcast.70), channel_id=2, replica_groups=mesh['lat'=16,'lon'=64] {'lat'}, dimensions={0}, use_global_device_ids=true | all-gather | bytes 905216 | tf_op jit(solution)/shard_map/all_gather | solution.py:132
  168.7 1.1 reshape.476
  169.8 1.2 slice.67
  171.0 0.7 reshape.477
  171.7 2.1 %fusion.60 = (bf16[10,2,8,1281]{3,2,1,0:T(8,128)(2,1)S(1)}, f32[10,2,8,1281]{3,2,1,0:T(8,128)}) fusion(f32[10,2,8,1281]{3,2,1,0:T(8,128)S(1)} %reshape.477, f32[10,8,1281]{2,1,0:T(8,128)} %multiply_add_fusion), kind=kLoop, calls=%fused_computation.119 | loop fusion | flops 409920 | bytes 2459520 | tf_op jit(solution)/shard_map/convert_element_type | solution.py:162
  174.0 1.4 fusion.9
  (56 shorter events, 4.6 us)
Async XLA Ops:
  0.6 115.0 %copy-start = (bf16[64,10,1281]{2,0,1:T(8,128)(2,1)S(1)}, bf16[64,10,1281]{2,0,1:T(8,128)(2,1)}, u32[]{:S(2)}) copy-start(bf16[64,10,1281]{2,0,1:T(8,128)(2,1)} %param.12) | copy-start | bytes 4919044
  2.7 22.3 %collective-permute-start = (bf16[8,2,64,10]{3,2,1,0:T(8,128)(2,1)}, bf16[8,2,64,10]{3,2,1,0:T(8,128)(2,1)S(1)}, u32[]{:S(2)}, u32[]{:S(2)}) collective-permute-start(bf16[8,2,64,10]{3,2,1,0:T(8,128)(2,1)} %get-tuple-element.29), channel_id=1, source_target_pairs={{0,1},{1,2},{2,3},{3,4},{4,5},{5,6},{6,7},{7,8},{8,9},{9,10},{10,1... | collective-permute-start | bytes 61448 | tf_op jit(solution)/shard_map/ppermute | solution.py:23
  8.4 16.6 %collective-permute-start.1 = (bf16[8,2,64,10]{3,2,1,0:T(8,128)(2,1)S(1)}, bf16[8,2,64,10]{3,2,1,0:T(8,128)(2,1)S(1)}, u32[]{:S(2)}, u32[]{:S(2)}) collective-permute-start(bf16[8,2,64,10]{3,2,1,0:T(8,128)(2,1)S(1)} %get-tuple-element.30), channel_id=1, source_target_pairs={{1,0},{2,1},{3,2},{4,3},{5,4},{6,5},{7,6},{8,7},{9,8},{10,9},{11,1... | collective-permute-start | bytes 61448 | tf_op jit(solution)/shard_map/ppermute | solution.py:24
  11.1 10.5 %copy-start.8 = (s32[640,2]{0,1:T(2,128)}, s32[640,2]{0,1:T(2,128)S(1)}, u32[]{:S(2)}) copy-start(s32[640,2]{0,1:T(2,128)S(1)} %pad_add_fusion) | copy-start | bytes 15364
  21.6 3.4 %copy-start.1 = (bf16[8,2,64,65]{3,2,1,0:T(8,128)(2,1)S(1)}, bf16[8,2,64,65]{3,2,1,0:T(8,128)(2,1)}, u32[]{:S(2)}) copy-start(bf16[8,2,64,65]{3,2,1,0:T(8,128)(2,1)} %param.7) | copy-start | bytes 399364
  21.6 15.1 %copy-start.9 = (s32[2,64,65]{2,1,0:T(8,128)S(1)}, s32[2,64,65]{2,1,0:T(8,128)}, u32[]{:S(2)}) copy-start(s32[2,64,65]{2,1,0:T(8,128)} %param.9) | copy-start | bytes 99844
  21.7 15.1 %copy-start.10 = (s32[2,64,65]{2,1,0:T(8,128)S(1)}, s32[2,64,65]{2,1,0:T(8,128)}, u32[]{:S(2)}) copy-start(s32[2,64,65]{2,1,0:T(8,128)} %param.8) | copy-start | bytes 99844
  21.7 16.5 %copy-start.11 = (bf16[2,64,65]{2,1,0:T(8,128)(2,1)S(1)}, bf16[2,64,65]{2,1,0:T(8,128)(2,1)}, u32[]{:S(2)}) copy-start(bf16[2,64,65]{2,1,0:T(8,128)(2,1)} %param.10) | copy-start | bytes 49924
  25.1 15.8 %collective-permute-start.3 = (bf16[8,2,1,85]{3,2,1,0:T(2,128)(2,1)S(1)}, bf16[8,2,1,85]{3,2,1,0:T(2,128)(2,1)S(1)}, u32[]{:S(2)}, u32[]{:S(2)}) collective-permute-start(bf16[8,2,1,85]{3,2,1,0:T(2,128)(2,1)S(1)} %get-tuple-element.26), channel_id=1, source_target_pairs={{64,0},{128,64},{192,128},{256,192},{320,256},{384,320},{448,384},... | collective-permute-start | bytes 8168 | tf_op jit(solution)/shard_map/ppermute | solution.py:24
  38.8 3.1 %collective-permute-start.2 = (bf16[8,2,1,85]{3,2,1,0:T(2,128)(2,1)S(1)}, bf16[8,2,1,85]{3,2,1,0:T(2,128)(2,1)S(1)}, u32[]{:S(2)}, u32[]{:S(2)}) collective-permute-start(bf16[8,2,1,85]{3,2,1,0:T(2,128)(2,1)S(1)} %get-tuple-element.25), channel_id=1, source_target_pairs={{0,64},{64,128},{128,192},{192,256},{256,320},{320,384},{384,448},... | collective-permute-start | bytes 8168 | tf_op jit(solution)/shard_map/ppermute | solution.py:23
  56.1 28.6 %all-to-all-start = ((bf16[8,2,64,65]{3,1,0,2:T(2,128)(2,1)}), bf16[8,2,64,65]{3,1,0,2:T(2,128)(2,1)}, u32[]{:S(2)}, u32[]{:S(2)}) async-start(bf16[8,2,64,65]{3,1,0,2:T(2,128)(2,1)} %copy.21), calls=%async_computation | async-start | bytes 524288 | tf_op jit(solution)/shard_map/all_to_all | solution.py:203
  90.1 13.0 %copy-start.6 = (f32[10,1,1281]{2,1,0:T(1,128)S(1)}, f32[10,1,1281]{2,1,0:T(1,128)}, u32[]{:S(2)}) copy-start(f32[10,1,1281]{2,1,0:T(1,128)} %get-tuple-element.41) | copy-start | bytes 153724
  90.1 13.0 %copy-start.7 = (f32[10,1,1281]{2,1,0:T(1,128)S(1)}, f32[10,1,1281]{2,1,0:T(1,128)}, u32[]{:S(2)}) copy-start(f32[10,1,1281]{2,1,0:T(1,128)} %get-tuple-element.42) | copy-start | bytes 153724
  98.0 16.4 %all-to-all-start.1 = ((bf16[64,2,320]{2,1,0:T(2,128)(2,1)}), bf16[64,2,320]{2,1,0:T(2,128)(2,1)S(1)}, u32[]{:S(2)}, u32[]{:S(2)}) async-start(bf16[64,2,320]{2,1,0:T(2,128)(2,1)} %reshape.487), calls=%async_computation.1 | async-start | bytes 196608 | tf_op jit(solution)/shard_map/all_to_all | solution.py:213
  121.6 12.4 %copy-start.2 = (f32[10,2,1281]{2,1,0:T(2,128)S(1)}, f32[10,2,1281]{2,1,0:T(2,128)}, u32[]{:S(2)}) copy-start(f32[10,2,1281]{2,1,0:T(2,128)} %pad_maximum_fusion) | copy-start | bytes 307444
  121.6 12.4 %copy-start.3 = (f32[10,2,1281]{2,1,0:T(2,128)S(1)}, f32[10,2,1281]{2,1,0:T(2,128)}, u32[]{:S(2)}) copy-start(f32[10,2,1281]{2,1,0:T(2,128)} %stack.58) | copy-start | bytes 307444
  121.6 13.1 %copy-start.5 = (f32[10,1281]{1,0:T(8,128)S(1)}, f32[10,1281]{1,0:T(8,128)}, u32[]{:S(2)}) copy-start(f32[10,1281]{1,0:T(8,128)} %get-tuple-element.31) | copy-start | bytes 153724
  121.6 13.1 %copy-start.12 = (f32[8]{0:T(128)S(1)}, f32[8]{0:T(128)}, u32[]{:S(2)}) copy-start(f32[8]{0:T(128)} %param.13) | copy-start | bytes 100
  124.3 26.9 %all-to-all-start.2 = ((bf16[16,13,1024]{2,1,0:T(8,128)(2,1)}), bf16[16,13,1024]{2,1,0:T(8,128)(2,1)S(1)}, u32[]{:S(2)}, u32[]{:S(2)}) async-start(bf16[16,13,1024]{2,1,0:T(8,128)(2,1)} %convert_element_type.122), calls=%async_computation.2 | async-start | bytes 1048576 | tf_op jit(solution)/shard_map/all_to_all | solution.py:130
  171.7 2.1 %copy-start.4 = (bf16[10,2,2,1281]{3,2,1,0:T(2,128)(2,1)S(1)}, bf16[10,2,2,1281]{3,2,1,0:T(2,128)(2,1)}, u32[]{:S(2)}) copy-start(bf16[10,2,2,1281]{3,2,1,0:T(2,128)(2,1)} %multiply_convert_fusion) | copy-start | bytes 307444

commit v5 on v4

--- a/solution.py
+++ b/solution.py
@@ -200,14 +200,11 @@
         col_shift,
         lon_weight,
     )
+    advected, pair_tie = lax.optimization_barrier((advected, pair_of_slot))
     row_data = lax.all_to_all(advected, "lon", split_axis=2, concat_axis=3, tiled=True)
     lat_rows = first_row + jnp.arange(row_count, dtype=jnp.int32)
     per_row = jnp.moveaxis(row_data, 2, 0)
-
-    def spectrum_of_row(row_item):
-        return row_spectrum(row_item[0], row_item[1], pair_of_slot)
-
-    spectra = lax.map(spectrum_of_row, (per_row, lat_rows))
+    spectra = jax.vmap(lambda row, lat: row_spectrum(row, lat, pair_tie))(per_row, lat_rows)
     gathered = jax.tree.map(
         lambda part, own: part.astype(own.dtype),
         lax.all_to_all(shortened(spectra), "lon", split_axis=1, concat_axis=0, tiled=True),

time: 177 us -> 178 us (level)
  other arithmetic: 28.7 us -> 32.8 us
  local copies, waits for them, and re-layouts: 24.1 us -> 22.3 us
  transfers between devices with their start and end apart: 7 -> 7, of which waited for: 4 -> 5; matrix products, arithmetic and copies ran while one was open for 14% -> 12% of each run, Pallas kernels for 0% -> 0%
where the time goes in v5:
time: 178 us; the launch traced here: 177 us
  starting transfers between devices  51.3 us (29%)
  waiting for transfers between devices  34.8 us (20%)
  other arithmetic  32.8 us (18%)
  local copies, waits for them, and re-layouts  22.3 us (13%)
  blocking collectives  17.4 us (10%)
  Pallas kernels  11 us (6%)
  matrix products  6.51 us (4%)
    all_gather x1, blocking collectives, lat_sum(): whole = lax.all_gather(reduced, 'lat', axis=0, tiled=True)  17.4 us
    all_to_all x1, starting transfers between devices, on_device(): lax.all_to_all(advected, 'lon', split_axis=2, concat_axis=3, tiled=True)  15.8 us
    all_to_all x1, waiting for transfers between devices, lat_sum(): pieces = lax.all_to_all(flat.astype(jnp.bfloat16), 'lat', 0, 0, tiled=True)  15.6 us
    ppermute x2, starting transfers between devices, extended_2(): after = lax.ppermute(initial, axis, down)  12.5 us
    pallas_call x1, Pallas kernels, depart_values(): pl.pallas_call(depart_kernel, grid=(field_count,), in_specs=[pl.BlockSpec...  11 us
    all_to_all x1, waiting for transfers between devices, on_device(): lax.all_to_all(shortened(spectra), 'lon', split_axis=1, concat_axis=0, ti...  10.5 us
    all_to_all x1, starting transfers between devices, lat_sum(): pieces = lax.all_to_all(flat.astype(jnp.bfloat16), 'lat', 0, 0, tiled=True)  10.2 us
    all_to_all x1, waiting for transfers between devices, on_device(): lax.all_to_all(advected, 'lon', split_axis=2, concat_axis=3, tiled=True)  7.84 us
  transfers between devices with their start and end apart: 7, of which 5 were waited for; matrix products, arithmetic and copies ran while one was open for 12% of the time, Pallas kernels for 0%

profile of v5, /device:TPU:1, one launch (start us, length us, event | category | flops | bytes accessed | tf_op | source)
XLA Modules:
  0.0 177.2 jit_solution(4114173639644650130)
XLA Ops:
  0.7 1.3 fusion.65
  2.0 5.7 %collective-permute-start = (bf16[8,2,64,10]{3,2,1,0:T(8,128)(2,1)S(1)}, bf16[8,2,64,10]{3,2,1,0:T(8,128)(2,1)S(1)}, u32[]{:S(2)}, u32[]{:S(2)}) collective-permute-start(bf16[8,2,64,10]{3,2,1,0:T(8,128)(2,1)S(1)} %get-tuple-element.18), channel_id=1, source_target_pairs={{0,1},{1,2},{2,3},{3,4},{4,5},{5,6},{6,7},{7,8},{8,9},{9,10},{10,1... | collective-permute-start | bytes 61448 | tf_op jit(solution)/shard_map/ppermute | solution.py:23
  7.7 1.3 collective-permute-start.1
  9.1 0.8 broadcast_subtract_fusion.1
  10.5 0.7 fusion.51
  11.3 0.9 fusion.48
  12.2 0.8 fusion.36
  13.1 2.3 %fusion.43.code_ref = s32[2,64,65]{2,1,0:T(8,128)} fusion(s32[2,64,65]{2,1,0:T(8,128)} %param.9, s32[2,64,65]{2,1,0:T(8,128)} %param.8, s32[]{:T(128)S(6)} %sub.173, s32[64]{0:T(128)S(1)} %get-tuple-element.34, s32[64]{0:T(128)S(1)} %get-tuple-element.35, s32[65]{0:T(128)S(1)} %iota_add_fusion.2, s32[64]{0:T(128)S(1)} %get-tuple-element.33, s32[]{:T(128)S(6)} %mul.440, ...), kind=kLoop, calls=%fused_computation.77 | loop fusion | flops 241280 | bytes 105292 | tf_op jit(solution)/shard_map/jit(_where)/select_n | solution.py:69
  16.4 1.5 pad_maximum_fusion.3
  17.9 11.2 %collective-permute-start.3 = (bf16[8,2,1,85]{3,2,1,0:T(2,128)(2,1)}, bf16[8,2,1,85]{3,2,1,0:T(2,128)(2,1)}, u32[]{:S(2)}, u32[]{:S(2)}) collective-permute-start(bf16[8,2,1,85]{3,2,1,0:T(2,128)(2,1)} %get-tuple-element.15), channel_id=1, source_target_pairs={{64,0},{128,64},{192,128},{256,192},{320,256},{384,320},{448,384},... | collective-permute-start | bytes 8168 | tf_op jit(solution)/shard_map/ppermute | solution.py:24
  29.7 1.4 convert_element_type.117.weight_ref
  31.1 1.0 mul.486
  32.1 1.5 mul.487
  33.6 1.5 stack.46
  35.2 1.9 %collective-permute-start.2 = (bf16[8,2,1,85]{3,2,1,0:T(2,128)(2,1)}, bf16[8,2,1,85]{3,2,1,0:T(2,128)(2,1)S(1)}, u32[]{:S(2)}, u32[]{:S(2)}) collective-permute-start(bf16[8,2,1,85]{3,2,1,0:T(2,128)(2,1)} %get-tuple-element.14), channel_id=1, source_target_pairs={{0,64},{64,128},{128,192},{192,256},{256,320},{320,384},{384,448},... | collective-permute-start | bytes 8168 | tf_op jit(solution)/shard_map/ppermute | solution.py:23
  37.1 0.8 broadcast_select_fusion
  38.4 1.2 maximum_convert_fusion.ext_ref
  39.6 11.0 %shard_map.86 = f32[8,2,64,65]{3,2,1,0:T(8,128)} custom-call(f32[8,2,66,85]{3,2,1,0:T(8,128)} %maximum_convert_fusion.ext_ref, s32[2,64,65]{2,1,0:T(8,128)} %fusion.43.code_ref, f32[2,64,65]{2,1,0:T(8,128)} %convert_element_type.117.weight_ref), custom_call_target="tpu_custom_call" | custom-call | tf_op jit(solution)/shard_map/pallas_call | solution.py:71
  50.6 1.1 select_convert_fusion
  51.8 2.2 %fusion.38 = (f32[32,640,2]{1,0,2:T(8,128)S(1)}, f32[32,640,2]{1,0,2:T(8,128)S(1)}) fusion(f32[]{:T(128)} %bitcast.4, pred[]{:T(512)} %bitcast.3, s32[]{:T(128)} %bitcast.2, s32[640,2]{0,1:T(2,128)S(1)} %pad_add_fusion), kind=kLoop, calls=%fused_computation.72 | loop fusion | flops 450560 | bytes 332809 | tf_op jit(solution)/shard_map/vmap()/cos | solution.py:88
  54.0 2.8 %fusion.31 = (f32[33,640,2]{1,0,2:T(8,128)S(1)}, f32[33,640,2]{1,0,2:T(8,128)S(1)}) fusion(f32[]{:T(128)} %bitcast.4, pred[]{:T(512)} %bitcast.3, s32[]{:T(128)} %bitcast.2, s32[33]{0:T(128)S(1)} %copy-done.12, s32[640,2]{0,1:T(2,128)S(1)} %pad_add_fusion), kind=kLoop, calls=%fused_computation.63 | loop fusion | flops 464640 | bytes 343181 | tf_op jit(solution)/shard_map/vmap()/cos | solution.py:88
  56.8 1.0 copy.21
  57.8 15.8 %all-to-all-start = ((bf16[8,2,64,65]{3,1,0,2:T(2,128)(2,1)}), bf16[8,2,64,65]{3,1,0,2:T(2,128)(2,1)S(1)}, u32[]{:S(2)}, u32[]{:S(2)}) async-start(bf16[8,2,64,65]{3,1,0,2:T(2,128)(2,1)} %copy.21), calls=%async_computation | async-start | bytes 524288 | tf_op jit(solution)/shard_map/all_to_all | solution.py:204
  73.6 2.0 %multiply_subtract_fusion = (bf16[33,32,640,2]{2,1,0,3:T(8,128)(2,1)S(1)}, bf16[33,32,640,2]{2,1,0,3:T(8,128)(2,1)S(1)}) fusion(f32[32,640,2]{1,0,2:T(8,128)S(1)} %get-tuple-element.27, f32[33,640,2]{1,0,2:T(8,128)S(1)} %get-tuple-element.23, f32[32,640,2]{1,0,2:T(8,128)S(1)} %get-tuple-element.26, f32[33,640,2]{1,0,2:T(8,128)S(1)} %get-tuple-element.22), kind=kLoop, calls=%fused_computation.3 | loop fusion | flops 12165120 | bytes 6072320 | tf_op jit(solution)/shard_map/vmap()/sub | solution.py:105
  75.7 3.3 %fusion.6 = (bf16[1040,640,2,1]{1,0,3,2:T(8,128)(2,1)}, bf16[1040,640,2,1]{1,0,3,2:T(8,128)(2,1)}) fusion(bf16[1,1056,640,2]{2,1,3,0:T(8,128)(2,1)S(1)} %bitcast.75, pred[640,2]{0,1:T(4,128)(4,1)S(1)} %multiply_compare_fusion, pred[1040]{0:T(1024)(128)(4,1)S(1)} %copy-done.10, bf16[1,1056,640,2]{2,1,3,0:T(8,128)(2,1)S(1)} %bitcast.76), kind=kLoop, calls=%fused_computation.11 | loop fusion | flops 3993600 | bytes 10651920 | tf_op jit(solution)/shard_map/vmap()/stack | solution.py:111
  79.5 7.8 %all-to-all-done = bf16[8,2,64,65]{3,1,0,2:T(2,128)(2,1)S(1)} async-done(((bf16[8,2,64,65]{3,1,0,2:T(2,128)(2,1)}), bf16[8,2,64,65]{3,1,0,2:T(2,128)(2,1)S(1)}, u32[]{:S(2)}, u32[]{:S(2)}) %all-to-all-start) | async-done | bytes 133152 | tf_op jit(solution)/shard_map/all_to_all | solution.py:204
  87.4 4.0 %copy.22 = bf16[8,2,64,65]{0,1,3,2:T(2,128)(2,1)} copy(bf16[8,2,64,65]{3,1,0,2:T(2,128)(2,1)S(1)} %all-to-all-done) | data formatting | bytes 266240 | tf_op jit(solution)/shard_map/all_to_all | solution.py:204
  91.4 4.5 %fusion.9 = f32[1,640,2,2,8,2,4]{1,4,6,5,3,2,0:T(8,128)S(1)} fusion(bf16[8,2,1040,4,1,1]{0,1,3,2,5,4:T(2,128)(2,1)} %bitcast.78, bf16[1040,640,2,1]{1,0,3,2:T(8,128)(2,1)} %get-tuple-element.29, bf16[1040,640,2,1]{1,0,3,2:T(8,128)(2,1)} %get-tuple-element.28), kind=kOutput, calls=%fused_computation.16 | convolution fusion | flops 351436800 | bytes 6113280 | tf_op jit(solution)/shard_map/vmap(aser,fhab->serfhb)/dot_general | solution.py:114
  96.7 1.7 reduce.4
  98.4 0.8 reshape.757
  99.2 5.1 %all-to-all-start.1 = ((bf16[64,2,320]{2,1,0:T(2,128)(2,1)}), bf16[64,2,320]{2,1,0:T(2,128)(2,1)S(1)}, u32[]{:S(2)}, u32[]{:S(2)}) async-start(bf16[64,2,320]{2,1,0:T(2,128)(2,1)} %reshape.757), calls=%async_computation.1 | async-start | bytes 196608 | tf_op jit(solution)/shard_map/all_to_all | solution.py:210
  104.3 0.8 pad_maximum_fusion
  105.1 10.5 %all-to-all-done.1 = bf16[64,2,320]{2,1,0:T(2,128)(2,1)S(1)} async-done(((bf16[64,2,320]{2,1,0:T(2,128)(2,1)}), bf16[64,2,320]{2,1,0:T(2,128)(2,1)S(1)}, u32[]{:S(2)}, u32[]{:S(2)}) %all-to-all-start.1) | async-done | bytes 81952 | tf_op jit(solution)/shard_map/all_to_all | solution.py:210
  115.7 1.0 bitcast_reduce_fusion
  117.7 1.0 fusion.64
  118.8 2.6 %squeeze.24 = f32[204960]{0:T(1024)} reshape(f32[10,1,2,8,1281]{4,3,2,1,0:T(8,128)} %get-tuple-element.13) | data formatting | bytes 1639680 | tf_op jit(solution)/shard_map/squeeze | solution.py:151
  121.4 1.4 squeeze.25
  122.9 1.5 add_convert_fusion
  124.5 1.1 convert_element_type.127
  125.6 10.2 %all-to-all-start.2 = ((bf16[16,13,1024]{2,1,0:T(8,128)(2,1)}), bf16[16,13,1024]{2,1,0:T(8,128)(2,1)S(1)}, u32[]{:S(2)}, u32[]{:S(2)}) async-start(bf16[16,13,1024]{2,1,0:T(8,128)(2,1)} %convert_element_type.127), calls=%async_computation.2 | async-start | bytes 1048576 | tf_op jit(solution)/shard_map/all_to_all | solution.py:130
  135.8 0.7 multiply_convert_fusion
  136.5 0.9 multiply_add_fusion
  137.4 15.6 %all-to-all-done.2 = bf16[16,13,1024]{2,1,0:T(8,128)(2,1)S(1)} async-done(((bf16[16,13,1024]{2,1,0:T(8,128)(2,1)}), bf16[16,13,1024]{2,1,0:T(8,128)(2,1)S(1)}, u32[]{:S(2)}, u32[]{:S(2)}) %all-to-all-start.2) | async-done | bytes 426016 | tf_op jit(solution)/shard_map/all_to_all | solution.py:130
  153.1 17.4 %all-gather.1 = f32[16,13,1024]{2,1,0:T(8,128)S(1)} all-gather(f32[1,13,1024]{2,1,0:T(8,128)S(1)} %bitcast.83), channel_id=2, replica_groups=mesh['lat'=16,'lon'=64] {'lat'}, dimensions={0}, use_global_device_ids=true | all-gather | bytes 905216 | tf_op jit(solution)/shard_map/all_gather | solution.py:132
  170.5 1.1 reshape.746
  171.5 1.2 slice.63
  173.5 2.1 %fusion.63 = (bf16[10,2,8,1281]{3,2,1,0:T(8,128)(2,1)S(1)}, f32[10,2,8,1281]{3,2,1,0:T(8,128)}) fusion(f32[10,2,8,1281]{3,2,1,0:T(8,128)S(1)} %reshape.747, f32[10,8,1281]{2,1,0:T(8,128)} %multiply_add_fusion), kind=kLoop, calls=%fused_computation.120 | loop fusion | flops 409920 | bytes 2459520 | tf_op jit(solution)/shard_map/convert_element_type | solution.py:162
  175.8 1.4 fusion.12
  (56 shorter events, 6.7 us)
Async XLA Ops:
  0.6 116.1 %copy-start = (bf16[64,10,1281]{2,0,1:T(8,128)(2,1)S(1)}, bf16[64,10,1281]{2,0,1:T(8,128)(2,1)}, u32[]{:S(2)}) copy-start(bf16[64,10,1281]{2,0,1:T(8,128)(2,1)} %param.12) | copy-start | bytes 4919044
  0.6 37.8 %copy-start.1 = (bf16[8,2,64,65]{3,2,1,0:T(8,128)(2,1)S(1)}, bf16[8,2,64,65]{3,2,1,0:T(8,128)(2,1)}, u32[]{:S(2)}) copy-start(bf16[8,2,64,65]{3,2,1,0:T(8,128)(2,1)} %param.7) | copy-start | bytes 399364
  2.0 14.0 %collective-permute-start = (bf16[8,2,64,10]{3,2,1,0:T(8,128)(2,1)S(1)}, bf16[8,2,64,10]{3,2,1,0:T(8,128)(2,1)S(1)}, u32[]{:S(2)}, u32[]{:S(2)}) collective-permute-start(bf16[8,2,64,10]{3,2,1,0:T(8,128)(2,1)S(1)} %get-tuple-element.18), channel_id=1, source_target_pairs={{0,1},{1,2},{2,3},{3,4},{4,5},{5,6},{6,7},{7,8},{8,9},{9,10},{10,1... | collective-permute-start | bytes 61448 | tf_op jit(solution)/shard_map/ppermute | solution.py:23
  7.7 8.7 %collective-permute-start.1 = (bf16[8,2,64,10]{3,2,1,0:T(8,128)(2,1)S(1)}, bf16[8,2,64,10]{3,2,1,0:T(8,128)(2,1)S(1)}, u32[]{:S(2)}, u32[]{:S(2)}) collective-permute-start(bf16[8,2,64,10]{3,2,1,0:T(8,128)(2,1)S(1)} %get-tuple-element.19), channel_id=1, source_target_pairs={{1,0},{2,1},{3,2},{4,3},{5,4},{6,5},{7,6},{8,7},{9,8},{10,9},{11,1... | collective-permute-start | bytes 61448 | tf_op jit(solution)/shard_map/ppermute | solution.py:24
  17.9 19.2 %collective-permute-start.3 = (bf16[8,2,1,85]{3,2,1,0:T(2,128)(2,1)}, bf16[8,2,1,85]{3,2,1,0:T(2,128)(2,1)}, u32[]{:S(2)}, u32[]{:S(2)}) collective-permute-start(bf16[8,2,1,85]{3,2,1,0:T(2,128)(2,1)} %get-tuple-element.15), channel_id=1, source_target_pairs={{64,0},{128,64},{192,128},{256,192},{320,256},{384,320},{448,384},... | collective-permute-start | bytes 8168 | tf_op jit(solution)/shard_map/ppermute | solution.py:24
  33.6 18.1 %copy-start.9 = (s32[640]{0:T(1024)S(1)}, s32[640]{0:T(1024)}, u32[]{:S(2)}) copy-start(s32[640]{0:T(1024)} %param.11) | copy-start | bytes 7684
  33.6 20.4 %copy-start.12 = (s32[33]{0:T(128)S(1)}, s32[33]{0:T(128)}, u32[]{:S(2)}) copy-start(s32[33]{0:T(128)} %iota_multiply_fusion) | copy-start | bytes 400
  35.2 3.3 %collective-permute-start.2 = (bf16[8,2,1,85]{3,2,1,0:T(2,128)(2,1)}, bf16[8,2,1,85]{3,2,1,0:T(2,128)(2,1)S(1)}, u32[]{:S(2)}, u32[]{:S(2)}) collective-permute-start(bf16[8,2,1,85]{3,2,1,0:T(2,128)(2,1)} %get-tuple-element.14), channel_id=1, source_target_pairs={{0,64},{64,128},{128,192},{192,256},{256,320},{320,384},{384,448},... | collective-permute-start | bytes 8168 | tf_op jit(solution)/shard_map/ppermute | solution.py:23
  57.8 29.6 %all-to-all-start = ((bf16[8,2,64,65]{3,1,0,2:T(2,128)(2,1)}), bf16[8,2,64,65]{3,1,0,2:T(2,128)(2,1)S(1)}, u32[]{:S(2)}, u32[]{:S(2)}) async-start(bf16[8,2,64,65]{3,1,0,2:T(2,128)(2,1)} %copy.21), calls=%async_computation | async-start | bytes 524288 | tf_op jit(solution)/shard_map/all_to_all | solution.py:204
  73.6 2.1 %copy-start.10 = (pred[1040]{0:T(1024)(128)(4,1)S(1)}, pred[1040]{0:T(1024)(128)(4,1)}, u32[]{:S(2)}) copy-start(pred[1040]{0:T(1024)(128)(4,1)} %iota_compare_fusion.2) | copy-start | bytes 3124
  91.4 12.9 %copy-start.7 = (f32[10,1,1281]{2,1,0:T(1,128)S(1)}, f32[10,1,1281]{2,1,0:T(1,128)}, u32[]{:S(2)}) copy-start(f32[10,1,1281]{2,1,0:T(1,128)} %get-tuple-element.31) | copy-start | bytes 153724
  99.2 16.4 %all-to-all-start.1 = ((bf16[64,2,320]{2,1,0:T(2,128)(2,1)}), bf16[64,2,320]{2,1,0:T(2,128)(2,1)S(1)}, u32[]{:S(2)}, u32[]{:S(2)}) async-start(bf16[64,2,320]{2,1,0:T(2,128)(2,1)} %reshape.757), calls=%async_computation.1 | async-start | bytes 196608 | tf_op jit(solution)/shard_map/all_to_all | solution.py:210
  116.8 0.7 copy-start.8
  117.7 5.1 %copy-start.2 = (f32[204960]{0:T(1024)S(1)}, f32[204960]{0:T(1024)}, u32[]{:S(2)}) copy-start(f32[204960]{0:T(1024)} %mul.487) | copy-start | bytes 2459524
  122.8 12.9 %copy-start.3 = (f32[10,2,1281]{2,1,0:T(2,128)S(1)}, f32[10,2,1281]{2,1,0:T(2,128)}, u32[]{:S(2)}) copy-start(f32[10,2,1281]{2,1,0:T(2,128)} %pad_maximum_fusion) | copy-start | bytes 307444
  122.8 12.9 %copy-start.4 = (f32[10,2,1281]{2,1,0:T(2,128)S(1)}, f32[10,2,1281]{2,1,0:T(2,128)}, u32[]{:S(2)}) copy-start(f32[10,2,1281]{2,1,0:T(2,128)} %stack.46) | copy-start | bytes 307444
  122.9 13.7 %copy-start.6 = (f32[10,1281]{1,0:T(8,128)S(1)}, f32[10,1281]{1,0:T(8,128)}, u32[]{:S(2)}) copy-start(f32[10,1281]{1,0:T(8,128)} %get-tuple-element.20) | copy-start | bytes 153724
  122.9 13.7 %copy-start.11 = (f32[8]{0:T(128)S(1)}, f32[8]{0:T(128)}, u32[]{:S(2)}) copy-start(f32[8]{0:T(128)} %param.13) | copy-start | bytes 100
  125.6 27.4 %all-to-all-start.2 = ((bf16[16,13,1024]{2,1,0:T(8,128)(2,1)}), bf16[16,13,1024]{2,1,0:T(8,128)(2,1)S(1)}, u32[]{:S(2)}, u32[]{:S(2)}) async-start(bf16[16,13,1024]{2,1,0:T(8,128)(2,1)} %convert_element_type.127), calls=%async_computation.2 | async-start | bytes 1048576 | tf_op jit(solution)/shard_map/all_to_all | solution.py:130
  173.4 2.1 %copy-start.5 = (bf16[10,2,2,1281]{3,2,1,0:T(2,128)(2,1)S(1)}, bf16[10,2,2,1281]{3,2,1,0:T(2,128)(2,1)}, u32[]{:S(2)}) copy-start(bf16[10,2,2,1281]{3,2,1,0:T(2,128)(2,1)} %multiply_convert_fusion) | copy-start | bytes 307444

commit v6 on v5

--- a/solution.py
+++ b/solution.py
@@ -124,6 +124,16 @@
 
 def lat_sum(value):
     peers = lax.axis_size("lat")
+    lead = value.shape[0]
+    grouped = value.reshape(lead, -1, value.shape[-1])
+    groups = grouped.shape[1]
+    if groups % peers == 0:
+        grouped = jnp.moveaxis(grouped, 1, 0)
+        pieces = lax.all_to_all(grouped.astype(jnp.bfloat16), "lat", 0, 0, tiled=True)
+        pieces = pieces.astype(jnp.float32).reshape((peers, groups // peers) + grouped.shape[1:])
+        reduced = jnp.sum(pieces, axis=0)
+        whole = lax.all_gather(reduced, "lat", axis=0, tiled=True)
+        return jnp.moveaxis(whole, 0, 1).reshape(value.shape)
     count = value.size
     pad = (-count) % (peers * 1024)
     flat = jnp.pad(value.reshape(-1), (0, pad)).reshape(peers, -1, 1024)

time: 178 us -> 170 us (0.955)
  local copies, waits for them, and re-layouts: 22.3 us -> 10.6 us
  waiting for transfers between devices: 34.8 us -> 43.5 us
  other arithmetic: 32.8 us -> 26.2 us
    all_to_all x1, waiting for transfers between devices: 15.6 us -> 21.1 us  [lat_sum(): lax.all_to_all(grouped.astype(jnp.bfloat16), 'lat', 0, 0, tiled=True)]
    squeeze x2 -> x0, local copies, waits for them, and re-layouts: 4.08 us -> none  [analyse(): return chosen[:, 0] + parity[:, None, None, :] * chosen[:, 1]]
    mul x2 -> x0, local copies, waits for them, and re-layouts: 2.47 us -> none  [analyse(): return chosen[:, 0] + parity[:, None, None, :] * chosen[:, 1]]
    ppermute x2, waiting for transfers between devices: 0.36 us -> 2.25 us  [extended_2(): after = lax.ppermute(initial, axis, down)]
  transfers between devices with their start and end apart: 7 -> 7, of which waited for: 5 -> 5; matrix products, arithmetic and copies ran while one was open for 12% -> 8% of each run, Pallas kernels for 0% -> 0%
where the time goes in v6:
time: 170 us; the launch traced here: 169 us
  starting transfers between devices  51.3 us (30%)
  waiting for transfers between devices  43.5 us (26%)
  other arithmetic  26.2 us (15%)
  blocking collectives  18.8 us (11%)
  Pallas kernels  11 us (6%)
  local copies, waits for them, and re-layouts  10.6 us (6%)
  matrix products  6.5 us (4%)
    all_to_all x1, waiting for transfers between devices, lat_sum(): lax.all_to_all(grouped.astype(jnp.bfloat16), 'lat', 0, 0, tiled=True)  21.1 us
    all_gather x1, blocking collectives, lat_sum(): whole = lax.all_gather(reduced, 'lat', axis=0, tiled=True)  18.8 us
    all_to_all x1, starting transfers between devices, on_device(): lax.all_to_all(advected, 'lon', split_axis=2, concat_axis=3, tiled=True)  15.8 us
    ppermute x2, starting transfers between devices, extended_2(): after = lax.ppermute(initial, axis, down)  12.5 us
    all_to_all x1, waiting for transfers between devices, on_device(): lax.all_to_all(shortened(spectra), 'lon', split_axis=1, concat_axis=0, ti...  11.1 us
    pallas_call x1, Pallas kernels, depart_values(): pl.pallas_call(depart_kernel, grid=(field_count,), in_specs=[pl.BlockSpec...  11 us
    all_to_all x1, starting transfers between devices, lat_sum(): lax.all_to_all(grouped.astype(jnp.bfloat16), 'lat', 0, 0, tiled=True)  10.2 us
    all_to_all x1, waiting for transfers between devices, on_device(): lax.all_to_all(advected, 'lon', split_axis=2, concat_axis=3, tiled=True)  7.85 us
  transfers between devices with their start and end apart: 7, of which 5 were waited for; matrix products, arithmetic and copies ran while one was open for 8% of the time, Pallas kernels for 0%

profile of v6, /device:TPU:1, one launch (start us, length us, event | category | flops | bytes accessed | tf_op | source)
XLA Modules:
  0.0 168.9 jit_solution(13290074367811698829)
XLA Ops:
  0.7 1.3 fusion.67
  2.0 5.7 %collective-permute-start = (bf16[8,2,64,10]{3,2,1,0:T(8,128)(2,1)S(1)}, bf16[8,2,64,10]{3,2,1,0:T(8,128)(2,1)S(1)}, u32[]{:S(2)}, u32[]{:S(2)}) collective-permute-start(bf16[8,2,64,10]{3,2,1,0:T(8,128)(2,1)S(1)} %get-tuple-element.18), channel_id=1, source_target_pairs={{0,1},{1,2},{2,3},{3,4},{4,5},{5,6},{6,7},{7,8},{8,9},{9,10},{10,1... | collective-permute-start | bytes 61448 | tf_op jit(solution)/shard_map/ppermute | solution.py:23
  7.7 1.3 collective-permute-start.1
  9.1 0.8 broadcast_subtract_fusion.1
  9.8 0.7 iota_compare_fusion
  10.7 0.3 fusion.50
  11.2 2.3 %fusion.45.code_ref = s32[2,64,65]{2,1,0:T(8,128)} fusion(s32[2,64,65]{2,1,0:T(8,128)} %param.9, s32[2,64,65]{2,1,0:T(8,128)} %param.8, s32[]{:T(128)S(6)} %sub.173, s32[64]{0:T(128)S(1)} %get-tuple-element.34, s32[64]{0:T(128)S(1)} %get-tuple-element.35, s32[65]{0:T(128)S(1)} %iota_add_fusion.2, s32[64]{0:T(128)S(1)} %get-tuple-element.33, s32[]{:T(128)S(6)} %mul.438, ...), kind=kLoop, calls=%fused_computation.79 | loop fusion | flops 241280 | bytes 105292 | tf_op jit(solution)/shard_map/jit(_where)/select_n | solution.py:69
  13.5 0.6 iota_compare_fusion.2
  14.1 2.2 %collective-permute-done.1 = bf16[8,2,64,10]{3,2,1,0:T(8,128)(2,1)S(1)} collective-permute-done((bf16[8,2,64,10]{3,2,1,0:T(8,128)(2,1)S(1)}, bf16[8,2,64,10]{3,2,1,0:T(8,128)(2,1)S(1)}, u32[]{:S(2)}, u32[]{:S(2)}) %collective-permute-start.1) | collective-permute-done | bytes 20512 | tf_op jit(solution)/shard_map/ppermute | solution.py:24
  16.4 0.9 pad_maximum_fusion.3
  17.3 11.2 %collective-permute-start.3 = (bf16[8,2,1,85]{3,2,1,0:T(2,128)(2,1)S(1)}, bf16[8,2,1,85]{3,2,1,0:T(2,128)(2,1)S(1)}, u32[]{:S(2)}, u32[]{:S(2)}) collective-permute-start(bf16[8,2,1,85]{3,2,1,0:T(2,128)(2,1)S(1)} %get-tuple-element.15), channel_id=1, source_target_pairs={{64,0},{128,64},{192,128},{256,192},{320,256},{384,320},{448,384},... | collective-permute-start | bytes 8168 | tf_op jit(solution)/shard_map/ppermute | solution.py:24
  28.5 1.4 convert_element_type.117.weight_ref
  30.0 1.9 %collective-permute-start.2 = (bf16[8,2,1,85]{3,2,1,0:T(2,128)(2,1)S(1)}, bf16[8,2,1,85]{3,2,1,0:T(2,128)(2,1)S(1)}, u32[]{:S(2)}, u32[]{:S(2)}) collective-permute-start(bf16[8,2,1,85]{3,2,1,0:T(2,128)(2,1)S(1)} %get-tuple-element.14), channel_id=1, source_target_pairs={{0,64},{64,128},{128,192},{192,256},{256,320},{320,384},{384,448},... | collective-permute-start | bytes 8168 | tf_op jit(solution)/shard_map/ppermute | solution.py:23
  32.0 1.1 collective-permute-done.2
  33.1 1.2 maximum_convert_fusion.ext_ref
  34.3 11.0 %shard_map.86 = f32[8,2,64,65]{3,2,1,0:T(8,128)} custom-call(f32[8,2,66,85]{3,2,1,0:T(8,128)} %maximum_convert_fusion.ext_ref, s32[2,64,65]{2,1,0:T(8,128)} %fusion.45.code_ref, f32[2,64,65]{2,1,0:T(8,128)} %convert_element_type.117.weight_ref), custom_call_target="tpu_custom_call" | custom-call | tf_op jit(solution)/shard_map/pallas_call | solution.py:71
  45.3 1.1 select_convert_fusion
  46.4 0.7 broadcast_subtract_fusion
  47.1 0.7 stack.36
  47.8 2.2 %fusion.40 = (f32[32,640,2]{1,0,2:T(8,128)S(1)}, f32[32,640,2]{1,0,2:T(8,128)S(1)}) fusion(f32[]{:T(128)} %bitcast.4, pred[]{:T(512)} %bitcast.3, s32[]{:T(128)} %bitcast.2, s32[640,2]{0,1:T(2,128)S(1)} %pad_add_fusion), kind=kLoop, calls=%fused_computation.74 | loop fusion | flops 450560 | bytes 332809 | tf_op jit(solution)/shard_map/vmap()/cos | solution.py:88
  50.0 2.8 %fusion.33 = (f32[33,640,2]{1,0,2:T(8,128)S(1)}, f32[33,640,2]{1,0,2:T(8,128)S(1)}) fusion(f32[]{:T(128)} %bitcast.4, pred[]{:T(512)} %bitcast.3, s32[]{:T(128)} %bitcast.2, s32[33]{0:T(128)S(1)} %iota_multiply_fusion, s32[640,2]{0,1:T(2,128)S(1)} %pad_add_fusion), kind=kLoop, calls=%fused_computation.65 | loop fusion | flops 464640 | bytes 343181 | tf_op jit(solution)/shard_map/vmap()/cos | solution.py:88
  52.8 1.0 copy.21
  53.8 15.8 %all-to-all-start = ((bf16[8,2,64,65]{3,1,0,2:T(2,128)(2,1)}), bf16[8,2,64,65]{3,1,0,2:T(2,128)(2,1)S(1)}, u32[]{:S(2)}, u32[]{:S(2)}) async-start(bf16[8,2,64,65]{3,1,0,2:T(2,128)(2,1)} %copy.21), calls=%async_computation | async-start | bytes 524288 | tf_op jit(solution)/shard_map/all_to_all | solution.py:214
  69.7 2.0 %multiply_subtract_fusion = (bf16[33,32,640,2]{2,1,0,3:T(8,128)(2,1)S(1)}, bf16[33,32,640,2]{2,1,0,3:T(8,128)(2,1)S(1)}) fusion(f32[32,640,2]{1,0,2:T(8,128)S(1)} %get-tuple-element.27, f32[33,640,2]{1,0,2:T(8,128)S(1)} %get-tuple-element.23, f32[32,640,2]{1,0,2:T(8,128)S(1)} %get-tuple-element.26, f32[33,640,2]{1,0,2:T(8,128)S(1)} %get-tuple-element.22), kind=kLoop, calls=%fused_computation.3 | loop fusion | flops 12165120 | bytes 6072320 | tf_op jit(solution)/shard_map/vmap()/sub | solution.py:105
  71.7 3.3 %fusion.6 = (bf16[1040,640,2,1]{1,0,3,2:T(8,128)(2,1)}, bf16[1040,640,2,1]{1,0,3,2:T(8,128)(2,1)}) fusion(bf16[1,1056,640,2]{2,1,3,0:T(8,128)(2,1)S(1)} %bitcast.81, pred[640,2]{0,1:T(4,128)(4,1)S(1)} %multiply_compare_fusion, pred[1040]{0:T(1024)(128)(4,1)S(1)} %copy-done.3, bf16[1,1056,640,2]{2,1,3,0:T(8,128)(2,1)S(1)} %bitcast.82), kind=kLoop, calls=%fused_computation.11 | loop fusion | flops 3993600 | bytes 10651920 | tf_op jit(solution)/shard_map/vmap()/stack | solution.py:111
  75.0 0.6 fusion.62
  75.6 7.9 %all-to-all-done = bf16[8,2,64,65]{3,1,0,2:T(2,128)(2,1)S(1)} async-done(((bf16[8,2,64,65]{3,1,0,2:T(2,128)(2,1)}), bf16[8,2,64,65]{3,1,0,2:T(2,128)(2,1)S(1)}, u32[]{:S(2)}, u32[]{:S(2)}) %all-to-all-start) | async-done | bytes 133152 | tf_op jit(solution)/shard_map/all_to_all | solution.py:214
  83.4 4.0 %copy.22 = bf16[8,2,64,65]{0,1,3,2:T(2,128)(2,1)} copy(bf16[8,2,64,65]{3,1,0,2:T(2,128)(2,1)S(1)} %all-to-all-done) | data formatting | bytes 266240 | tf_op jit(solution)/shard_map/all_to_all | solution.py:214
  87.4 4.5 %fusion.11 = f32[1,640,2,2,8,2,4]{1,4,6,5,3,2,0:T(8,128)S(1)} fusion(bf16[8,2,1040,4,1,1]{0,1,3,2,5,4:T(2,128)(2,1)} %bitcast.85, bf16[1040,640,2,1]{1,0,3,2:T(8,128)(2,1)} %get-tuple-element.29, bf16[1040,640,2,1]{1,0,3,2:T(8,128)(2,1)} %get-tuple-element.28), kind=kOutput, calls=%fused_computation.20 | convolution fusion | flops 351436800 | bytes 6113280 | tf_op jit(solution)/shard_map/vmap(aser,fhab->serfhb)/dot_general | solution.py:114
  92.0 0.2 copy.25
  92.2 0.5 broadcast.792
  92.8 1.7 reduce.6
  94.4 0.8 reshape.751
  95.2 5.1 %all-to-all-start.1 = ((bf16[64,2,320]{2,1,0:T(2,128)(2,1)}), bf16[64,2,320]{2,1,0:T(2,128)(2,1)S(1)}, u32[]{:S(2)}, u32[]{:S(2)}) async-start(bf16[64,2,320]{2,1,0:T(2,128)(2,1)} %reshape.751), calls=%async_computation.1 | async-start | bytes 196608 | tf_op jit(solution)/shard_map/all_to_all | solution.py:220
  100.5 11.1 %all-to-all-done.1 = bf16[64,2,320]{2,1,0:T(2,128)(2,1)S(1)} async-done(((bf16[64,2,320]{2,1,0:T(2,128)(2,1)}), bf16[64,2,320]{2,1,0:T(2,128)(2,1)S(1)}, u32[]{:S(2)}, u32[]{:S(2)}) %all-to-all-start.1) | async-done | bytes 81952 | tf_op jit(solution)/shard_map/all_to_all | solution.py:220
  111.6 0.2 reshape.752
  111.8 1.0 bitcast_reduce_fusion
  112.8 0.7 fusion.26
  113.6 0.2 fusion.8
  113.9 0.3 copy.28
  114.2 0.3 copy.29
  114.6 1.0 fusion.10
  115.6 10.2 %all-to-all-start.2 = ((bf16[16,10,1281]{2,1,0:T(8,128)(2,1)}), bf16[16,10,1281]{2,1,0:T(8,128)(2,1)S(1)}, u32[]{:S(2)}, u32[]{:S(2)}) async-start(bf16[16,10,1281]{2,1,0:T(8,128)(2,1)} %bitcast.30), calls=%async_computation.2 | async-start | bytes 1441792 | tf_op jit(solution)/shard_map/all_to_all | solution.py:132
  126.0 21.1 %all-to-all-done.2 = bf16[16,10,1281]{2,1,0:T(8,128)(2,1)S(1)} async-done(((bf16[16,10,1281]{2,1,0:T(8,128)(2,1)}), bf16[16,10,1281]{2,1,0:T(8,128)(2,1)S(1)}, u32[]{:S(2)}, u32[]{:S(2)}) %all-to-all-start.2) | async-done | bytes 409952 | tf_op jit(solution)/shard_map/all_to_all | solution.py:132
  147.3 18.8 %all-gather.1 = f32[16,10,1281]{2,1,0:T(8,128)S(1)} all-gather(f32[1,10,1281]{2,1,0:T(8,128)S(1)} %bitcast.87), channel_id=2, replica_groups=mesh['lat'=16,'lon'=64] {'lat'}, dimensions={0}, use_global_device_ids=true | all-gather | bytes 871080 | tf_op jit(solution)/shard_map/all_gather | solution.py:135
  166.0 1.3 fusion.65
  167.3 0.3 broadcast_multiply_fusion
  167.5 1.4 fusion.14
  (33 shorter events, 1.3 us)
Async XLA Ops:
  0.6 112.2 %copy-start = (bf16[64,10,1281]{2,0,1:T(8,128)(2,1)S(1)}, bf16[64,10,1281]{2,0,1:T(8,128)(2,1)}, u32[]{:S(2)}) copy-start(bf16[64,10,1281]{2,0,1:T(8,128)(2,1)} %param.12) | copy-start | bytes 4919044
  0.6 32.5 %copy-start.1 = (bf16[8,2,64,65]{3,2,1,0:T(8,128)(2,1)S(1)}, bf16[8,2,64,65]{3,2,1,0:T(8,128)(2,1)}, u32[]{:S(2)}) copy-start(bf16[8,2,64,65]{3,2,1,0:T(8,128)(2,1)} %param.7) | copy-start | bytes 399364
  2.0 12.2 %collective-permute-start = (bf16[8,2,64,10]{3,2,1,0:T(8,128)(2,1)S(1)}, bf16[8,2,64,10]{3,2,1,0:T(8,128)(2,1)S(1)}, u32[]{:S(2)}, u32[]{:S(2)}) collective-permute-start(bf16[8,2,64,10]{3,2,1,0:T(8,128)(2,1)S(1)} %get-tuple-element.18), channel_id=1, source_target_pairs={{0,1},{1,2},{2,3},{3,4},{4,5},{5,6},{6,7},{7,8},{8,9},{9,10},{10,1... | collective-permute-start | bytes 61448 | tf_op jit(solution)/shard_map/ppermute | solution.py:23
  7.7 8.7 %collective-permute-start.1 = (bf16[8,2,64,10]{3,2,1,0:T(8,128)(2,1)S(1)}, bf16[8,2,64,10]{3,2,1,0:T(8,128)(2,1)S(1)}, u32[]{:S(2)}, u32[]{:S(2)}) collective-permute-start(bf16[8,2,64,10]{3,2,1,0:T(8,128)(2,1)S(1)} %get-tuple-element.19), channel_id=1, source_target_pairs={{1,0},{2,1},{3,2},{4,3},{5,4},{6,5},{7,6},{8,7},{9,8},{10,9},{11,1... | collective-permute-start | bytes 61448 | tf_op jit(solution)/shard_map/ppermute | solution.py:24
  17.3 14.7 %collective-permute-start.3 = (bf16[8,2,1,85]{3,2,1,0:T(2,128)(2,1)S(1)}, bf16[8,2,1,85]{3,2,1,0:T(2,128)(2,1)S(1)}, u32[]{:S(2)}, u32[]{:S(2)}) collective-permute-start(bf16[8,2,1,85]{3,2,1,0:T(2,128)(2,1)S(1)} %get-tuple-element.15), channel_id=1, source_target_pairs={{64,0},{128,64},{192,128},{256,192},{320,256},{384,320},{448,384},... | collective-permute-start | bytes 8168 | tf_op jit(solution)/shard_map/ppermute | solution.py:24
  30.0 3.1 %collective-permute-start.2 = (bf16[8,2,1,85]{3,2,1,0:T(2,128)(2,1)S(1)}, bf16[8,2,1,85]{3,2,1,0:T(2,128)(2,1)S(1)}, u32[]{:S(2)}, u32[]{:S(2)}) collective-permute-start(bf16[8,2,1,85]{3,2,1,0:T(2,128)(2,1)S(1)} %get-tuple-element.14), channel_id=1, source_target_pairs={{0,64},{64,128},{128,192},{192,256},{256,320},{320,384},{384,448},... | collective-permute-start | bytes 8168 | tf_op jit(solution)/shard_map/ppermute | solution.py:23
  53.8 29.6 %all-to-all-start = ((bf16[8,2,64,65]{3,1,0,2:T(2,128)(2,1)}), bf16[8,2,64,65]{3,1,0,2:T(2,128)(2,1)S(1)}, u32[]{:S(2)}, u32[]{:S(2)}) async-start(bf16[8,2,64,65]{3,1,0,2:T(2,128)(2,1)} %copy.21), calls=%async_computation | async-start | bytes 524288 | tf_op jit(solution)/shard_map/all_to_all | solution.py:214
  69.6 2.1 %copy-start.3 = (pred[1040]{0:T(1024)(128)(4,1)S(1)}, pred[1040]{0:T(1024)(128)(4,1)}, u32[]{:S(2)}) copy-start(pred[1040]{0:T(1024)(128)(4,1)} %iota_compare_fusion.2) | copy-start | bytes 3124
  95.2 16.4 %all-to-all-start.1 = ((bf16[64,2,320]{2,1,0:T(2,128)(2,1)}), bf16[64,2,320]{2,1,0:T(2,128)(2,1)S(1)}, u32[]{:S(2)}, u32[]{:S(2)}) async-start(bf16[64,2,320]{2,1,0:T(2,128)(2,1)} %reshape.751), calls=%async_computation.1 | async-start | bytes 196608 | tf_op jit(solution)/shard_map/all_to_all | solution.py:220
  112.8 0.7 copy-start.2
  114.5 11.4 %copy-start.4 = (f32[8]{0:T(128)S(1)}, f32[8]{0:T(128)}, u32[]{:S(2)}) copy-start(f32[8]{0:T(128)} %param.13) | copy-start | bytes 100
  115.6 31.5 %all-to-all-start.2 = ((bf16[16,10,1281]{2,1,0:T(8,128)(2,1)}), bf16[16,10,1281]{2,1,0:T(8,128)(2,1)S(1)}, u32[]{:S(2)}, u32[]{:S(2)}) async-start(bf16[16,10,1281]{2,1,0:T(8,128)(2,1)} %bitcast.30), calls=%async_computation.2 | async-start | bytes 1441792 | tf_op jit(solution)/shard_map/all_to_all | solution.py:132

commit v7 on v6

--- a/solution.py
+++ b/solution.py
@@ -39,8 +39,9 @@
     rows, cols = code.shape[1], code.shape[2]
     left = jnp.zeros(code.shape, jnp.float32)
     right = left
+    reach = ((WL - 8, WL + 6), (WL - 5, WL + 6), (WL - 5, WL + 9))
     for dr in range(ext_ref.shape[2] - rows + 1):
-        for dc in range(1, ext_ref.shape[3] - cols - 1):
+        for dc in range(*reach[dr]):
             window = ext_ref[0, :, dr : dr + rows, dc : dc + cols]
             key = dr * 64 + dc
             left = jnp.where(code == key, window, left)

time: 170 us -> 168 us (0.988)
  Pallas kernels: 11 us -> 8.64 us
    pallas_call x1, Pallas kernels: 11 us -> 8.64 us  [depart_values(): pl.pallas_call(depart_kernel, grid=(field_count,), in_specs=[pl.BlockSpec...]
where the time goes in v7:
time: 168 us; the launch traced here: 167 us
  starting transfers between devices  51.3 us (31%)
  waiting for transfers between devices  43.5 us (26%)
  other arithmetic  26.2 us (16%)
  blocking collectives  18.8 us (11%)
  local copies, waits for them, and re-layouts  10.6 us (6%)
  Pallas kernels  8.64 us (5%)
  matrix products  6.5 us (4%)
    all_to_all x1, waiting for transfers between devices, lat_sum(): lax.all_to_all(grouped.astype(jnp.bfloat16), 'lat', 0, 0, tiled=True)  21.1 us
    all_gather x1, blocking collectives, lat_sum(): whole = lax.all_gather(reduced, 'lat', axis=0, tiled=True)  18.8 us
    all_to_all x1, starting transfers between devices, on_device(): lax.all_to_all(advected, 'lon', split_axis=2, concat_axis=3, tiled=True)  15.8 us
    ppermute x2, starting transfers between devices, extended_2(): after = lax.ppermute(initial, axis, down)  12.5 us
    all_to_all x1, waiting for transfers between devices, on_device(): lax.all_to_all(shortened(spectra), 'lon', split_axis=1, concat_axis=0, ti...  11.1 us
    all_to_all x1, starting transfers between devices, lat_sum(): lax.all_to_all(grouped.astype(jnp.bfloat16), 'lat', 0, 0, tiled=True)  10.2 us
    pallas_call x1, Pallas kernels, depart_values(): pl.pallas_call(depart_kernel, grid=(field_count,), in_specs=[pl.BlockSpec...  8.64 us
    all_to_all x1, waiting for transfers between devices, on_device(): lax.all_to_all(advected, 'lon', split_axis=2, concat_axis=3, tiled=True)  7.85 us
  transfers between devices with their start and end apart: 7, of which 5 were waited for; matrix products, arithmetic and copies ran while one was open for 8% of the time, Pallas kernels for 0%

profile of v7, /device:TPU:1, one launch (start us, length us, event | category | flops | bytes accessed | tf_op | source)
XLA Modules:
  0.0 166.5 jit_solution(2965563274092047245)
XLA Ops:
  0.7 1.3 fusion.67
  2.0 5.7 %collective-permute-start = (bf16[8,2,64,10]{3,2,1,0:T(8,128)(2,1)S(1)}, bf16[8,2,64,10]{3,2,1,0:T(8,128)(2,1)S(1)}, u32[]{:S(2)}, u32[]{:S(2)}) collective-permute-start(bf16[8,2,64,10]{3,2,1,0:T(8,128)(2,1)S(1)} %get-tuple-element.18), channel_id=1, source_target_pairs={{0,1},{1,2},{2,3},{3,4},{4,5},{5,6},{6,7},{7,8},{8,9},{9,10},{10,1... | collective-permute-start | bytes 61448 | tf_op jit(solution)/shard_map/ppermute | solution.py:23
  7.7 1.3 collective-permute-start.1
  9.1 0.8 broadcast_subtract_fusion.1
  9.8 0.7 iota_compare_fusion
  10.7 0.3 fusion.50
  11.2 2.3 %fusion.45.code_ref = s32[2,64,65]{2,1,0:T(8,128)} fusion(s32[2,64,65]{2,1,0:T(8,128)} %param.9, s32[2,64,65]{2,1,0:T(8,128)} %param.8, s32[]{:T(128)S(6)} %sub.173, s32[64]{0:T(128)S(1)} %get-tuple-element.34, s32[64]{0:T(128)S(1)} %get-tuple-element.35, s32[65]{0:T(128)S(1)} %iota_add_fusion.2, s32[64]{0:T(128)S(1)} %get-tuple-element.33, s32[]{:T(128)S(6)} %mul.438, ...), kind=kLoop, calls=%fused_computation.79 | loop fusion | flops 241280 | bytes 105292 | tf_op jit(solution)/shard_map/jit(_where)/select_n | solution.py:70
  13.5 0.6 iota_compare_fusion.2
  14.1 2.2 %collective-permute-done.1 = bf16[8,2,64,10]{3,2,1,0:T(8,128)(2,1)S(1)} collective-permute-done((bf16[8,2,64,10]{3,2,1,0:T(8,128)(2,1)S(1)}, bf16[8,2,64,10]{3,2,1,0:T(8,128)(2,1)S(1)}, u32[]{:S(2)}, u32[]{:S(2)}) %collective-permute-start.1) | collective-permute-done | bytes 20512 | tf_op jit(solution)/shard_map/ppermute | solution.py:24
  16.4 0.9 pad_maximum_fusion.3
  17.3 11.2 %collective-permute-start.3 = (bf16[8,2,1,85]{3,2,1,0:T(2,128)(2,1)S(1)}, bf16[8,2,1,85]{3,2,1,0:T(2,128)(2,1)S(1)}, u32[]{:S(2)}, u32[]{:S(2)}) collective-permute-start(bf16[8,2,1,85]{3,2,1,0:T(2,128)(2,1)S(1)} %get-tuple-element.15), channel_id=1, source_target_pairs={{64,0},{128,64},{192,128},{256,192},{320,256},{384,320},{448,384},... | collective-permute-start | bytes 8168 | tf_op jit(solution)/shard_map/ppermute | solution.py:24
  28.5 1.4 convert_element_type.117.weight_ref
  30.0 1.9 %collective-permute-start.2 = (bf16[8,2,1,85]{3,2,1,0:T(2,128)(2,1)S(1)}, bf16[8,2,1,85]{3,2,1,0:T(2,128)(2,1)S(1)}, u32[]{:S(2)}, u32[]{:S(2)}) collective-permute-start(bf16[8,2,1,85]{3,2,1,0:T(2,128)(2,1)S(1)} %get-tuple-element.14), channel_id=1, source_target_pairs={{0,64},{64,128},{128,192},{192,256},{256,320},{320,384},{384,448},... | collective-permute-start | bytes 8168 | tf_op jit(solution)/shard_map/ppermute | solution.py:23
  32.0 1.1 collective-permute-done.2
  33.1 1.2 maximum_convert_fusion.ext_ref
  34.3 8.6 %shard_map.86 = f32[8,2,64,65]{3,2,1,0:T(8,128)} custom-call(f32[8,2,66,85]{3,2,1,0:T(8,128)} %maximum_convert_fusion.ext_ref, s32[2,64,65]{2,1,0:T(8,128)} %fusion.45.code_ref, f32[2,64,65]{2,1,0:T(8,128)} %convert_element_type.117.weight_ref), custom_call_target="tpu_custom_call" | custom-call | tf_op jit(solution)/shard_map/pallas_call | solution.py:72
  42.9 1.1 select_convert_fusion
  44.0 0.7 broadcast_subtract_fusion
  44.7 0.7 stack.36
  45.5 2.2 %fusion.40 = (f32[32,640,2]{1,0,2:T(8,128)S(1)}, f32[32,640,2]{1,0,2:T(8,128)S(1)}) fusion(f32[]{:T(128)} %bitcast.4, pred[]{:T(512)} %bitcast.3, s32[]{:T(128)} %bitcast.2, s32[640,2]{0,1:T(2,128)S(1)} %pad_add_fusion), kind=kLoop, calls=%fused_computation.74 | loop fusion | flops 450560 | bytes 332809 | tf_op jit(solution)/shard_map/vmap()/cos | solution.py:89
  47.7 2.8 %fusion.33 = (f32[33,640,2]{1,0,2:T(8,128)S(1)}, f32[33,640,2]{1,0,2:T(8,128)S(1)}) fusion(f32[]{:T(128)} %bitcast.4, pred[]{:T(512)} %bitcast.3, s32[]{:T(128)} %bitcast.2, s32[33]{0:T(128)S(1)} %iota_multiply_fusion, s32[640,2]{0,1:T(2,128)S(1)} %pad_add_fusion), kind=kLoop, calls=%fused_computation.65 | loop fusion | flops 464640 | bytes 343181 | tf_op jit(solution)/shard_map/vmap()/cos | solution.py:89
  50.5 1.0 copy.21
  51.5 15.8 %all-to-all-start = ((bf16[8,2,64,65]{3,1,0,2:T(2,128)(2,1)}), bf16[8,2,64,65]{3,1,0,2:T(2,128)(2,1)S(1)}, u32[]{:S(2)}, u32[]{:S(2)}) async-start(bf16[8,2,64,65]{3,1,0,2:T(2,128)(2,1)} %copy.21), calls=%async_computation | async-start | bytes 524288 | tf_op jit(solution)/shard_map/all_to_all | solution.py:215
  67.3 2.0 %multiply_subtract_fusion = (bf16[33,32,640,2]{2,1,0,3:T(8,128)(2,1)S(1)}, bf16[33,32,640,2]{2,1,0,3:T(8,128)(2,1)S(1)}) fusion(f32[32,640,2]{1,0,2:T(8,128)S(1)} %get-tuple-element.27, f32[33,640,2]{1,0,2:T(8,128)S(1)} %get-tuple-element.23, f32[32,640,2]{1,0,2:T(8,128)S(1)} %get-tuple-element.26, f32[33,640,2]{1,0,2:T(8,128)S(1)} %get-tuple-element.22), kind=kLoop, calls=%fused_computation.3 | loop fusion | flops 12165120 | bytes 6072320 | tf_op jit(solution)/shard_map/vmap()/sub | solution.py:106
  69.3 3.3 %fusion.6 = (bf16[1040,640,2,1]{1,0,3,2:T(8,128)(2,1)}, bf16[1040,640,2,1]{1,0,3,2:T(8,128)(2,1)}) fusion(bf16[1,1056,640,2]{2,1,3,0:T(8,128)(2,1)S(1)} %bitcast.81, pred[640,2]{0,1:T(4,128)(4,1)S(1)} %multiply_compare_fusion, pred[1040]{0:T(1024)(128)(4,1)S(1)} %copy-done.3, bf16[1,1056,640,2]{2,1,3,0:T(8,128)(2,1)S(1)} %bitcast.82), kind=kLoop, calls=%fused_computation.11 | loop fusion | flops 3993600 | bytes 10651920 | tf_op jit(solution)/shard_map/vmap()/stack | solution.py:112
  72.6 0.6 fusion.62
  73.2 7.9 %all-to-all-done = bf16[8,2,64,65]{3,1,0,2:T(2,128)(2,1)S(1)} async-done(((bf16[8,2,64,65]{3,1,0,2:T(2,128)(2,1)}), bf16[8,2,64,65]{3,1,0,2:T(2,128)(2,1)S(1)}, u32[]{:S(2)}, u32[]{:S(2)}) %all-to-all-start) | async-done | bytes 133152 | tf_op jit(solution)/shard_map/all_to_all | solution.py:215
  81.1 4.0 %copy.22 = bf16[8,2,64,65]{0,1,3,2:T(2,128)(2,1)} copy(bf16[8,2,64,65]{3,1,0,2:T(2,128)(2,1)S(1)} %all-to-all-done) | data formatting | bytes 266240 | tf_op jit(solution)/shard_map/all_to_all | solution.py:215
  85.1 4.4 %fusion.11 = f32[1,640,2,2,8,2,4]{1,4,6,5,3,2,0:T(8,128)S(1)} fusion(bf16[8,2,1040,4,1,1]{0,1,3,2,5,4:T(2,128)(2,1)} %bitcast.85, bf16[1040,640,2,1]{1,0,3,2:T(8,128)(2,1)} %get-tuple-element.29, bf16[1040,640,2,1]{1,0,3,2:T(8,128)(2,1)} %get-tuple-element.28), kind=kOutput, calls=%fused_computation.20 | convolution fusion | flops 351436800 | bytes 6113280 | tf_op jit(solution)/shard_map/vmap(aser,fhab->serfhb)/dot_general | solution.py:115
  89.7 0.2 copy.25
  89.9 0.5 broadcast.792
  90.4 1.7 reduce.6
  92.0 0.8 reshape.751
  92.9 5.1 %all-to-all-start.1 = ((bf16[64,2,320]{2,1,0:T(2,128)(2,1)}), bf16[64,2,320]{2,1,0:T(2,128)(2,1)S(1)}, u32[]{:S(2)}, u32[]{:S(2)}) async-start(bf16[64,2,320]{2,1,0:T(2,128)(2,1)} %reshape.751), calls=%async_computation.1 | async-start | bytes 196608 | tf_op jit(solution)/shard_map/all_to_all | solution.py:221
  98.1 11.1 %all-to-all-done.1 = bf16[64,2,320]{2,1,0:T(2,128)(2,1)S(1)} async-done(((bf16[64,2,320]{2,1,0:T(2,128)(2,1)}), bf16[64,2,320]{2,1,0:T(2,128)(2,1)S(1)}, u32[]{:S(2)}, u32[]{:S(2)}) %all-to-all-start.1) | async-done | bytes 81952 | tf_op jit(solution)/shard_map/all_to_all | solution.py:221
  109.2 0.2 reshape.752
  109.4 1.0 bitcast_reduce_fusion
  110.5 0.7 fusion.26
  111.2 0.2 fusion.8
  111.5 0.3 copy.28
  111.9 0.3 copy.29
  112.2 1.0 fusion.10
  113.2 10.2 %all-to-all-start.2 = ((bf16[16,10,1281]{2,1,0:T(8,128)(2,1)}), bf16[16,10,1281]{2,1,0:T(8,128)(2,1)S(1)}, u32[]{:S(2)}, u32[]{:S(2)}) async-start(bf16[16,10,1281]{2,1,0:T(8,128)(2,1)} %bitcast.30), calls=%async_computation.2 | async-start | bytes 1441792 | tf_op jit(solution)/shard_map/all_to_all | solution.py:133
  123.6 21.1 %all-to-all-done.2 = bf16[16,10,1281]{2,1,0:T(8,128)(2,1)S(1)} async-done(((bf16[16,10,1281]{2,1,0:T(8,128)(2,1)}), bf16[16,10,1281]{2,1,0:T(8,128)(2,1)S(1)}, u32[]{:S(2)}, u32[]{:S(2)}) %all-to-all-start.2) | async-done | bytes 409952 | tf_op jit(solution)/shard_map/all_to_all | solution.py:133
  144.9 18.8 %all-gather.1 = f32[16,10,1281]{2,1,0:T(8,128)S(1)} all-gather(f32[1,10,1281]{2,1,0:T(8,128)S(1)} %bitcast.87), channel_id=2, replica_groups=mesh['lat'=16,'lon'=64] {'lat'}, dimensions={0}, use_global_device_ids=true | all-gather | bytes 871080 | tf_op jit(solution)/shard_map/all_gather | solution.py:136
  163.7 1.3 fusion.65
  164.9 0.3 broadcast_multiply_fusion
  165.2 1.4 fusion.14
  (33 shorter events, 1.3 us)
Async XLA Ops:
  0.6 109.8 %copy-start = (bf16[64,10,1281]{2,0,1:T(8,128)(2,1)S(1)}, bf16[64,10,1281]{2,0,1:T(8,128)(2,1)}, u32[]{:S(2)}) copy-start(bf16[64,10,1281]{2,0,1:T(8,128)(2,1)} %param.12) | copy-start | bytes 4919044
  0.6 32.5 %copy-start.1 = (bf16[8,2,64,65]{3,2,1,0:T(8,128)(2,1)S(1)}, bf16[8,2,64,65]{3,2,1,0:T(8,128)(2,1)}, u32[]{:S(2)}) copy-start(bf16[8,2,64,65]{3,2,1,0:T(8,128)(2,1)} %param.7) | copy-start | bytes 399364
  2.0 12.2 %collective-permute-start = (bf16[8,2,64,10]{3,2,1,0:T(8,128)(2,1)S(1)}, bf16[8,2,64,10]{3,2,1,0:T(8,128)(2,1)S(1)}, u32[]{:S(2)}, u32[]{:S(2)}) collective-permute-start(bf16[8,2,64,10]{3,2,1,0:T(8,128)(2,1)S(1)} %get-tuple-element.18), channel_id=1, source_target_pairs={{0,1},{1,2},{2,3},{3,4},{4,5},{5,6},{6,7},{7,8},{8,9},{9,10},{10,1... | collective-permute-start | bytes 61448 | tf_op jit(solution)/shard_map/ppermute | solution.py:23
  7.7 8.7 %collective-permute-start.1 = (bf16[8,2,64,10]{3,2,1,0:T(8,128)(2,1)S(1)}, bf16[8,2,64,10]{3,2,1,0:T(8,128)(2,1)S(1)}, u32[]{:S(2)}, u32[]{:S(2)}) collective-permute-start(bf16[8,2,64,10]{3,2,1,0:T(8,128)(2,1)S(1)} %get-tuple-element.19), channel_id=1, source_target_pairs={{1,0},{2,1},{3,2},{4,3},{5,4},{6,5},{7,6},{8,7},{9,8},{10,9},{11,1... | collective-permute-start | bytes 61448 | tf_op jit(solution)/shard_map/ppermute | solution.py:24
  17.3 14.7 %collective-permute-start.3 = (bf16[8,2,1,85]{3,2,1,0:T(2,128)(2,1)S(1)}, bf16[8,2,1,85]{3,2,1,0:T(2,128)(2,1)S(1)}, u32[]{:S(2)}, u32[]{:S(2)}) collective-permute-start(bf16[8,2,1,85]{3,2,1,0:T(2,128)(2,1)S(1)} %get-tuple-element.15), channel_id=1, source_target_pairs={{64,0},{128,64},{192,128},{256,192},{320,256},{384,320},{448,384},... | collective-permute-start | bytes 8168 | tf_op jit(solution)/shard_map/ppermute | solution.py:24
  30.0 3.1 %collective-permute-start.2 = (bf16[8,2,1,85]{3,2,1,0:T(2,128)(2,1)S(1)}, bf16[8,2,1,85]{3,2,1,0:T(2,128)(2,1)S(1)}, u32[]{:S(2)}, u32[]{:S(2)}) collective-permute-start(bf16[8,2,1,85]{3,2,1,0:T(2,128)(2,1)S(1)} %get-tuple-element.14), channel_id=1, source_target_pairs={{0,64},{64,128},{128,192},{192,256},{256,320},{320,384},{384,448},... | collective-permute-start | bytes 8168 | tf_op jit(solution)/shard_map/ppermute | solution.py:23
  51.5 29.6 %all-to-all-start = ((bf16[8,2,64,65]{3,1,0,2:T(2,128)(2,1)}), bf16[8,2,64,65]{3,1,0,2:T(2,128)(2,1)S(1)}, u32[]{:S(2)}, u32[]{:S(2)}) async-start(bf16[8,2,64,65]{3,1,0,2:T(2,128)(2,1)} %copy.21), calls=%async_computation | async-start | bytes 524288 | tf_op jit(solution)/shard_map/all_to_all | solution.py:215
  67.3 2.1 %copy-start.3 = (pred[1040]{0:T(1024)(128)(4,1)S(1)}, pred[1040]{0:T(1024)(128)(4,1)}, u32[]{:S(2)}) copy-start(pred[1040]{0:T(1024)(128)(4,1)} %iota_compare_fusion.2) | copy-start | bytes 3124
  92.9 16.4 %all-to-all-start.1 = ((bf16[64,2,320]{2,1,0:T(2,128)(2,1)}), bf16[64,2,320]{2,1,0:T(2,128)(2,1)S(1)}, u32[]{:S(2)}, u32[]{:S(2)}) async-start(bf16[64,2,320]{2,1,0:T(2,128)(2,1)} %reshape.751), calls=%async_computation.1 | async-start | bytes 196608 | tf_op jit(solution)/shard_map/all_to_all | solution.py:221
  110.5 0.7 copy-start.2
  112.2 11.3 %copy-start.4 = (f32[8]{0:T(128)S(1)}, f32[8]{0:T(128)}, u32[]{:S(2)}) copy-start(f32[8]{0:T(128)} %param.13) | copy-start | bytes 100
  113.2 31.5 %all-to-all-start.2 = ((bf16[16,10,1281]{2,1,0:T(8,128)(2,1)}), bf16[16,10,1281]{2,1,0:T(8,128)(2,1)S(1)}, u32[]{:S(2)}, u32[]{:S(2)}) async-start(bf16[16,10,1281]{2,1,0:T(8,128)(2,1)} %bitcast.30), calls=%async_computation.2 | async-start | bytes 1441792 | tf_op jit(solution)/shard_map/all_to_all | solution.py:133

commit v8 on v7

--- a/solution.py
+++ b/solution.py
@@ -46,7 +46,7 @@
             key = dr * 64 + dc
             left = jnp.where(code == key, window, left)
             right = jnp.where(code == key - 1, window, right)
-    blend = weight_ref[...]
+    blend = weight_ref[...].astype(jnp.float32)
     out_ref[0] = (1.0 - blend) * left + blend * right
 
 
@@ -79,12 +79,16 @@
         ],
         out_specs=pl.BlockSpec((1,) + code.shape, lambda f: (f, 0, 0, 0)),
         out_shape=jax.ShapeDtypeStruct((field_count,) + code.shape, jnp.float32),
-    )(extended.astype(jnp.float32), code, lon_weight.astype(jnp.float32))
+    )(extended.astype(jnp.float32), code, lon_weight)
     return jnp.where(lon_index < length, blended, 0.0).astype(jnp.bfloat16)
 
 
 def phase_table(orders, steps, quarter_len):
-    phase_idx = orders[None] * steps[:, None, None] % quarter_len
+    product = orders[None] * steps[:, None, None]
+    whole = jnp.floor(product.astype(jnp.float32) / quarter_len.astype(jnp.float32))
+    phase_idx = product - whole.astype(jnp.int32) * quarter_len
+    phase_idx = jnp.where(phase_idx < 0, phase_idx + quarter_len, phase_idx)
+    phase_idx = jnp.where(phase_idx >= quarter_len, phase_idx - quarter_len, phase_idx)
     angles = phase_idx.astype(jnp.float32) * (2.0 * math.pi) / quarter_len.astype(jnp.float32)
     return jnp.cos(angles), jnp.sin(angles)
 

time: 168 us -> 163 us (0.970)
  other arithmetic: 26.2 us -> 21.4 us
    cos x2, other arithmetic: 5.02 us -> 1.57 us  [phase_table(): return (jnp.cos(angles), jnp.sin(angles))]
  transfers between devices with their start and end apart: 7 -> 7, of which waited for: 5 -> 5; matrix products, arithmetic and copies ran while one was open for 8% -> 7% of each run, Pallas kernels for 0% -> 0%
where the time goes in v8:
time: 163 us; the launch traced here: 162 us
  starting transfers between devices  51.3 us (31%)
  waiting for transfers between devices  43.5 us (27%)
  other arithmetic  21.4 us (13%)
  blocking collectives  18.8 us (12%)
  local copies, waits for them, and re-layouts  10.6 us (7%)
  Pallas kernels  8.63 us (5%)
  matrix products  6.5 us (4%)
    all_to_all x1, waiting for transfers between devices, lat_sum(): lax.all_to_all(grouped.astype(jnp.bfloat16), 'lat', 0, 0, tiled=True)  21.1 us
    all_gather x1, blocking collectives, lat_sum(): whole = lax.all_gather(reduced, 'lat', axis=0, tiled=True)  18.8 us
    all_to_all x1, starting transfers between devices, on_device(): lax.all_to_all(advected, 'lon', split_axis=2, concat_axis=3, tiled=True)  15.8 us
    ppermute x2, starting transfers between devices, extended_2(): after = lax.ppermute(initial, axis, down)  12.5 us
    all_to_all x1, waiting for transfers between devices, on_device(): lax.all_to_all(shortened(spectra), 'lon', split_axis=1, concat_axis=0, ti...  11.1 us
    all_to_all x1, starting transfers between devices, lat_sum(): lax.all_to_all(grouped.astype(jnp.bfloat16), 'lat', 0, 0, tiled=True)  10.2 us
    pallas_call x1, Pallas kernels, depart_values(): pl.pallas_call(depart_kernel, grid=(field_count,), in_specs=[pl.BlockSpec...  8.63 us
    all_to_all x1, waiting for transfers between devices, on_device(): lax.all_to_all(advected, 'lon', split_axis=2, concat_axis=3, tiled=True)  7.85 us
  transfers between devices with their start and end apart: 7, of which 5 were waited for; matrix products, arithmetic and copies ran while one was open for 7% of the time, Pallas kernels for 0%

profile of v8, /device:TPU:1, one launch (start us, length us, event | category | flops | bytes accessed | tf_op | source)
XLA Modules:
  0.0 161.7 jit_solution(3079558253599917472)
XLA Ops:
  0.7 1.3 fusion.63
  2.0 5.7 %collective-permute-start = (bf16[8,2,64,10]{3,2,1,0:T(8,128)(2,1)S(1)}, bf16[8,2,64,10]{3,2,1,0:T(8,128)(2,1)S(1)}, u32[]{:S(2)}, u32[]{:S(2)}) collective-permute-start(bf16[8,2,64,10]{3,2,1,0:T(8,128)(2,1)S(1)} %get-tuple-element.18), channel_id=1, source_target_pairs={{0,1},{1,2},{2,3},{3,4},{4,5},{5,6},{6,7},{7,8},{8,9},{9,10},{10,1... | collective-permute-start | bytes 61448 | tf_op jit(solution)/shard_map/ppermute | solution.py:23
  7.7 1.3 collective-permute-start.1
  9.1 0.8 broadcast_subtract_fusion.1
  9.8 0.7 iota_compare_fusion
  10.7 0.3 fusion.46
  11.0 0.1 fusion.33
  11.2 2.3 %fusion.41.code_ref = s32[2,64,65]{2,1,0:T(8,128)} fusion(s32[2,64,65]{2,1,0:T(8,128)} %param.9, s32[2,64,65]{2,1,0:T(8,128)} %param.8, s32[]{:T(128)S(6)} %sub.231, s32[64]{0:T(128)S(1)} %get-tuple-element.34, s32[64]{0:T(128)S(1)} %get-tuple-element.35, s32[65]{0:T(128)S(1)} %iota_add_fusion.2, s32[64]{0:T(128)S(1)} %get-tuple-element.33, s32[]{:T(128)S(6)} %mul.474, ...), kind=kLoop, calls=%fused_computation.77 | loop fusion | flops 241280 | bytes 105292 | tf_op jit(solution)/shard_map/jit(_where)/select_n | solution.py:70
  13.5 0.6 iota_compare_fusion.2
  14.1 2.2 %collective-permute-done.1 = bf16[8,2,64,10]{3,2,1,0:T(8,128)(2,1)S(1)} collective-permute-done((bf16[8,2,64,10]{3,2,1,0:T(8,128)(2,1)S(1)}, bf16[8,2,64,10]{3,2,1,0:T(8,128)(2,1)S(1)}, u32[]{:S(2)}, u32[]{:S(2)}) %collective-permute-start.1) | collective-permute-done | bytes 20512 | tf_op jit(solution)/shard_map/ppermute | solution.py:24
  16.4 0.9 pad_maximum_fusion.3
  17.3 11.2 %collective-permute-start.3 = (bf16[8,2,1,85]{3,2,1,0:T(2,128)(2,1)S(1)}, bf16[8,2,1,85]{3,2,1,0:T(2,128)(2,1)S(1)}, u32[]{:S(2)}, u32[]{:S(2)}) collective-permute-start(bf16[8,2,1,85]{3,2,1,0:T(2,128)(2,1)S(1)} %get-tuple-element.15), channel_id=1, source_target_pairs={{64,0},{128,64},{192,128},{256,192},{320,256},{384,320},{448,384},... | collective-permute-start | bytes 8168 | tf_op jit(solution)/shard_map/ppermute | solution.py:24
  28.6 1.9 %collective-permute-start.2 = (bf16[8,2,1,85]{3,2,1,0:T(2,128)(2,1)S(1)}, bf16[8,2,1,85]{3,2,1,0:T(2,128)(2,1)S(1)}, u32[]{:S(2)}, u32[]{:S(2)}) collective-permute-start(bf16[8,2,1,85]{3,2,1,0:T(2,128)(2,1)S(1)} %get-tuple-element.14), channel_id=1, source_target_pairs={{0,64},{64,128},{128,192},{192,256},{256,320},{320,384},{384,448},... | collective-permute-start | bytes 8168 | tf_op jit(solution)/shard_map/ppermute | solution.py:23
  30.6 1.1 collective-permute-done.2
  31.7 1.2 maximum_convert_fusion.ext_ref
  32.9 8.6 %shard_map.86 = f32[8,2,64,65]{3,2,1,0:T(8,128)} custom-call(f32[8,2,66,85]{3,2,1,0:T(8,128)} %maximum_convert_fusion.ext_ref, s32[2,64,65]{2,1,0:T(8,128)} %fusion.41.code_ref, bf16[2,64,65]{2,1,0:T(8,128)(2,1)} %weight_ref.1), custom_call_target="tpu_custom_call" | custom-call | tf_op jit(solution)/shard_map/pallas_call | solution.py:72
  41.5 1.1 select_convert_fusion
  42.6 0.7 broadcast_subtract_fusion
  43.3 0.7 stack.36
  44.0 0.7 fusion.36
  44.7 0.9 fusion.29
  45.6 1.0 copy.21
  46.6 15.8 %all-to-all-start = ((bf16[8,2,64,65]{3,1,0,2:T(2,128)(2,1)}), bf16[8,2,64,65]{3,1,0,2:T(2,128)(2,1)S(1)}, u32[]{:S(2)}, u32[]{:S(2)}) async-start(bf16[8,2,64,65]{3,1,0,2:T(2,128)(2,1)} %copy.21), calls=%async_computation | async-start | bytes 524288 | tf_op jit(solution)/shard_map/all_to_all | solution.py:219
  62.4 2.0 %multiply_subtract_fusion = (bf16[33,32,640,2]{2,1,0,3:T(8,128)(2,1)S(1)}, bf16[33,32,640,2]{2,1,0,3:T(8,128)(2,1)S(1)}) fusion(f32[32,640,2]{1,0,2:T(8,128)S(1)} %get-tuple-element.27, f32[33,640,2]{1,0,2:T(8,128)S(1)} %get-tuple-element.23, f32[32,640,2]{1,0,2:T(8,128)S(1)} %get-tuple-element.26, f32[33,640,2]{1,0,2:T(8,128)S(1)} %get-tuple-element.22), kind=kLoop, calls=%fused_computation.3 | loop fusion | flops 12165120 | bytes 6072320 | tf_op jit(solution)/shard_map/vmap()/sub | solution.py:110
  64.5 3.3 %fusion.6 = (bf16[1040,640,2,1]{1,0,3,2:T(8,128)(2,1)}, bf16[1040,640,2,1]{1,0,3,2:T(8,128)(2,1)}) fusion(bf16[1,1056,640,2]{2,1,3,0:T(8,128)(2,1)S(1)} %bitcast.79, pred[640,2]{0,1:T(4,128)(4,1)S(1)} %multiply_compare_fusion, pred[1040]{0:T(1024)(128)(4,1)S(1)} %copy-done.3, bf16[1,1056,640,2]{2,1,3,0:T(8,128)(2,1)S(1)} %bitcast.80), kind=kLoop, calls=%fused_computation.11 | loop fusion | flops 3993600 | bytes 10651920 | tf_op jit(solution)/shard_map/vmap()/stack | solution.py:116
  67.7 0.6 fusion.58
  68.3 7.9 %all-to-all-done = bf16[8,2,64,65]{3,1,0,2:T(2,128)(2,1)S(1)} async-done(((bf16[8,2,64,65]{3,1,0,2:T(2,128)(2,1)}), bf16[8,2,64,65]{3,1,0,2:T(2,128)(2,1)S(1)}, u32[]{:S(2)}, u32[]{:S(2)}) %all-to-all-start) | async-done | bytes 133152 | tf_op jit(solution)/shard_map/all_to_all | solution.py:219
  76.2 4.0 %copy.22 = bf16[8,2,64,65]{0,1,3,2:T(2,128)(2,1)} copy(bf16[8,2,64,65]{3,1,0,2:T(2,128)(2,1)S(1)} %all-to-all-done) | data formatting | bytes 266240 | tf_op jit(solution)/shard_map/all_to_all | solution.py:219
  80.2 4.5 %fusion.11 = f32[1,640,2,2,8,2,4]{1,4,6,5,3,2,0:T(8,128)S(1)} fusion(bf16[8,2,1040,4,1,1]{0,1,3,2,5,4:T(2,128)(2,1)} %bitcast.83, bf16[1040,640,2,1]{1,0,3,2:T(8,128)(2,1)} %get-tuple-element.29, bf16[1040,640,2,1]{1,0,3,2:T(8,128)(2,1)} %get-tuple-element.28), kind=kOutput, calls=%fused_computation.20 | convolution fusion | flops 351436800 | bytes 6113280 | tf_op jit(solution)/shard_map/vmap(aser,fhab->serfhb)/dot_general | solution.py:119
  84.8 0.2 copy.25
  85.0 0.5 broadcast.807
  85.5 1.7 %reduce.6 = bf16[640,64]{1,0:T(8,128)(2,1)S(1)} reduce(bf16[640,1,64]{2,1,0:T(2,128)(2,1)S(1)} %bitcast.84, bf16[]{:T(256)} %broadcast.807), dimensions={1}, to_apply=%bitcast.72.reduce_sub_computation | reduce | bytes 163842
  87.2 0.8 reshape.762
  88.0 5.1 %all-to-all-start.1 = ((bf16[64,2,320]{2,1,0:T(2,128)(2,1)}), bf16[64,2,320]{2,1,0:T(2,128)(2,1)S(1)}, u32[]{:S(2)}, u32[]{:S(2)}) async-start(bf16[64,2,320]{2,1,0:T(2,128)(2,1)} %reshape.762), calls=%async_computation.1 | async-start | bytes 196608 | tf_op jit(solution)/shard_map/all_to_all | solution.py:225
  93.2 11.1 %all-to-all-done.1 = bf16[64,2,320]{2,1,0:T(2,128)(2,1)S(1)} async-done(((bf16[64,2,320]{2,1,0:T(2,128)(2,1)}), bf16[64,2,320]{2,1,0:T(2,128)(2,1)S(1)}, u32[]{:S(2)}, u32[]{:S(2)}) %all-to-all-start.1) | async-done | bytes 81952 | tf_op jit(solution)/shard_map/all_to_all | solution.py:225
  104.4 0.2 reshape.763
  104.5 1.0 bitcast_reduce_fusion
  105.6 0.7 fusion.26
  106.3 0.2 fusion.8
  106.7 0.3 copy.28
  107.0 0.3 copy.29
  107.3 1.0 fusion.10
  108.3 10.2 %all-to-all-start.2 = ((bf16[16,10,1281]{2,1,0:T(8,128)(2,1)}), bf16[16,10,1281]{2,1,0:T(8,128)(2,1)S(1)}, u32[]{:S(2)}, u32[]{:S(2)}) async-start(bf16[16,10,1281]{2,1,0:T(8,128)(2,1)} %bitcast.28), calls=%async_computation.2 | async-start | bytes 1441792 | tf_op jit(solution)/shard_map/all_to_all | solution.py:137
  118.8 21.1 %all-to-all-done.2 = bf16[16,10,1281]{2,1,0:T(8,128)(2,1)S(1)} async-done(((bf16[16,10,1281]{2,1,0:T(8,128)(2,1)}), bf16[16,10,1281]{2,1,0:T(8,128)(2,1)S(1)}, u32[]{:S(2)}, u32[]{:S(2)}) %all-to-all-start.2) | async-done | bytes 409952 | tf_op jit(solution)/shard_map/all_to_all | solution.py:137
  140.0 18.8 %all-gather.1 = f32[16,10,1281]{2,1,0:T(8,128)S(1)} all-gather(f32[1,10,1281]{2,1,0:T(8,128)S(1)} %bitcast.85), channel_id=2, replica_groups=mesh['lat'=16,'lon'=64] {'lat'}, dimensions={0}, use_global_device_ids=true | all-gather | bytes 871080 | tf_op jit(solution)/shard_map/all_gather | solution.py:140
  158.8 1.3 fusion.61
  160.0 0.3 broadcast_multiply_fusion
  160.3 1.4 fusion.14
  (32 shorter events, 1.2 us)
Async XLA Ops:
  0.6 104.9 %copy-start = (bf16[64,10,1281]{2,0,1:T(8,128)(2,1)S(1)}, bf16[64,10,1281]{2,0,1:T(8,128)(2,1)}, u32[]{:S(2)}) copy-start(bf16[64,10,1281]{2,0,1:T(8,128)(2,1)} %param.12) | copy-start | bytes 4919044
  0.6 31.0 %copy-start.1 = (bf16[8,2,64,65]{3,2,1,0:T(8,128)(2,1)S(1)}, bf16[8,2,64,65]{3,2,1,0:T(8,128)(2,1)}, u32[]{:S(2)}) copy-start(bf16[8,2,64,65]{3,2,1,0:T(8,128)(2,1)} %param.7) | copy-start | bytes 399364
  2.0 12.2 %collective-permute-start = (bf16[8,2,64,10]{3,2,1,0:T(8,128)(2,1)S(1)}, bf16[8,2,64,10]{3,2,1,0:T(8,128)(2,1)S(1)}, u32[]{:S(2)}, u32[]{:S(2)}) collective-permute-start(bf16[8,2,64,10]{3,2,1,0:T(8,128)(2,1)S(1)} %get-tuple-element.18), channel_id=1, source_target_pairs={{0,1},{1,2},{2,3},{3,4},{4,5},{5,6},{6,7},{7,8},{8,9},{9,10},{10,1... | collective-permute-start | bytes 61448 | tf_op jit(solution)/shard_map/ppermute | solution.py:23
  7.7 8.7 %collective-permute-start.1 = (bf16[8,2,64,10]{3,2,1,0:T(8,128)(2,1)S(1)}, bf16[8,2,64,10]{3,2,1,0:T(8,128)(2,1)S(1)}, u32[]{:S(2)}, u32[]{:S(2)}) collective-permute-start(bf16[8,2,64,10]{3,2,1,0:T(8,128)(2,1)S(1)} %get-tuple-element.19), channel_id=1, source_target_pairs={{1,0},{2,1},{3,2},{4,3},{5,4},{6,5},{7,6},{8,7},{9,8},{10,9},{11,1... | collective-permute-start | bytes 61448 | tf_op jit(solution)/shard_map/ppermute | solution.py:24
  17.3 13.3 %collective-permute-start.3 = (bf16[8,2,1,85]{3,2,1,0:T(2,128)(2,1)S(1)}, bf16[8,2,1,85]{3,2,1,0:T(2,128)(2,1)S(1)}, u32[]{:S(2)}, u32[]{:S(2)}) collective-permute-start(bf16[8,2,1,85]{3,2,1,0:T(2,128)(2,1)S(1)} %get-tuple-element.15), channel_id=1, source_target_pairs={{64,0},{128,64},{192,128},{256,192},{320,256},{384,320},{448,384},... | collective-permute-start | bytes 8168 | tf_op jit(solution)/shard_map/ppermute | solution.py:24
  28.6 3.1 %collective-permute-start.2 = (bf16[8,2,1,85]{3,2,1,0:T(2,128)(2,1)S(1)}, bf16[8,2,1,85]{3,2,1,0:T(2,128)(2,1)S(1)}, u32[]{:S(2)}, u32[]{:S(2)}) collective-permute-start(bf16[8,2,1,85]{3,2,1,0:T(2,128)(2,1)S(1)} %get-tuple-element.14), channel_id=1, source_target_pairs={{0,64},{64,128},{128,192},{192,256},{256,320},{320,384},{384,448},... | collective-permute-start | bytes 8168 | tf_op jit(solution)/shard_map/ppermute | solution.py:23
  46.6 29.6 %all-to-all-start = ((bf16[8,2,64,65]{3,1,0,2:T(2,128)(2,1)}), bf16[8,2,64,65]{3,1,0,2:T(2,128)(2,1)S(1)}, u32[]{:S(2)}, u32[]{:S(2)}) async-start(bf16[8,2,64,65]{3,1,0,2:T(2,128)(2,1)} %copy.21), calls=%async_computation | async-start | bytes 524288 | tf_op jit(solution)/shard_map/all_to_all | solution.py:219
  62.4 2.1 %copy-start.3 = (pred[1040]{0:T(1024)(128)(4,1)S(1)}, pred[1040]{0:T(1024)(128)(4,1)}, u32[]{:S(2)}) copy-start(pred[1040]{0:T(1024)(128)(4,1)} %iota_compare_fusion.2) | copy-start | bytes 3124
  88.0 16.4 %all-to-all-start.1 = ((bf16[64,2,320]{2,1,0:T(2,128)(2,1)}), bf16[64,2,320]{2,1,0:T(2,128)(2,1)S(1)}, u32[]{:S(2)}, u32[]{:S(2)}) async-start(bf16[64,2,320]{2,1,0:T(2,128)(2,1)} %reshape.762), calls=%async_computation.1 | async-start | bytes 196608 | tf_op jit(solution)/shard_map/all_to_all | solution.py:225
  105.6 0.7 copy-start.2
  107.3 11.3 %copy-start.4 = (f32[8]{0:T(128)S(1)}, f32[8]{0:T(128)}, u32[]{:S(2)}) copy-start(f32[8]{0:T(128)} %param.13) | copy-start | bytes 100
  108.3 31.5 %all-to-all-start.2 = ((bf16[16,10,1281]{2,1,0:T(8,128)(2,1)}), bf16[16,10,1281]{2,1,0:T(8,128)(2,1)S(1)}, u32[]{:S(2)}, u32[]{:S(2)}) async-start(bf16[16,10,1281]{2,1,0:T(8,128)(2,1)} %bitcast.28), calls=%async_computation.2 | async-start | bytes 1441792 | tf_op jit(solution)/shard_map/all_to_all | solution.py:137

commit v9 on v8

--- a/solution.py
+++ b/solution.py
@@ -42,7 +42,7 @@
     reach = ((WL - 8, WL + 6), (WL - 5, WL + 6), (WL - 5, WL + 9))
     for dr in range(ext_ref.shape[2] - rows + 1):
         for dc in range(*reach[dr]):
-            window = ext_ref[0, :, dr : dr + rows, dc : dc + cols]
+            window = ext_ref[0, :, dr : dr + rows, dc : dc + cols].astype(jnp.float32)
             key = dr * 64 + dc
             left = jnp.where(code == key, window, left)
             right = jnp.where(code == key - 1, window, right)
@@ -79,7 +79,7 @@
         ],
         out_specs=pl.BlockSpec((1,) + code.shape, lambda f: (f, 0, 0, 0)),
         out_shape=jax.ShapeDtypeStruct((field_count,) + code.shape, jnp.float32),
-    )(extended.astype(jnp.float32), code, lon_weight)
+    )(extended, code, lon_weight)
     return jnp.where(lon_index < length, blended, 0.0).astype(jnp.bfloat16)
 
 

time: 163 us -> 159 us (0.975)
  Pallas kernels: 8.63 us -> 6.48 us
    pallas_call x1, Pallas kernels: 8.63 us -> 6.48 us  [depart_values(): pl.pallas_call(depart_kernel, grid=(field_count,), in_specs=[pl.BlockSpec...]
where the time goes in v9:
time: 159 us; the launch traced here: 158 us
  starting transfers between devices  51.3 us (32%)
  waiting for transfers between devices  43.5 us (27%)
  other arithmetic  20.6 us (13%)
  blocking collectives  18.8 us (12%)
  local copies, waits for them, and re-layouts  9.92 us (6%)
  matrix products  6.5 us (4%)
  Pallas kernels  6.48 us (4%)
    all_to_all x1, waiting for transfers between devices, lat_sum(): lax.all_to_all(grouped.astype(jnp.bfloat16), 'lat', 0, 0, tiled=True)  21.1 us
    all_gather x1, blocking collectives, lat_sum(): whole = lax.all_gather(reduced, 'lat', axis=0, tiled=True)  18.8 us
    all_to_all x1, starting transfers between devices, on_device(): lax.all_to_all(advected, 'lon', split_axis=2, concat_axis=3, tiled=True)  15.8 us
    ppermute x2, starting transfers between devices, extended_2(): after = lax.ppermute(initial, axis, down)  12.5 us
    all_to_all x1, waiting for transfers between devices, on_device(): lax.all_to_all(shortened(spectra), 'lon', split_axis=1, concat_axis=0, ti...  11.1 us
    all_to_all x1, starting transfers between devices, lat_sum(): lax.all_to_all(grouped.astype(jnp.bfloat16), 'lat', 0, 0, tiled=True)  10.2 us
    all_to_all x1, waiting for transfers between devices, on_device(): lax.all_to_all(advected, 'lon', split_axis=2, concat_axis=3, tiled=True)  7.88 us
    ppermute x2, starting transfers between devices, extended_2(): before = lax.ppermute(last, axis, up)  7.66 us
  transfers between devices with their start and end apart: 7, of which 5 were waited for; matrix products, arithmetic and copies ran while one was open for 7% of the time, Pallas kernels for 0%

profile of v9, /device:TPU:1, one launch (start us, length us, event | category | flops | bytes accessed | tf_op | source)
XLA Modules:
  0.0 158.1 jit_solution(9930995856229227345)
XLA Ops:
  0.7 1.3 fusion.63
  2.0 5.7 %collective-permute-start = (bf16[8,2,64,10]{3,2,1,0:T(8,128)(2,1)S(1)}, bf16[8,2,64,10]{3,2,1,0:T(8,128)(2,1)S(1)}, u32[]{:S(2)}, u32[]{:S(2)}) collective-permute-start(bf16[8,2,64,10]{3,2,1,0:T(8,128)(2,1)S(1)} %get-tuple-element.18), channel_id=1, source_target_pairs={{0,1},{1,2},{2,3},{3,4},{4,5},{5,6},{6,7},{7,8},{8,9},{9,10},{10,1... | collective-permute-start | bytes 61448 | tf_op jit(solution)/shard_map/ppermute | solution.py:23
  7.7 1.3 collective-permute-start.1
  9.1 0.8 broadcast_subtract_fusion.1
  9.8 0.7 iota_compare_fusion
  10.5 0.1 fusion.49
  10.7 0.3 fusion.46
  11.0 0.1 fusion.33
  11.2 2.3 %fusion.41.code_ref = s32[2,64,65]{2,1,0:T(8,128)} fusion(s32[2,64,65]{2,1,0:T(8,128)} %param.9, s32[2,64,65]{2,1,0:T(8,128)} %param.8, s32[]{:T(128)S(6)} %sub.231, s32[64]{0:T(128)S(1)} %get-tuple-element.34, s32[64]{0:T(128)S(1)} %get-tuple-element.35, s32[65]{0:T(128)S(1)} %iota_add_fusion.2, s32[64]{0:T(128)S(1)} %get-tuple-element.33, s32[]{:T(128)S(6)} %mul.474, ...), kind=kLoop, calls=%fused_computation.77 | loop fusion | flops 241280 | bytes 105292 | tf_op jit(solution)/shard_map/jit(_where)/select_n | solution.py:70
  13.6 0.6 iota_compare_fusion.2
  14.1 2.2 %collective-permute-done.1 = bf16[8,2,64,10]{3,2,1,0:T(8,128)(2,1)S(1)} collective-permute-done((bf16[8,2,64,10]{3,2,1,0:T(8,128)(2,1)S(1)}, bf16[8,2,64,10]{3,2,1,0:T(8,128)(2,1)S(1)}, u32[]{:S(2)}, u32[]{:S(2)}) %collective-permute-start.1) | collective-permute-done | bytes 20512 | tf_op jit(solution)/shard_map/ppermute | solution.py:24
  16.4 0.9 pad_maximum_fusion.4
  17.3 11.2 %collective-permute-start.3 = (bf16[8,2,1,85]{3,2,1,0:T(2,128)(2,1)S(1)}, bf16[8,2,1,85]{3,2,1,0:T(2,128)(2,1)S(1)}, u32[]{:S(2)}, u32[]{:S(2)}) collective-permute-start(bf16[8,2,1,85]{3,2,1,0:T(2,128)(2,1)S(1)} %get-tuple-element.15), channel_id=1, source_target_pairs={{64,0},{128,64},{192,128},{256,192},{320,256},{384,320},{448,384},... | collective-permute-start | bytes 8168 | tf_op jit(solution)/shard_map/ppermute | solution.py:24
  28.6 1.9 %collective-permute-start.2 = (bf16[8,2,1,85]{3,2,1,0:T(2,128)(2,1)S(1)}, bf16[8,2,1,85]{3,2,1,0:T(2,128)(2,1)S(1)}, u32[]{:S(2)}, u32[]{:S(2)}) collective-permute-start(bf16[8,2,1,85]{3,2,1,0:T(2,128)(2,1)S(1)} %get-tuple-element.14), channel_id=1, source_target_pairs={{0,64},{64,128},{128,192},{192,256},{256,320},{320,384},{384,448},... | collective-permute-start | bytes 8168 | tf_op jit(solution)/shard_map/ppermute | solution.py:23
  30.6 1.1 collective-permute-done.2
  31.7 1.1 pad_maximum_fusion.ext_ref
  32.8 6.5 %shard_map.86 = f32[8,2,64,65]{3,2,1,0:T(8,128)} custom-call(bf16[8,2,66,85]{3,2,1,0:T(8,128)(2,1)} %pad_maximum_fusion.ext_ref, s32[2,64,65]{2,1,0:T(8,128)} %fusion.41.code_ref, bf16[2,64,65]{2,1,0:T(8,128)(2,1)} %weight_ref.1), custom_call_target="tpu_custom_call" | custom-call | tf_op jit(solution)/shard_map/pallas_call | solution.py:72
  39.3 1.1 select_convert_fusion
  40.5 0.7 fusion.36
  41.1 0.9 fusion.29
  42.0 1.0 copy.21
  43.0 15.8 %all-to-all-start = ((bf16[8,2,64,65]{3,1,0,2:T(2,128)(2,1)}), bf16[8,2,64,65]{3,1,0,2:T(2,128)(2,1)S(1)}, u32[]{:S(2)}, u32[]{:S(2)}) async-start(bf16[8,2,64,65]{3,1,0,2:T(2,128)(2,1)} %copy.21), calls=%async_computation | async-start | bytes 524288 | tf_op jit(solution)/shard_map/all_to_all | solution.py:219
  58.8 2.0 %multiply_subtract_fusion = (bf16[33,32,640,2]{2,1,0,3:T(8,128)(2,1)S(1)}, bf16[33,32,640,2]{2,1,0,3:T(8,128)(2,1)S(1)}) fusion(f32[32,640,2]{1,0,2:T(8,128)S(1)} %get-tuple-element.27, f32[33,640,2]{1,0,2:T(8,128)S(1)} %get-tuple-element.23, f32[32,640,2]{1,0,2:T(8,128)S(1)} %get-tuple-element.26, f32[33,640,2]{1,0,2:T(8,128)S(1)} %get-tuple-element.22), kind=kLoop, calls=%fused_computation.3 | loop fusion | flops 12165120 | bytes 6072320 | tf_op jit(solution)/shard_map/vmap()/sub | solution.py:110
  60.9 3.2 %fusion.6 = (bf16[1040,640,2,1]{1,0,3,2:T(8,128)(2,1)}, bf16[1040,640,2,1]{1,0,3,2:T(8,128)(2,1)}) fusion(bf16[1,1056,640,2]{2,1,3,0:T(8,128)(2,1)S(1)} %bitcast.79, pred[640,2]{0,1:T(4,128)(4,1)S(1)} %multiply_compare_fusion, pred[1040]{0:T(1024)(128)(4,1)S(1)} %copy-done.4, bf16[1,1056,640,2]{2,1,3,0:T(8,128)(2,1)S(1)} %bitcast.80), kind=kLoop, calls=%fused_computation.11 | loop fusion | flops 3993600 | bytes 10651920 | tf_op jit(solution)/shard_map/vmap()/stack | solution.py:116
  64.1 0.6 fusion.58
  64.7 7.9 %all-to-all-done = bf16[8,2,64,65]{3,1,0,2:T(2,128)(2,1)S(1)} async-done(((bf16[8,2,64,65]{3,1,0,2:T(2,128)(2,1)}), bf16[8,2,64,65]{3,1,0,2:T(2,128)(2,1)S(1)}, u32[]{:S(2)}, u32[]{:S(2)}) %all-to-all-start) | async-done | bytes 133152 | tf_op jit(solution)/shard_map/all_to_all | solution.py:219
  72.6 4.0 %copy.22 = bf16[8,2,64,65]{0,1,3,2:T(2,128)(2,1)} copy(bf16[8,2,64,65]{3,1,0,2:T(2,128)(2,1)S(1)} %all-to-all-done) | data formatting | bytes 266240 | tf_op jit(solution)/shard_map/all_to_all | solution.py:219
  76.7 4.5 %fusion.11 = f32[1,640,2,2,8,2,4]{1,4,6,5,3,2,0:T(8,128)S(1)} fusion(bf16[8,2,1040,4,1,1]{0,1,3,2,5,4:T(2,128)(2,1)} %bitcast.83, bf16[1040,640,2,1]{1,0,3,2:T(8,128)(2,1)} %get-tuple-element.29, bf16[1040,640,2,1]{1,0,3,2:T(8,128)(2,1)} %get-tuple-element.28), kind=kOutput, calls=%fused_computation.20 | convolution fusion | flops 351436800 | bytes 6113280 | tf_op jit(solution)/shard_map/vmap(aser,fhab->serfhb)/dot_general | solution.py:119
  81.2 0.2 copy.25
  81.5 0.5 broadcast.807
  82.0 1.7 %reduce.6 = bf16[640,64]{1,0:T(8,128)(2,1)S(1)} reduce(bf16[640,1,64]{2,1,0:T(2,128)(2,1)S(1)} %bitcast.84, bf16[]{:T(256)} %broadcast.807), dimensions={1}, to_apply=%bitcast.72.reduce_sub_computation | reduce | bytes 163842
  83.6 0.8 reshape.762
  84.4 5.1 %all-to-all-start.1 = ((bf16[64,2,320]{2,1,0:T(2,128)(2,1)}), bf16[64,2,320]{2,1,0:T(2,128)(2,1)S(1)}, u32[]{:S(2)}, u32[]{:S(2)}) async-start(bf16[64,2,320]{2,1,0:T(2,128)(2,1)} %reshape.762), calls=%async_computation.1 | async-start | bytes 196608 | tf_op jit(solution)/shard_map/all_to_all | solution.py:225
  89.7 11.1 %all-to-all-done.1 = bf16[64,2,320]{2,1,0:T(2,128)(2,1)S(1)} async-done(((bf16[64,2,320]{2,1,0:T(2,128)(2,1)}), bf16[64,2,320]{2,1,0:T(2,128)(2,1)S(1)}, u32[]{:S(2)}, u32[]{:S(2)}) %all-to-all-start.1) | async-done | bytes 81952 | tf_op jit(solution)/shard_map/all_to_all | solution.py:225
  100.8 0.2 reshape.763
  101.0 1.0 bitcast_reduce_fusion
  102.0 0.7 fusion.26
  102.8 0.2 fusion.8
  103.1 0.3 copy.28
  103.4 0.3 copy.29
  103.8 1.0 fusion.10
  104.8 10.2 %all-to-all-start.2 = ((bf16[16,10,1281]{2,1,0:T(8,128)(2,1)}), bf16[16,10,1281]{2,1,0:T(8,128)(2,1)S(1)}, u32[]{:S(2)}, u32[]{:S(2)}) async-start(bf16[16,10,1281]{2,1,0:T(8,128)(2,1)} %bitcast.28), calls=%async_computation.2 | async-start | bytes 1441792 | tf_op jit(solution)/shard_map/all_to_all | solution.py:137
  115.2 21.1 %all-to-all-done.2 = bf16[16,10,1281]{2,1,0:T(8,128)(2,1)S(1)} async-done(((bf16[16,10,1281]{2,1,0:T(8,128)(2,1)}), bf16[16,10,1281]{2,1,0:T(8,128)(2,1)S(1)}, u32[]{:S(2)}, u32[]{:S(2)}) %all-to-all-start.2) | async-done | bytes 409952 | tf_op jit(solution)/shard_map/all_to_all | solution.py:137
  136.3 0.1 convert_reduce_fusion
  136.4 18.8 %all-gather.1 = f32[16,10,1281]{2,1,0:T(8,128)S(1)} all-gather(f32[1,10,1281]{2,1,0:T(8,128)S(1)} %bitcast.85), channel_id=2, replica_groups=mesh['lat'=16,'lon'=64] {'lat'}, dimensions={0}, use_global_device_ids=true | all-gather | bytes 871080 | tf_op jit(solution)/shard_map/all_gather | solution.py:140
  155.2 1.3 fusion.61
  156.5 0.3 broadcast_multiply_fusion
  156.7 1.4 fusion.14
  (34 shorter events, 0.9 us)
Async XLA Ops:
  0.6 101.4 %copy-start = (bf16[64,10,1281]{2,0,1:T(8,128)(2,1)S(1)}, bf16[64,10,1281]{2,0,1:T(8,128)(2,1)}, u32[]{:S(2)}) copy-start(bf16[64,10,1281]{2,0,1:T(8,128)(2,1)} %param.12) | copy-start | bytes 4919044
  0.6 31.0 %copy-start.1 = (bf16[8,2,64,65]{3,2,1,0:T(8,128)(2,1)S(1)}, bf16[8,2,64,65]{3,2,1,0:T(8,128)(2,1)}, u32[]{:S(2)}) copy-start(bf16[8,2,64,65]{3,2,1,0:T(8,128)(2,1)} %param.7) | copy-start | bytes 399364
  2.0 12.2 %collective-permute-start = (bf16[8,2,64,10]{3,2,1,0:T(8,128)(2,1)S(1)}, bf16[8,2,64,10]{3,2,1,0:T(8,128)(2,1)S(1)}, u32[]{:S(2)}, u32[]{:S(2)}) collective-permute-start(bf16[8,2,64,10]{3,2,1,0:T(8,128)(2,1)S(1)} %get-tuple-element.18), channel_id=1, source_target_pairs={{0,1},{1,2},{2,3},{3,4},{4,5},{5,6},{6,7},{7,8},{8,9},{9,10},{10,1... | collective-permute-start | bytes 61448 | tf_op jit(solution)/shard_map/ppermute | solution.py:23
  7.7 8.7 %collective-permute-start.1 = (bf16[8,2,64,10]{3,2,1,0:T(8,128)(2,1)S(1)}, bf16[8,2,64,10]{3,2,1,0:T(8,128)(2,1)S(1)}, u32[]{:S(2)}, u32[]{:S(2)}) collective-permute-start(bf16[8,2,64,10]{3,2,1,0:T(8,128)(2,1)S(1)} %get-tuple-element.19), channel_id=1, source_target_pairs={{1,0},{2,1},{3,2},{4,3},{5,4},{6,5},{7,6},{8,7},{9,8},{10,9},{11,1... | collective-permute-start | bytes 61448 | tf_op jit(solution)/shard_map/ppermute | solution.py:24
  14.1 26.2 %copy-start.3 = (s32[640]{0:T(1024)S(1)}, s32[640]{0:T(1024)}, u32[]{:S(2)}) copy-start(s32[640]{0:T(1024)} %param.11) | copy-start | bytes 7684
  17.3 13.3 %collective-permute-start.3 = (bf16[8,2,1,85]{3,2,1,0:T(2,128)(2,1)S(1)}, bf16[8,2,1,85]{3,2,1,0:T(2,128)(2,1)S(1)}, u32[]{:S(2)}, u32[]{:S(2)}) collective-permute-start(bf16[8,2,1,85]{3,2,1,0:T(2,128)(2,1)S(1)} %get-tuple-element.15), channel_id=1, source_target_pairs={{64,0},{128,64},{192,128},{256,192},{320,256},{384,320},{448,384},... | collective-permute-start | bytes 8168 | tf_op jit(solution)/shard_map/ppermute | solution.py:24
  28.6 3.1 %collective-permute-start.2 = (bf16[8,2,1,85]{3,2,1,0:T(2,128)(2,1)S(1)}, bf16[8,2,1,85]{3,2,1,0:T(2,128)(2,1)S(1)}, u32[]{:S(2)}, u32[]{:S(2)}) collective-permute-start(bf16[8,2,1,85]{3,2,1,0:T(2,128)(2,1)S(1)} %get-tuple-element.14), channel_id=1, source_target_pairs={{0,64},{64,128},{128,192},{192,256},{256,320},{320,384},{384,448},... | collective-permute-start | bytes 8168 | tf_op jit(solution)/shard_map/ppermute | solution.py:23
  43.0 29.6 %all-to-all-start = ((bf16[8,2,64,65]{3,1,0,2:T(2,128)(2,1)}), bf16[8,2,64,65]{3,1,0,2:T(2,128)(2,1)S(1)}, u32[]{:S(2)}, u32[]{:S(2)}) async-start(bf16[8,2,64,65]{3,1,0,2:T(2,128)(2,1)} %copy.21), calls=%async_computation | async-start | bytes 524288 | tf_op jit(solution)/shard_map/all_to_all | solution.py:219
  58.8 2.1 %copy-start.4 = (pred[1040]{0:T(1024)(128)(4,1)S(1)}, pred[1040]{0:T(1024)(128)(4,1)}, u32[]{:S(2)}) copy-start(pred[1040]{0:T(1024)(128)(4,1)} %iota_compare_fusion.2) | copy-start | bytes 3124
  84.4 16.4 %all-to-all-start.1 = ((bf16[64,2,320]{2,1,0:T(2,128)(2,1)}), bf16[64,2,320]{2,1,0:T(2,128)(2,1)S(1)}, u32[]{:S(2)}, u32[]{:S(2)}) async-start(bf16[64,2,320]{2,1,0:T(2,128)(2,1)} %reshape.762), calls=%async_computation.1 | async-start | bytes 196608 | tf_op jit(solution)/shard_map/all_to_all | solution.py:225
  102.0 0.7 copy-start.2
  103.8 11.3 %copy-start.5 = (f32[8]{0:T(128)S(1)}, f32[8]{0:T(128)}, u32[]{:S(2)}) copy-start(f32[8]{0:T(128)} %param.13) | copy-start | bytes 100
  104.8 31.5 %all-to-all-start.2 = ((bf16[16,10,1281]{2,1,0:T(8,128)(2,1)}), bf16[16,10,1281]{2,1,0:T(8,128)(2,1)S(1)}, u32[]{:S(2)}, u32[]{:S(2)}) async-start(bf16[16,10,1281]{2,1,0:T(8,128)(2,1)} %bitcast.28), calls=%async_computation.2 | async-start | bytes 1441792 | tf_op jit(solution)/shard_map/all_to_all | solution.py:137
